TPU v7x, 1024 devices: a whole 4x4x32 slice. The times are simulated.
1024 devices in a mesh: region: 32 (over x, z_hi, core), group: 32 (over z_lo, y).
Axes of the slice: x: 4, y: 4, z: 32 (z_hi: 4, z_lo: 8; z = z_hi * 8 + z_lo), core: 2. Of those that a mesh axis runs over, the one named last changes fastest.
Arguments:
- right_side: float32 [216, 393216], P(None, ('region', 'group')), may hold values from -4 to 4
- stiff_fine: float32 [216, 216], replicated
- smooth_fine: float32 [216, 216], replicated
- restrict_fine: float32 [27, 216], replicated, may hold values from -1.25 to 1.25
- stiff_middle: float32 [27, 27], replicated
- smooth_middle: float32 [27, 27], replicated
- restrict_middle: float32 [8, 27], replicated, may hold values from -1.25 to 1.25
- neighbor: int32 [393216, 6], P(('region', 'group')), may hold values from 0 to 864, as said below
- send_group: int32 [1024, 2, 192], P(('region', 'group')), may hold values from 0 to 383, as said below
- send_region: int32 [1024, 2, 48], P(('region', 'group')), may hold values from 0 to 383, as said below
- ghost_orient: int32 [1024, 480], P(('region', 'group')), may hold values from 0 to 7, as said below
- corners: int32 [393216, 8], P(('region', 'group')), may hold values from 0 to 14624, as said below
Outputs:
- solution: float32 [216, 393216], P(None, ('region', 'group'))
Inputs may be any that keep to these rules, and one draw needn't show every extreme that they name: `neighbor`: Device-local slot indices; entries at or above 384 follow the ghost ranges of the steps, matching send_group and send_region of the adjacent devices; 864 marks the box's z ends. `send_group`: Device-local slots; position k is y * 24 + z of the element on that side. `send_region`: Device-local slots; position k is x * 24 + z of the element on that side. `ghost_orient`: positions follow the ghost ranges of neighbor; the two sides of one shared face carry mutually inverse codes. The elements of device (r, g) have corners only on vertex planes g * 2 to (g + 1) * 2 along x.
All inputs are finite; a program needn't handle non-finite values.
Results may differ from a plain program's by a relative error of at most 0.0003.
Values sent between devices are 32-bit elements; how exact they have to be, the bound alone decides.
No kernel may reach another device: no remote copies, remote signals or barrier semaphores. Data moves between devices by JAX's collectives and lax.ppermute only.
A program may use at most 32 MiB of HBM per device.

v0:
```python
import math

import jax
import jax.numpy as jnp
import numpy as np
from jax import lax
from jax.sharding import PartitionSpec as P

FINE_PTS = 6
MID_PTS = 3
BX = 2
BY = 8
BZ = 24


HIGHEST = lax.Precision.HIGHEST
penalty_fine = 1.0
penalty_middle = 1.0


def extended(block, sides, width):
    for axis, dim in sides:
        count = lax.axis_size(axis)
        forward = [(i, i + 1) for i in range(count - 1)]
        backward = [(target, source) for source, target in forward]
        low = lax.ppermute(
            lax.slice_in_dim(block, block.shape[dim] - width, None, axis=dim), axis, forward
        )
        high = lax.ppermute(lax.slice_in_dim(block, 0, width, axis=dim), axis, backward)
        block = jnp.concatenate([low, block, high], axis=dim)
    return block


def orient_lookup(points):
    lookup = np.zeros((8, points * points), np.int32)
    for code_index in range(8):
        for row_index in range(points):
            for col_index in range(points):
                first_pos, second_pos = (row_index, col_index)
                if code_index >= 4:
                    first_pos, second_pos = (second_pos, first_pos)
                for rotation in range(code_index % 4):
                    first_pos, second_pos = (second_pos, points - 1 - first_pos)
                lookup[code_index, row_index * points + col_index] = first_pos * points + second_pos
    return lookup


def reorient(blocks, code_rows, points):
    stacked = blocks[:, orient_lookup(points), :]
    picked = (code_rows[:, None, :] == jnp.arange(8, dtype=jnp.int32)[None, :, None]).astype(
        jnp.float32
    )
    return jnp.sum(stacked * picked[:, :, None, :], axis=1)


def face_traces(current, points):
    rest = current.shape[1:]
    blocked = current.reshape((points, points, points) + rest)
    last_node = points - 1
    pieces = [
        blocked[0],
        blocked[last_node],
        blocked[:, 0],
        blocked[:, last_node],
        blocked[:, :, 0],
        blocked[:, :, last_node],
    ]
    return [face_piece.reshape((points * points,) + rest) for face_piece in pieces]


def ghost_columns(traces, send_group, send_region, ghost_orient, points):
    group_count = send_group.shape[2]
    region_count = send_region.shape[2]
    outgoing = jnp.stack([traces[0][:, send_group[0, 0]], traces[1][:, send_group[0, 1]]])
    arrived = extended(outgoing, (("group", 0),), 1)
    group_codes = ghost_orient[0, : 2 * group_count].reshape(2, group_count)
    from_group = reorient(jnp.stack([arrived[0], arrived[3]]), group_codes, points)
    leaving = jnp.stack([traces[2][:, send_region[0, 0]], traces[3][:, send_region[0, 1]]])
    landed = extended(leaving, (("region", 0),), 1)
    region_codes = ghost_orient[0, 2 * group_count :].reshape(2, region_count)
    from_region = reorient(jnp.stack([landed[0], landed[3]]), region_codes, points)
    return jnp.concatenate([from_group[0], from_group[1], from_region[0], from_region[1]], axis=1)


def apply_level(current, stiffness, penalty, points, tables):
    neighbor, send_group, send_region, ghost_orient = tables
    traces = face_traces(current, points)
    ghosts = ghost_columns(traces, send_group, send_region, ghost_orient, points)
    plane_size = points * points
    elements = current.shape[1]
    padding = jnp.zeros((plane_size, 1), jnp.float32)
    product = jnp.dot(stiffness, current, precision=HIGHEST, preferred_element_type=jnp.float32)
    blocked = product.reshape(points, points, points, elements)
    jump_terms = []
    for face_index in range(6):
        source = jnp.concatenate([traces[face_index ^ 1], ghosts, padding], axis=1)
        outside = jnp.take(source, neighbor[:, face_index], axis=1)
        jump_terms.append(
            (penalty * (traces[face_index] - outside)).reshape(points, points, elements)
        )
    last_node = points - 1
    blocked = blocked.at[0].add(jump_terms[0])
    blocked = blocked.at[last_node].add(jump_terms[1])
    blocked = blocked.at[:, 0].add(jump_terms[2])
    blocked = blocked.at[:, last_node].add(jump_terms[3])
    blocked = blocked.at[:, :, 0].add(jump_terms[4])
    blocked = blocked.at[:, :, last_node].add(jump_terms[5])
    return blocked.reshape(points * points * points, elements)


def sine_basis(extent):
    ordinal = jnp.arange(1, extent + 1, dtype=jnp.int32)
    wrapped = ordinal[:, None] * ordinal[None, :] % (2 * (extent + 1))
    return math.sqrt(2.0 / (extent + 1)) * jnp.sin(
        wrapped.astype(jnp.float32) * (math.pi / (extent + 1))
    )


def spectrum(extent):
    cosine = jnp.cos(
        jnp.arange(1, extent + 1, dtype=jnp.int32).astype(jnp.float32) * (math.pi / (extent + 1))
    )
    return (2.0 - 2.0 * cosine, (4.0 + 2.0 * cosine) / 6.0)


def transform(volume, basis_z, basis_y, basis_x):
    turned = jnp.einsum("zyx,xk->zyk", volume, basis_x, precision=HIGHEST)
    turned = jnp.einsum("zyk,yj->zjk", turned, basis_y, precision=HIGHEST)
    return jnp.einsum("zjk,zi->ijk", turned, basis_z, precision=HIGHEST)


def coarse_solve(interior):
    depth_count, height_count, breadth_count = interior.shape
    basis_z, basis_y, basis_x = (
        sine_basis(depth_count),
        sine_basis(height_count),
        sine_basis(breadth_count),
    )
    stiff_z, mass_z = spectrum(depth_count)
    stiff_y, mass_y = spectrum(height_count)
    stiff_x, mass_x = spectrum(breadth_count)
    eigen_sum = (
        stiff_z[:, None, None] * mass_y[None, :, None] * mass_x[None, None, :]
        + mass_z[:, None, None] * stiff_y[None, :, None] * mass_x[None, None, :]
        + mass_z[:, None, None] * mass_y[None, :, None] * stiff_x[None, None, :]
    )
    return transform(
        transform(interior, basis_z, basis_y, basis_x) / eigen_sum, basis_z, basis_y, basis_x
    )


def body(
    right_side,
    stiff_fine,
    smooth_fine,
    restrict_fine,
    stiff_middle,
    smooth_middle,
    restrict_middle,
    neighbor,
    send_group,
    send_region,
    ghost_orient,
    corners,
):
    tables = (neighbor, send_group, send_region, ghost_orient)
    smoothed = jnp.dot(
        smooth_fine, right_side, precision=HIGHEST, preferred_element_type=jnp.float32
    )
    residual = right_side - apply_level(smoothed, stiff_fine, penalty_fine, FINE_PTS, tables)
    middle_rhs = jnp.dot(
        restrict_fine, residual, precision=HIGHEST, preferred_element_type=jnp.float32
    )
    middle_fix = jnp.dot(
        smooth_middle, middle_rhs, precision=HIGHEST, preferred_element_type=jnp.float32
    )
    middle_res = middle_rhs - apply_level(middle_fix, stiff_middle, penalty_middle, MID_PTS, tables)
    corner_terms = jnp.dot(
        restrict_middle, middle_res, precision=HIGHEST, preferred_element_type=jnp.float32
    )
    corner_ids = corners.T
    width_group = lax.axis_size("group")
    vert_x = width_group * BX + 1
    assembled = (
        jnp.zeros(((BZ + 1) * (BY + 1) * vert_x,), jnp.float32)
        .at[corner_ids.reshape(-1)]
        .add(corner_terms.reshape(-1))
    )
    interior = assembled.reshape(BZ + 1, BY + 1, vert_x)[1:BZ, 1:BY, 1 : vert_x - 1]
    interior = lax.psum(interior, "group")
    solved = coarse_solve(interior)
    padded = jnp.pad(solved, ((1, 1), (1, 1), (1, 1))).reshape(-1)
    coarse_fix = padded[corner_ids]
    middle_corr = middle_fix + jnp.dot(
        restrict_middle.T, coarse_fix, precision=HIGHEST, preferred_element_type=jnp.float32
    )
    middle_left = middle_rhs - apply_level(
        middle_corr, stiff_middle, penalty_middle, MID_PTS, tables
    )
    middle_post = middle_corr + jnp.dot(
        smooth_middle, middle_left, precision=HIGHEST, preferred_element_type=jnp.float32
    )
    current = smoothed + jnp.dot(
        restrict_fine.T, middle_post, precision=HIGHEST, preferred_element_type=jnp.float32
    )
    left_over = right_side - apply_level(current, stiff_fine, penalty_fine, FINE_PTS, tables)
    return current + jnp.dot(
        smooth_fine, left_over, precision=HIGHEST, preferred_element_type=jnp.float32
    )


def solution(mesh):
    return jax.shard_map(
        body,
        mesh=mesh,
        in_specs=(
            P(None, ("region", "group")),
            P(),
            P(),
            P(),
            P(),
            P(),
            P(),
            P(("region", "group"), None),
            P(("region", "group"), None, None),
            P(("region", "group"), None, None),
            P(("region", "group"), None),
            P(("region", "group"), None),
        ),
        out_specs=P(None, ("region", "group")),
        check_vma=False,
    )
```

profile of v0, /device:TPU:1, one launch (start us, length us, event | category | flops | bytes accessed | tf_op | source)
XLA Modules:
  0.0 460.1 jit_solution(2083317042983994635)
XLA Ops:
  3.1 4.0 collective-permute-start
  10.6 16.3 %collective-permute-start.2 = (f32[1,36,48]{1,2,0:T(8,128)S(1)}, f32[1,36,48]{1,2,0:T(8,128)S(1)}, u32[]{:S(2)}, u32[]{:S(2)}) collective-permute-start(f32[1,36,48]{1,2,0:T(8,128)S(1)} %bitcast.419), channel_id=1, source_target_pairs={{0,32},{32,64},{64,96},{96,128},{128,160},{160,192},{192,224},{224... | collective-permute-start | bytes 20744 | tf_op jit(solution)/shard_map/ppermute | solution.py:26
  27.7 1.9 collective-permute-start.3
  32.8 8.7 %collective-permute-done.3 = f32[1,36,48]{1,2,0:T(8,128)S(1)} collective-permute-done((f32[1,36,48]{1,2,0:T(8,128)S(1)}, f32[1,36,48]{1,2,0:T(8,128)S(1)}, u32[]{:S(2)}, u32[]{:S(2)}) %collective-permute-start.3) | collective-permute-done | bytes 6944 | tf_op jit(solution)/shard_map/ppermute | solution.py:29
  41.6 2.1 gather_fusion.5
  44.7 2.6 gather_fusion.2
  57.5 2.1 scatter-add.94
  59.7 2.1 scatter-add.95
  64.5 4.6 collective-permute-start.6
  69.9 1.9 collective-permute-start.7
  72.6 4.3 collective-permute-start.4
  79.6 4.9 %collective-permute-done.7 = f32[1,9,48]{1,2,0:T(8,128)S(1)} collective-permute-done((f32[1,9,48]{1,2,0:T(8,128)S(1)}, f32[1,9,48]{1,2,0:T(8,128)S(1)}, u32[]{:S(2)}, u32[]{:S(2)}) %collective-permute-start.7) | collective-permute-done | bytes 1760 | tf_op jit(solution)/shard_map/ppermute | solution.py:29
  97.1 16.6 %scatter_custom_fusion = f32[14625]{0:T(1024)S(1)} fusion(s32[3072]{0:T(1024)S(1)} %bitcast.423, f32[3072]{0:T(1024)S(1)} %reshape.1697, f32[]{:T(128)} %constant.648.clone.1), kind=kCustom, calls=%fused_computation.151 | custom fusion | flops 3072 | bytes 58504 | tf_op jit(solution)/shard_map/scatter-add | solution.py:187
  114.0 209.1 %psum.7 = f32[23,7,63]{2,0,1:T(8,128)S(1)} all-reduce(f32[23,7,63]{2,0,1:T(8,128)S(1)} %copy.673), channel_id=1, replica_groups=mesh['region'=32,'group'=32] {'group'}, use_global_device_ids=true, to_apply=%region_5.0 | all-reduce | flops 10143 | bytes 81144 | tf_op jit(solution)/shard_map/psum | solution.py:190
  326.5 17.4 %gather_fusion.12 = f32[3072]{0:T(1024)S(1)} fusion(f32[14625]{0:T(1024)S(1)} %reshape.1284, s32[3072]{0:T(1024)S(1)} %broadcast_clamp_fusion), kind=kCustom, calls=%fused_computation.36 | custom fusion | bytes 36864 | tf_op jit(solution)/shard_map/gather | solution.py:193
  345.1 37.2 %collective-permute-start.10 = (f32[1,9,48]{1,2,0:T(8,128)S(1)}, f32[1,9,48]{1,2,0:T(8,128)S(1)}, u32[]{:S(2)}, u32[]{:S(2)}) collective-permute-start(f32[1,9,48]{1,2,0:T(8,128)S(1)} %bitcast.431), channel_id=1, source_target_pairs={{0,32},{32,64},{64,96},{96,128},{128,160},{160,192},{192,224},{224... | collective-permute-start | bytes 5192 | tf_op jit(solution)/shard_map/ppermute | solution.py:26
  383.1 1.9 collective-permute-start.11
  389.7 7.2 %collective-permute-done.11 = f32[1,9,48]{1,2,0:T(8,128)S(1)} collective-permute-done((f32[1,9,48]{1,2,0:T(8,128)S(1)}, f32[1,9,48]{1,2,0:T(8,128)S(1)}, u32[]{:S(2)}, u32[]{:S(2)}) %collective-permute-start.11) | collective-permute-done | bytes 1760 | tf_op jit(solution)/shard_map/ppermute | solution.py:29
  410.9 9.0 %collective-permute-start.14 = (f32[1,36,48]{1,2,0:T(8,128)S(1)}, f32[1,36,48]{1,2,0:T(8,128)S(1)}, u32[]{:S(2)}, u32[]{:S(2)}) collective-permute-start(f32[1,36,48]{1,2,0:T(8,128)S(1)} %bitcast.421), channel_id=1, source_target_pairs={{0,32},{32,64},{64,96},{96,128},{128,160},{160,192},{192,224},{224... | collective-permute-start | bytes 20744 | tf_op jit(solution)/shard_map/ppermute | solution.py:26
  427.4 7.0 %collective-permute-done.15 = f32[1,36,48]{1,2,0:T(8,128)S(1)} collective-permute-done((f32[1,36,48]{1,2,0:T(8,128)S(1)}, f32[1,36,48]{1,2,0:T(8,128)S(1)}, u32[]{:S(2)}, u32[]{:S(2)}) %collective-permute-start.15) | collective-permute-done | bytes 6944 | tf_op jit(solution)/shard_map/ppermute | solution.py:29
  434.5 2.1 gather_fusion.24
  437.6 2.6 gather_fusion.21
  453.5 2.1 scatter-add.150
  455.7 2.1 scatter-add.151
  (447 shorter events, 87.7 us)
Async XLA Ops:
  0.0 31.2 %copy-start = (f32[216,216]{1,0:T(8,128)S(1)}, f32[216,216]{1,0:T(8,128)}, u32[]{:S(2)}) copy-start(f32[216,216]{1,0:T(8,128)} %param.81) | copy-start | bytes 559876
  3.1 41.3 %collective-permute-start = (f32[1,36,192]{1,2,0:T(8,128)S(1)}, f32[1,36,192]{1,2,0:T(8,128)S(1)}, u32[]{:S(2)}, u32[]{:S(2)}) collective-permute-start(f32[1,36,192]{1,2,0:T(8,128)S(1)} %bitcast.415), channel_id=1, source_target_pairs={{0,1},{1,2},{2,3},{3,4},{4,5},{5,6},{6,7},{7,8},{8,9},{9,10},{10,1... | collective-permute-start | bytes 82952 | tf_op jit(solution)/shard_map/ppermute | solution.py:26
  8.0 36.5 %collective-permute-start.1 = (f32[1,36,192]{1,2,0:T(8,128)S(1)}, f32[1,36,192]{1,2,0:T(8,128)S(1)}, u32[]{:S(2)}, u32[]{:S(2)}) collective-permute-start(f32[1,36,192]{1,2,0:T(8,128)S(1)} %bitcast.416), channel_id=1, source_target_pairs={{1,0},{2,1},{3,2},{4,3},{5,4},{6,5},{7,6},{8,7},{9,8},{10,9},{11,1... | collective-permute-start | bytes 82952 | tf_op jit(solution)/shard_map/ppermute | solution.py:29
  10.6 22.2 %collective-permute-start.2 = (f32[1,36,48]{1,2,0:T(8,128)S(1)}, f32[1,36,48]{1,2,0:T(8,128)S(1)}, u32[]{:S(2)}, u32[]{:S(2)}) collective-permute-start(f32[1,36,48]{1,2,0:T(8,128)S(1)} %bitcast.419), channel_id=1, source_target_pairs={{0,32},{32,64},{64,96},{96,128},{128,160},{160,192},{192,224},{224... | collective-permute-start | bytes 20744 | tf_op jit(solution)/shard_map/ppermute | solution.py:26
  27.7 13.9 %collective-permute-start.3 = (f32[1,36,48]{1,2,0:T(8,128)S(1)}, f32[1,36,48]{1,2,0:T(8,128)S(1)}, u32[]{:S(2)}, u32[]{:S(2)}) collective-permute-start(f32[1,36,48]{1,2,0:T(8,128)S(1)} %bitcast.420), channel_id=1, source_target_pairs={{32,0},{64,32},{96,64},{128,96},{160,128},{192,160},{224,192},{256... | collective-permute-start | bytes 20744 | tf_op jit(solution)/shard_map/ppermute | solution.py:29
  29.7 378.6 %copy-start.10 = (pred[384]{0:T(512)(128)(4,1)}, pred[384]{0:T(512)(128)(4,1)S(1)}, u32[]{:S(2)}) copy-start(pred[384]{0:T(512)(128)(4,1)S(1)} %get-tuple-element.365) | copy-start | bytes 1156
  29.7 378.6 %copy-start.12 = (pred[384]{0:T(512)(128)(4,1)}, pred[384]{0:T(512)(128)(4,1)S(1)}, u32[]{:S(2)}) copy-start(pred[384]{0:T(512)(128)(4,1)S(1)} %get-tuple-element.366) | copy-start | bytes 1156
  29.8 374.1 %copy-start.16 = (pred[384]{0:T(512)(128)(4,1)}, pred[384]{0:T(512)(128)(4,1)S(1)}, u32[]{:S(2)}) copy-start(pred[384]{0:T(512)(128)(4,1)S(1)} %get-tuple-element.363) | copy-start | bytes 1156
  29.8 375.6 %copy-start.14 = (pred[384]{0:T(512)(128)(4,1)}, pred[384]{0:T(512)(128)(4,1)S(1)}, u32[]{:S(2)}) copy-start(pred[384]{0:T(512)(128)(4,1)S(1)} %get-tuple-element.364) | copy-start | bytes 1156
  30.1 370.8 %copy-start.20 = (pred[384]{0:T(512)(128)(4,1)}, pred[384]{0:T(512)(128)(4,1)S(1)}, u32[]{:S(2)}) copy-start(pred[384]{0:T(512)(128)(4,1)S(1)} %get-tuple-element.361) | copy-start | bytes 1156
  30.1 372.2 %copy-start.18 = (pred[384]{0:T(512)(128)(4,1)}, pred[384]{0:T(512)(128)(4,1)S(1)}, u32[]{:S(2)}) copy-start(pred[384]{0:T(512)(128)(4,1)S(1)} %get-tuple-element.362) | copy-start | bytes 1156
  32.5 367.1 %copy-start.7 = (s32[1024]{0:T(1024)}, s32[1024]{0:T(1024)S(1)}, u32[]{:S(2)}) copy-start(s32[1024]{0:T(1024)S(1)} %pad_clamp_fusion.1) | copy-start | bytes 12292
  64.5 15.0 %collective-permute-start.6 = (f32[1,9,48]{1,2,0:T(8,128)S(1)}, f32[1,9,48]{1,2,0:T(8,128)S(1)}, u32[]{:S(2)}, u32[]{:S(2)}) collective-permute-start(f32[1,9,48]{1,2,0:T(8,128)S(1)} %bitcast.430), channel_id=1, source_target_pairs={{0,32},{32,64},{64,96},{96,128},{128,160},{160,192},{192,224},{224... | collective-permute-start | bytes 5192 | tf_op jit(solution)/shard_map/ppermute | solution.py:26
  69.9 14.7 %collective-permute-start.7 = (f32[1,9,48]{1,2,0:T(8,128)S(1)}, f32[1,9,48]{1,2,0:T(8,128)S(1)}, u32[]{:S(2)}, u32[]{:S(2)}) collective-permute-start(f32[1,9,48]{1,2,0:T(8,128)S(1)} %bitcast.432), channel_id=1, source_target_pairs={{32,0},{64,32},{96,64},{128,96},{160,128},{192,160},{224,192},{256... | collective-permute-start | bytes 5192 | tf_op jit(solution)/shard_map/ppermute | solution.py:29
  72.6 12.8 %collective-permute-start.4 = (f32[1,9,192]{1,2,0:T(8,128)S(1)}, f32[1,9,192]{1,2,0:T(8,128)S(1)}, u32[]{:S(2)}, u32[]{:S(2)}) collective-permute-start(f32[1,9,192]{1,2,0:T(8,128)S(1)} %bitcast.426), channel_id=1, source_target_pairs={{0,1},{1,2},{2,3},{3,4},{4,5},{5,6},{6,7},{7,8},{8,9},{9,10},{10,1... | collective-permute-start | bytes 20744 | tf_op jit(solution)/shard_map/ppermute | solution.py:26
  77.8 7.7 %collective-permute-start.5 = (f32[1,9,192]{1,2,0:T(8,128)S(1)}, f32[1,9,192]{1,2,0:T(8,128)S(1)}, u32[]{:S(2)}, u32[]{:S(2)}) collective-permute-start(f32[1,9,192]{1,2,0:T(8,128)S(1)} %bitcast.427), channel_id=1, source_target_pairs={{1,0},{2,1},{3,2},{4,3},{5,4},{6,5},{7,6},{8,7},{9,8},{10,9},{11,1... | collective-permute-start | bytes 20744 | tf_op jit(solution)/shard_map/ppermute | solution.py:29
  345.1 44.5 %collective-permute-start.10 = (f32[1,9,48]{1,2,0:T(8,128)S(1)}, f32[1,9,48]{1,2,0:T(8,128)S(1)}, u32[]{:S(2)}, u32[]{:S(2)}) collective-permute-start(f32[1,9,48]{1,2,0:T(8,128)S(1)} %bitcast.431), channel_id=1, source_target_pairs={{0,32},{32,64},{64,96},{96,128},{128,160},{160,192},{192,224},{224... | collective-permute-start | bytes 5192 | tf_op jit(solution)/shard_map/ppermute | solution.py:26
  383.1 13.9 %collective-permute-start.11 = (f32[1,9,48]{1,2,0:T(8,128)S(1)}, f32[1,9,48]{1,2,0:T(8,128)S(1)}, u32[]{:S(2)}, u32[]{:S(2)}) collective-permute-start(f32[1,9,48]{1,2,0:T(8,128)S(1)} %bitcast.433), channel_id=1, source_target_pairs={{32,0},{64,32},{96,64},{128,96},{160,128},{192,160},{224,192},{256... | collective-permute-start | bytes 5192 | tf_op jit(solution)/shard_map/ppermute | solution.py:29
  385.9 11.9 %collective-permute-start.8 = (f32[1,9,192]{1,2,0:T(8,128)S(1)}, f32[1,9,192]{1,2,0:T(8,128)S(1)}, u32[]{:S(2)}, u32[]{:S(2)}) collective-permute-start(f32[1,9,192]{1,2,0:T(8,128)S(1)} %bitcast.428), channel_id=1, source_target_pairs={{0,1},{1,2},{2,3},{3,4},{4,5},{5,6},{6,7},{7,8},{8,9},{9,10},{10,1... | collective-permute-start | bytes 20744 | tf_op jit(solution)/shard_map/ppermute | solution.py:26
  388.0 9.9 %collective-permute-start.9 = (f32[1,9,192]{1,2,0:T(8,128)S(1)}, f32[1,9,192]{1,2,0:T(8,128)S(1)}, u32[]{:S(2)}, u32[]{:S(2)}) collective-permute-start(f32[1,9,192]{1,2,0:T(8,128)S(1)} %bitcast.429), channel_id=1, source_target_pairs={{1,0},{2,1},{3,2},{4,3},{5,4},{6,5},{7,6},{8,7},{9,8},{10,9},{11,1... | collective-permute-start | bytes 20744 | tf_op jit(solution)/shard_map/ppermute | solution.py:29
  410.9 16.5 %collective-permute-start.14 = (f32[1,36,48]{1,2,0:T(8,128)S(1)}, f32[1,36,48]{1,2,0:T(8,128)S(1)}, u32[]{:S(2)}, u32[]{:S(2)}) collective-permute-start(f32[1,36,48]{1,2,0:T(8,128)S(1)} %bitcast.421), channel_id=1, source_target_pairs={{0,32},{32,64},{64,96},{96,128},{128,160},{160,192},{192,224},{224... | collective-permute-start | bytes 20744 | tf_op jit(solution)/shard_map/ppermute | solution.py:26
  420.6 13.9 %collective-permute-start.15 = (f32[1,36,48]{1,2,0:T(8,128)S(1)}, f32[1,36,48]{1,2,0:T(8,128)S(1)}, u32[]{:S(2)}, u32[]{:S(2)}) collective-permute-start(f32[1,36,48]{1,2,0:T(8,128)S(1)} %bitcast.422), channel_id=1, source_target_pairs={{32,0},{64,32},{96,64},{128,96},{160,128},{192,160},{224,192},{256... | collective-permute-start | bytes 20744 | tf_op jit(solution)/shard_map/ppermute | solution.py:29
  423.6 13.7 %collective-permute-start.12 = (f32[1,36,192]{1,2,0:T(8,128)S(1)}, f32[1,36,192]{1,2,0:T(8,128)S(1)}, u32[]{:S(2)}, u32[]{:S(2)}) collective-permute-start(f32[1,36,192]{1,2,0:T(8,128)S(1)} %bitcast.417), channel_id=1, source_target_pairs={{0,1},{1,2},{2,3},{3,4},{4,5},{5,6},{6,7},{7,8},{8,9},{9,10},{10,1... | collective-permute-start | bytes 82952 | tf_op jit(solution)/shard_map/ppermute | solution.py:26
  425.8 11.6 %collective-permute-start.13 = (f32[1,36,192]{1,2,0:T(8,128)S(1)}, f32[1,36,192]{1,2,0:T(8,128)S(1)}, u32[]{:S(2)}, u32[]{:S(2)}) collective-permute-start(f32[1,36,192]{1,2,0:T(8,128)S(1)} %bitcast.418), channel_id=1, source_target_pairs={{1,0},{2,1},{3,2},{4,3},{5,4},{6,5},{7,6},{8,7},{9,8},{10,9},{11,1... | collective-permute-start | bytes 82952 | tf_op jit(solution)/shard_map/ppermute | solution.py:29
  (21 other events, 20.2 us)
where the time goes:
time: 461 us; the launch traced here: 460 us
  blocking collectives  209 us (45%)
  local copies, waits for them, and re-layouts  101 us (22%)
  starting transfers between devices  91.4 us (20%)
  waiting for transfers between devices  27.9 us (6%)
  other arithmetic  20.1 us (4%)
  matrix products  8.43 us (2%)
    psum x1, blocking collectives, body(): interior = lax.psum(interior, 'group')  209 us
    ppermute x8, starting transfers between devices, extended(): lax.ppermute(lax.slice_in_dim(block, block.shape[dim] - width, None, axis...  77.9 us
    gather x48, local copies, waits for them, and re-layouts, apply_level(): outside = jnp.take(source, neighbor[:, face_index], axis=1)  29.3 us
    ppermute x8, waiting for transfers between devices, extended(): lax.ppermute(lax.slice_in_dim(block, 0, width, axis=dim), axis, backward)  27.9 us
    gather x2, local copies, waits for them, and re-layouts, body(): coarse_fix = padded[corner_ids]  17.4 us
    scatter-add x1, other arithmetic, body(): assembled = jnp.zeros(((BZ + 1) * (BY + 1) * vert_x,), jnp.float32).at[co...  16.6 us
    ppermute x8, starting transfers between devices, extended(): lax.ppermute(lax.slice_in_dim(block, 0, width, axis=dim), axis, backward)  13.5 us
    gather x10, local copies, waits for them, and re-layouts, reorient(): stacked = blocks[:, orient_lookup(points), :]  12.8 us
  transfers between devices with their start and end apart: 16, of which 4 were waited for; matrix products, arithmetic and copies ran while one was open for 4% of the time, Pallas kernels for 0%

commit v1 on v0

v1 whole, which is shorter than its diff:
```python
import math

import jax
import jax.numpy as jnp
import numpy as np
from jax import lax
from jax.sharding import PartitionSpec as P

FINE_PTS = 6
MID_PTS = 3
BX = 2
BY = 8
BZ = 24


HIGHEST = lax.Precision.HIGHEST
penalty_fine = 1.0
penalty_middle = 1.0


def mm(a, b):
    return jnp.dot(a, b, precision=HIGHEST, preferred_element_type=jnp.float32)


def orient_lookup(points):
    lookup = np.zeros((8, points * points), np.int32)
    for code_index in range(8):
        for row_index in range(points):
            for col_index in range(points):
                first_pos, second_pos = (row_index, col_index)
                if code_index >= 4:
                    first_pos, second_pos = (second_pos, first_pos)
                for rotation in range(code_index % 4):
                    first_pos, second_pos = (second_pos, points - 1 - first_pos)
                lookup[code_index, row_index * points + col_index] = first_pos * points + second_pos
    return lookup


def orient_matrix(points):
    lookup = orient_lookup(points)
    plane = points * points
    mat = np.zeros((8 * plane, plane), np.float32)
    for code_index in range(8):
        mat[code_index * plane + np.arange(plane), lookup[code_index]] = 1.0
    return mat


def face_nodes(points):
    ids = np.arange(points**3).reshape(points, points, points)
    last = points - 1
    pieces = [ids[0], ids[last], ids[:, 0], ids[:, last], ids[:, :, 0], ids[:, :, last]]
    return np.stack([p.reshape(-1) for p in pieces])


def trace_matrix(points):
    nodes = face_nodes(points)
    plane = points * points
    mat = np.zeros((6 * plane, points**3), np.float32)
    for face_index in range(6):
        mat[face_index * plane + np.arange(plane), nodes[face_index]] = 1.0
    return mat


def make_tables(neighbor, send_group, send_region, ghost_orient):
    elements = neighbor.shape[0]
    group_count = send_group.shape[2]
    region_count = send_region.shape[2]
    ghosts = 2 * group_count + 2 * region_count
    slots = jnp.arange(elements, dtype=jnp.int32)
    sources = jnp.arange(elements + ghosts, dtype=jnp.int32)
    gather = (neighbor.T[:, None, :] == sources[None, :, None]).astype(jnp.float32)
    pick_group = (send_group[0][:, None, :] == slots[None, :, None]).astype(jnp.float32)
    pick_region = (send_region[0][:, None, :] == slots[None, :, None]).astype(jnp.float32)
    codes = (ghost_orient[0][None, :] == jnp.arange(8, dtype=jnp.int32)[:, None]).astype(
        jnp.float32
    )
    return gather, pick_group, pick_region, codes


def shift(block, axis, step):
    count = lax.axis_size(axis)
    if step > 0:
        pairs = [(i, i + 1) for i in range(count - 1)]
    else:
        pairs = [(i + 1, i) for i in range(count - 1)]
    return lax.ppermute(block, axis, pairs)


def apply_level(current, stiffness, points, tables):
    gather, pick_group, pick_region, codes = tables
    plane = points * points
    cube = points**3
    elements = current.shape[1]
    select = jnp.asarray(trace_matrix(points))
    both = mm(jnp.concatenate([stiffness, select], axis=0), current)
    product = both[:cube]
    traces = both[cube:].reshape(6, plane, elements)
    group_out = jnp.einsum(
        "snj,sjk->snk", traces[0:2], pick_group, precision=HIGHEST,
        preferred_element_type=jnp.float32,
    )
    region_out = jnp.einsum(
        "snj,sjk->snk", traces[2:4], pick_region, precision=HIGHEST,
        preferred_element_type=jnp.float32,
    )
    raw = jnp.concatenate(
        [
            shift(group_out[1], "group", 1),
            shift(group_out[0], "group", -1),
            shift(region_out[1], "region", 1),
            shift(region_out[0], "region", -1),
        ],
        axis=1,
    )
    turned = mm(jnp.asarray(orient_matrix(points)), raw).reshape(8, plane, -1)
    ghosts = jnp.sum(turned * codes[:, None, :], axis=0)
    swapped = traces[np.array([1, 0, 3, 2, 5, 4])]
    source = jnp.concatenate(
        [swapped, jnp.broadcast_to(ghosts[None], (6,) + ghosts.shape)], axis=2
    )
    outside = jnp.einsum(
        "fnq,fqe->fne", source, gather, precision=HIGHEST, preferred_element_type=jnp.float32
    )
    jumps = (traces - outside).reshape(6 * plane, elements)
    return product + mm(select.T, jumps)


def sine_basis(extent):
    ordinal = jnp.arange(1, extent + 1, dtype=jnp.int32)
    wrapped = ordinal[:, None] * ordinal[None, :] % (2 * (extent + 1))
    return math.sqrt(2.0 / (extent + 1)) * jnp.sin(
        wrapped.astype(jnp.float32) * (math.pi / (extent + 1))
    )


def spectrum(extent):
    cosine = jnp.cos(
        jnp.arange(1, extent + 1, dtype=jnp.int32).astype(jnp.float32) * (math.pi / (extent + 1))
    )
    return (2.0 - 2.0 * cosine, (4.0 + 2.0 * cosine) / 6.0)


def transform(volume, basis_z, basis_y, basis_x):
    turned = jnp.einsum("zyx,xk->zyk", volume, basis_x, precision=HIGHEST)
    turned = jnp.einsum("zyk,yj->zjk", turned, basis_y, precision=HIGHEST)
    return jnp.einsum("zjk,zi->ijk", turned, basis_z, precision=HIGHEST)


def coarse_solve(interior):
    depth_count, height_count, breadth_count = interior.shape
    basis_z, basis_y, basis_x = (
        sine_basis(depth_count),
        sine_basis(height_count),
        sine_basis(breadth_count),
    )
    stiff_z, mass_z = spectrum(depth_count)
    stiff_y, mass_y = spectrum(height_count)
    stiff_x, mass_x = spectrum(breadth_count)
    eigen_sum = (
        stiff_z[:, None, None] * mass_y[None, :, None] * mass_x[None, None, :]
        + mass_z[:, None, None] * stiff_y[None, :, None] * mass_x[None, None, :]
        + mass_z[:, None, None] * mass_y[None, :, None] * stiff_x[None, None, :]
    )
    return transform(
        transform(interior, basis_z, basis_y, basis_x) / eigen_sum, basis_z, basis_y, basis_x
    )


def gather_slab(local, width):
    count = local.shape[0]
    index = lax.axis_index("group")
    full = lax.dynamic_update_slice(
        jnp.zeros((count, BX * width + 1), jnp.float32), local, (0, BX * index)
    )
    for bit in range(int(math.log2(width))):
        partner = [(i, i ^ (1 << bit)) for i in range(width)]
        full = full + lax.ppermute(full, "group", partner)
    return full


def body(
    right_side,
    stiff_fine,
    smooth_fine,
    restrict_fine,
    stiff_middle,
    smooth_middle,
    restrict_middle,
    neighbor,
    send_group,
    send_region,
    ghost_orient,
    corners,
):
    tables = make_tables(neighbor, send_group, send_region, ghost_orient)
    smoothed = mm(smooth_fine, right_side)
    residual = right_side - apply_level(smoothed, stiff_fine, FINE_PTS, tables)
    middle_rhs = mm(restrict_fine, residual)
    middle_fix = mm(smooth_middle, middle_rhs)
    middle_res = middle_rhs - apply_level(middle_fix, stiff_middle, MID_PTS, tables)
    corner_terms = mm(restrict_middle, middle_res)

    width_group = lax.axis_size("group")
    vert_x = width_group * BX + 1
    planes = (BZ + 1) * (BY + 1)
    corner_ids = corners.T.reshape(-1)
    plane_ids = corner_ids // vert_x
    column = corner_ids - plane_ids * vert_x - BX * lax.axis_index("group")
    on_plane = (plane_ids[None, :] == jnp.arange(planes, dtype=jnp.int32)[:, None]).astype(
        jnp.float32
    )
    on_column = (column[:, None] == jnp.arange(BX + 1, dtype=jnp.int32)[None, :]).astype(
        jnp.float32
    )
    local = mm(on_plane, corner_terms.reshape(-1)[:, None] * on_column)
    assembled = gather_slab(local, width_group)
    interior = assembled.reshape(BZ + 1, BY + 1, vert_x)[1:BZ, 1:BY, 1 : vert_x - 1]
    solved = coarse_solve(interior)
    padded = jnp.pad(solved, ((1, 1), (1, 1), (1, 1)))
    mine = lax.dynamic_slice_in_dim(padded, BX * lax.axis_index("group"), BX + 1, axis=2)
    picked = mm(mine.reshape(planes, BX + 1).T, on_plane)
    coarse_fix = jnp.sum(picked * on_column.T, axis=0).reshape(corners.shape[1], -1)

    middle_corr = middle_fix + mm(restrict_middle.T, coarse_fix)
    middle_left = middle_rhs - apply_level(middle_corr, stiff_middle, MID_PTS, tables)
    middle_post = middle_corr + mm(smooth_middle, middle_left)
    current = smoothed + mm(restrict_fine.T, middle_post)
    left_over = right_side - apply_level(current, stiff_fine, FINE_PTS, tables)
    return current + mm(smooth_fine, left_over)


def solution(mesh):
    return jax.shard_map(
        body,
        mesh=mesh,
        in_specs=(
            P(None, ("region", "group")),
            P(),
            P(),
            P(),
            P(),
            P(),
            P(),
            P(("region", "group"), None),
            P(("region", "group"), None, None),
            P(("region", "group"), None, None),
            P(("region", "group"), None),
            P(("region", "group"), None),
        ),
        out_specs=P(None, ("region", "group")),
        check_vma=False,
    )
```

time: 461 us -> 193 us (0.42)
  blocking collectives: 209 us -> 0 us
  local copies, waits for them, and re-layouts: 101 us -> 11.4 us
  waiting for transfers between devices: 27.9 us -> 51.7 us
  matrix products: 8.43 us -> 30.5 us
  other arithmetic: 20.1 us -> 1.71 us
    psum x1 -> x0, blocking collectives: 209 us -> none  [body(): interior = lax.psum(interior, 'group')]
    gather x76 -> x4, local copies, waits for them, and re-layouts: 69.8 us -> 3.75 us  [apply_level(): swapped = traces[np.array([1, 0, 3, 2, 5, 4])]]
    ppermute x16 -> x21, waiting for transfers between devices: 27.9 us -> 51.7 us  [the longest x16 41.2 us: shift(): return lax.ppermute(block, axis, pairs)]
    dot_general x12 -> x34, matrix products: 6.08 us -> 28.1 us  [the longest x22 13.1 us: mm(): return jnp.dot(a, b, precision=HIGHEST, preferred_element_type=jnp.float32)]
    scatter-add x13 -> x0, other arithmetic: 16.8 us -> none  [the longest x1 16.6 us: body(): assembled = jnp.zeros(((BZ + 1) * (BY + 1) * vert_x,), jnp.float32).at[co...]
    scatter-add x12 -> x0, local copies, waits for them, and re-layouts: 8.82 us -> none  [the longest x4 4.39 us: apply_level(): blocked = blocked.at[:, :, 0].add(jump_terms[4])]
    concatenate x48 -> x0, local copies, waits for them, and re-layouts: 7.21 us -> none  [apply_level(): source = jnp.concatenate([traces[face_index ^ 1], ghosts, padding], axis=1)]
    ppermute x16 -> x21, starting transfers between devices: 91.4 us -> 93 us  [the longest x16 59.9 us: shift(): return lax.ppermute(block, axis, pairs)]
  transfers between devices with their start and end apart: 16 -> 21, of which waited for: 4 -> 9; matrix products, arithmetic and copies ran while one was open for 4% -> 4% of each run, Pallas kernels for 0% -> 0%
where the time goes in v1:
time: 193 us; the launch traced here: 189 us
  starting transfers between devices  93 us (48%)
  waiting for transfers between devices  51.7 us (27%)
  matrix products  30.5 us (16%)
  local copies, waits for them, and re-layouts  11.4 us (6%)
    ppermute x16, starting transfers between devices, shift(): return lax.ppermute(block, axis, pairs)  59.9 us
    ppermute x16, waiting for transfers between devices, shift(): return lax.ppermute(block, axis, pairs)  41.2 us
    ppermute x5, starting transfers between devices, gather_slab(): full = full + lax.ppermute(full, 'group', partner)  33.1 us
    dot_general x22, matrix products, mm(): return jnp.dot(a, b, precision=HIGHEST, preferred_element_type=jnp.float32)  13.1 us
    dot_general x4, matrix products, apply_level(): jnp.einsum('fnq,fqe->fne', source, gather, precision=HIGHEST, preferred_e...  11.7 us
    ppermute x5, waiting for transfers between devices, gather_slab(): full = full + lax.ppermute(full, 'group', partner)  10.5 us
    unnamed x59, local copies, waits for them, and re-layouts  4.8 us
  transfers between devices with their start and end apart: 21, of which 9 were waited for; matrix products, arithmetic and copies ran while one was open for 4% of the time, Pallas kernels for 0%

profile of v1, /device:TPU:1, one launch (start us, length us, event | category | flops | bytes accessed | tf_op | source)
XLA Modules:
  0.0 189.5 jit_solution(16211082127542723037)
XLA Ops:
  4.6 4.0 %collective-permute-start = (f32[36,192]{1,0:T(8,128)S(1)}, f32[36,192]{1,0:T(8,128)S(1)}, u32[]{:S(2)}, u32[]{:S(2)}) collective-permute-start(f32[36,192]{1,0:T(8,128)S(1)} %get-tuple-element.15), channel_id=1, source_target_pairs={{0,1},{1,2},{2,3},{3,4},{4,5},{5,6},{6,7},{7,8},{8,9},{9,10},{10,1... | collective-permute-start | bytes 82952 | tf_op jit(solution)/shard_map/ppermute | solution.py:86
  10.3 16.3 %collective-permute-start.2 = (f32[36,48]{1,0:T(8,128)S(1)}, f32[36,48]{1,0:T(8,128)S(1)}, u32[]{:S(2)}, u32[]{:S(2)}) collective-permute-start(f32[36,48]{1,0:T(8,128)S(1)} %get-tuple-element.19), channel_id=1, source_target_pairs={{0,32},{32,64},{64,96},{96,128},{128,160},{160,192},{192,224},{224... | collective-permute-start | bytes 20744 | tf_op jit(solution)/shard_map/ppermute | solution.py:86
  32.6 7.8 %collective-permute-done.3 = f32[36,48]{1,0:T(8,128)S(1)} collective-permute-done((f32[36,48]{1,0:T(8,128)S(1)}, f32[36,48]{1,0:T(8,128)S(1)}, u32[]{:S(2)}, u32[]{:S(2)}) %collective-permute-start.3) | collective-permute-done | bytes 6944 | tf_op jit(solution)/shard_map/ppermute | solution.py:86
  42.2 3.6 %fusion.11 = f32[6,36,384]{2,1,0:T(8,128)} fusion(f32[6,36,384]{2,1,0:T(8,128)S(1)} %reshape.280, s32[6,384]{1,0:T(8,128)S(1)} %bitcast.116, f32[6,36,480]{2,1,0:T(8,128)S(1)} %broadcast_in_dim.19, f32[6,36,384]{2,1,0:T(8,128)S(1)} %copy-done.9), kind=kOutput, calls=%fused_computation.18 | convolution fusion | flops 862223616 | bytes 1419264 | tf_op jit(solution)/shard_map/fnq,fqe->fne/dot_general | solution.py:121
  49.2 4.3 %collective-permute-start.4 = (f32[9,192]{1,0:T(8,128)S(1)}, f32[9,192]{1,0:T(8,128)S(1)}, u32[]{:S(2)}, u32[]{:S(2)}) collective-permute-start(f32[9,192]{1,0:T(8,128)S(1)} %get-tuple-element.23), channel_id=1, source_target_pairs={{0,1},{1,2},{2,3},{3,4},{4,5},{5,6},{6,7},{7,8},{8,9},{9,10},{10,1... | collective-permute-start | bytes 20744 | tf_op jit(solution)/shard_map/ppermute | solution.py:86
  55.1 4.9 %collective-permute-start.6 = (f32[9,48]{1,0:T(8,128)S(1)}, f32[9,48]{1,0:T(8,128)S(1)}, u32[]{:S(2)}, u32[]{:S(2)}) collective-permute-start(f32[9,48]{1,0:T(8,128)S(1)} %get-tuple-element.27), channel_id=1, source_target_pairs={{0,32},{32,64},{64,96},{96,128},{128,160},{160,192},{192,224},{224... | collective-permute-start | bytes 5192 | tf_op jit(solution)/shard_map/ppermute | solution.py:86
  59.9 1.9 %collective-permute-start.7 = (f32[9,48]{1,0:T(8,128)S(1)}, f32[9,48]{1,0:T(8,128)S(1)}, u32[]{:S(2)}, u32[]{:S(2)}) collective-permute-start(f32[9,48]{1,0:T(8,128)S(1)} %get-tuple-element.28), channel_id=1, source_target_pairs={{32,0},{64,32},{96,64},{128,96},{160,128},{192,160},{224,192},{256... | collective-permute-start | bytes 5192 | tf_op jit(solution)/shard_map/ppermute | solution.py:86
  62.5 11.6 %collective-permute-done.7 = f32[9,48]{1,0:T(8,128)S(1)} collective-permute-done((f32[9,48]{1,0:T(8,128)S(1)}, f32[9,48]{1,0:T(8,128)S(1)}, u32[]{:S(2)}, u32[]{:S(2)}) %collective-permute-start.7) | collective-permute-done | bytes 1760 | tf_op jit(solution)/shard_map/ppermute | solution.py:86
  74.6 2.7 %fusion.17 = f32[6,9,384]{2,1,0:T(8,128)S(1)} fusion(f32[6,9,384]{2,1,0:T(8,128)S(1)} %reshape.284, s32[6,384]{1,0:T(8,128)S(1)} %bitcast.117, f32[6,9,480]{2,1,0:T(8,128)S(1)} %broadcast_in_dim.22, f32[6,9,384]{2,1,0:T(8,128)S(1)} %gather_fusion.1), kind=kOutput, calls=%fused_computation.28 | convolution fusion | flops 217048896 | bytes 361728 | tf_op jit(solution)/shard_map/fnq,fqe->fne/dot_general | solution.py:121
  79.2 4.2 %collective-permute-start.8 = (f32[225,65]{0,1:T(8,128)S(1)}, f32[225,65]{0,1:T(8,128)S(1)}, u32[]{:S(2)}, u32[]{:S(2)}) collective-permute-start(f32[225,65]{0,1:T(8,128)S(1)} %dynamic_update_slice.5), channel_id=1, source_target_pairs={{0,1},{1,0},{2,3},{3,2},{4,5},{5,4},{6,7},{7,6},{8,9},{9,8},{10,11... | collective-permute-start | bytes 175508 | tf_op jit(solution)/shard_map/ppermute | solution.py:177
  85.5 5.5 %collective-permute-start.9 = (f32[225,65]{0,1:T(8,128)S(1)}, f32[225,65]{0,1:T(8,128)S(1)}, u32[]{:S(2)}, u32[]{:S(2)}) collective-permute-start(f32[225,65]{0,1:T(8,128)S(1)} %add.201), channel_id=1, source_target_pairs={{0,2},{1,3},{2,0},{3,1},{4,6},{5,7},{6,4},{7,5},{8,10},{9,11},{10,... | collective-permute-start | bytes 175508 | tf_op jit(solution)/shard_map/ppermute | solution.py:177
  92.8 6.6 %collective-permute-start.10 = (f32[225,65]{0,1:T(8,128)S(1)}, f32[225,65]{0,1:T(8,128)S(1)}, u32[]{:S(2)}, u32[]{:S(2)}) collective-permute-start(f32[225,65]{0,1:T(8,128)S(1)} %add.202), channel_id=1, source_target_pairs={{0,4},{1,5},{2,6},{3,7},{4,0},{5,1},{6,2},{7,3},{8,12},{9,13},{10,... | collective-permute-start | bytes 175508 | tf_op jit(solution)/shard_map/ppermute | solution.py:177
  99.4 2.0 %collective-permute-done.10 = f32[225,65]{0,1:T(8,128)S(1)} collective-permute-done((f32[225,65]{0,1:T(8,128)S(1)}, f32[225,65]{0,1:T(8,128)S(1)}, u32[]{:S(2)}, u32[]{:S(2)}) %collective-permute-start.10) | collective-permute-done | bytes 58532 | tf_op jit(solution)/shard_map/ppermute | solution.py:177
  101.4 4.6 %collective-permute-start.11 = (f32[225,65]{0,1:T(8,128)S(1)}, f32[225,65]{0,1:T(8,128)S(1)}, u32[]{:S(2)}, u32[]{:S(2)}) collective-permute-start(f32[225,65]{0,1:T(8,128)S(1)} %add.203), channel_id=1, source_target_pairs={{0,8},{1,9},{2,10},{3,11},{4,12},{5,13},{6,14},{7,15},{8,0},{9,1},... | collective-permute-start | bytes 175508 | tf_op jit(solution)/shard_map/ppermute | solution.py:177
  107.8 12.3 %collective-permute-start.12 = (f32[225,65]{0,1:T(8,128)S(1)}, f32[225,65]{0,1:T(8,128)S(1)}, u32[]{:S(2)}, u32[]{:S(2)}) collective-permute-start(f32[225,65]{0,1:T(8,128)S(1)} %add.204), channel_id=1, source_target_pairs={{0,16},{1,17},{2,18},{3,19},{4,20},{5,21},{6,22},{7,23},{8,24},{9,... | collective-permute-start | bytes 175508 | tf_op jit(solution)/shard_map/ppermute | solution.py:177
  120.1 3.2 %collective-permute-done.12 = f32[225,65]{0,1:T(8,128)S(1)} collective-permute-done((f32[225,65]{0,1:T(8,128)S(1)}, f32[225,65]{0,1:T(8,128)S(1)}, u32[]{:S(2)}, u32[]{:S(2)}) %collective-permute-start.12) | collective-permute-done | bytes 58532 | tf_op jit(solution)/shard_map/ppermute | solution.py:177
  131.9 4.8 %collective-permute-start.15 = (f32[9,48]{1,0:T(8,128)S(1)}, f32[9,48]{1,0:T(8,128)S(1)}, u32[]{:S(2)}, u32[]{:S(2)}) collective-permute-start(f32[9,48]{1,0:T(8,128)S(1)} %get-tuple-element.25), channel_id=1, source_target_pairs={{0,32},{32,64},{64,96},{96,128},{128,160},{160,192},{192,224},{224... | collective-permute-start | bytes 5192 | tf_op jit(solution)/shard_map/ppermute | solution.py:86
  139.2 11.1 %collective-permute-done.16 = f32[9,48]{1,0:T(8,128)S(1)} collective-permute-done((f32[9,48]{1,0:T(8,128)S(1)}, f32[9,48]{1,0:T(8,128)S(1)}, u32[]{:S(2)}, u32[]{:S(2)}) %collective-permute-start.16) | collective-permute-done | bytes 1760 | tf_op jit(solution)/shard_map/ppermute | solution.py:86
  150.8 2.7 %fusion.18 = f32[6,9,384]{2,1,0:T(8,128)S(1)} fusion(f32[6,9,384]{2,1,0:T(8,128)S(1)} %reshape.290, s32[6,384]{1,0:T(8,128)S(1)} %bitcast.118, f32[6,9,480]{2,1,0:T(8,128)S(1)} %broadcast_in_dim.24, f32[6,9,384]{2,1,0:T(8,128)S(1)} %gather_fusion.2), kind=kOutput, calls=%fused_computation.29 | convolution fusion | flops 217048896 | bytes 361728 | tf_op jit(solution)/shard_map/fnq,fqe->fne/dot_general | solution.py:121
  156.0 4.3 %collective-permute-start.17 = (f32[36,192]{1,0:T(8,128)S(1)}, f32[36,192]{1,0:T(8,128)S(1)}, u32[]{:S(2)}, u32[]{:S(2)}) collective-permute-start(f32[36,192]{1,0:T(8,128)S(1)} %get-tuple-element.13), channel_id=1, source_target_pairs={{0,1},{1,2},{2,3},{3,4},{4,5},{5,6},{6,7},{7,8},{8,9},{9,10},{10,1... | collective-permute-start | bytes 82952 | tf_op jit(solution)/shard_map/ppermute | solution.py:86
  161.9 6.7 %collective-permute-start.19 = (f32[36,48]{1,0:T(8,128)S(1)}, f32[36,48]{1,0:T(8,128)S(1)}, u32[]{:S(2)}, u32[]{:S(2)}) collective-permute-start(f32[36,48]{1,0:T(8,128)S(1)} %get-tuple-element.17), channel_id=1, source_target_pairs={{0,32},{32,64},{64,96},{96,128},{128,160},{160,192},{192,224},{224... | collective-permute-start | bytes 20744 | tf_op jit(solution)/shard_map/ppermute | solution.py:86
  168.5 2.1 %collective-permute-start.20 = (f32[36,48]{1,0:T(8,128)S(1)}, f32[36,48]{1,0:T(8,128)S(1)}, u32[]{:S(2)}, u32[]{:S(2)}) collective-permute-start(f32[36,48]{1,0:T(8,128)S(1)} %get-tuple-element.18), channel_id=1, source_target_pairs={{32,0},{64,32},{96,64},{128,96},{160,128},{192,160},{224,192},{256... | collective-permute-start | bytes 20744 | tf_op jit(solution)/shard_map/ppermute | solution.py:86
  172.1 10.6 %collective-permute-done.20 = f32[36,48]{1,0:T(8,128)S(1)} collective-permute-done((f32[36,48]{1,0:T(8,128)S(1)}, f32[36,48]{1,0:T(8,128)S(1)}, u32[]{:S(2)}, u32[]{:S(2)}) %collective-permute-start.20) | collective-permute-done | bytes 6944 | tf_op jit(solution)/shard_map/ppermute | solution.py:86
  184.6 2.8 %fusion.12 = f32[6,36,384]{2,1,0:T(8,128)S(1)} fusion(f32[6,36,384]{2,1,0:T(8,128)S(1)} %copy-done.4, s32[6,384]{1,0:T(8,128)S(1)} %bitcast.119, f32[6,36,480]{2,1,0:T(8,128)S(1)} %broadcast_in_dim.26, f32[6,36,384]{2,1,0:T(8,128)S(1)} %copy-done.8), kind=kOutput, calls=%fused_computation.19 | convolution fusion | flops 862223616 | bytes 1419264 | tf_op jit(solution)/shard_map/fnq,fqe->fne/dot_general | solution.py:121
  (192 shorter events, 47.7 us)
Async XLA Ops:
  3.4 25.2 %copy-start.24 = (s32[6]{0:T(128)S(1)}, s32[6]{0:T(128)}, u32[]{:S(2)}) copy-start(s32[6]{0:T(128)} %constant.126) | copy-start | bytes 76
  3.4 25.2 %copy-start.18 = (s32[384,8]{0,1:T(8,128)S(1)}, s32[384,8]{0,1:T(8,128)}, u32[]{:S(2)}) copy-start(s32[384,8]{0,1:T(8,128)} %param.39) | copy-start | bytes 36868
  4.6 35.8 %collective-permute-start = (f32[36,192]{1,0:T(8,128)S(1)}, f32[36,192]{1,0:T(8,128)S(1)}, u32[]{:S(2)}, u32[]{:S(2)}) collective-permute-start(f32[36,192]{1,0:T(8,128)S(1)} %get-tuple-element.15), channel_id=1, source_target_pairs={{0,1},{1,2},{2,3},{3,4},{4,5},{5,6},{6,7},{7,8},{8,9},{9,10},{10,1... | collective-permute-start | bytes 82952 | tf_op jit(solution)/shard_map/ppermute | solution.py:86
  8.6 31.8 %collective-permute-start.1 = (f32[36,192]{1,0:T(8,128)S(1)}, f32[36,192]{1,0:T(8,128)S(1)}, u32[]{:S(2)}, u32[]{:S(2)}) collective-permute-start(f32[36,192]{1,0:T(8,128)S(1)} %get-tuple-element.16), channel_id=1, source_target_pairs={{1,0},{2,1},{3,2},{4,3},{5,4},{6,5},{7,6},{8,7},{9,8},{10,9},{11,1... | collective-permute-start | bytes 82952 | tf_op jit(solution)/shard_map/ppermute | solution.py:86
  10.3 22.3 %collective-permute-start.2 = (f32[36,48]{1,0:T(8,128)S(1)}, f32[36,48]{1,0:T(8,128)S(1)}, u32[]{:S(2)}, u32[]{:S(2)}) collective-permute-start(f32[36,48]{1,0:T(8,128)S(1)} %get-tuple-element.19), channel_id=1, source_target_pairs={{0,32},{32,64},{64,96},{96,128},{128,160},{160,192},{192,224},{224... | collective-permute-start | bytes 20744 | tf_op jit(solution)/shard_map/ppermute | solution.py:86
  26.6 13.8 %collective-permute-start.3 = (f32[36,48]{1,0:T(8,128)S(1)}, f32[36,48]{1,0:T(8,128)S(1)}, u32[]{:S(2)}, u32[]{:S(2)}) collective-permute-start(f32[36,48]{1,0:T(8,128)S(1)} %get-tuple-element.20), channel_id=1, source_target_pairs={{32,0},{64,32},{96,64},{128,96},{160,128},{192,160},{224,192},{256... | collective-permute-start | bytes 20744 | tf_op jit(solution)/shard_map/ppermute | solution.py:86
  48.6 25.5 %copy-start.11 = (f32[72,9]{1,0:T(8,128)S(1)}, f32[72,9]{1,0:T(8,128)}, u32[]{:S(2)}) copy-start(f32[72,9]{1,0:T(8,128)} %constant.116.clone) | copy-start | bytes 7780
  49.2 24.9 %collective-permute-start.4 = (f32[9,192]{1,0:T(8,128)S(1)}, f32[9,192]{1,0:T(8,128)S(1)}, u32[]{:S(2)}, u32[]{:S(2)}) collective-permute-start(f32[9,192]{1,0:T(8,128)S(1)} %get-tuple-element.23), channel_id=1, source_target_pairs={{0,1},{1,2},{2,3},{3,4},{4,5},{5,6},{6,7},{7,8},{8,9},{9,10},{10,1... | collective-permute-start | bytes 20744 | tf_op jit(solution)/shard_map/ppermute | solution.py:86
  53.5 20.7 %collective-permute-start.5 = (f32[9,192]{1,0:T(8,128)S(1)}, f32[9,192]{1,0:T(8,128)S(1)}, u32[]{:S(2)}, u32[]{:S(2)}) collective-permute-start(f32[9,192]{1,0:T(8,128)S(1)} %get-tuple-element.24), channel_id=1, source_target_pairs={{1,0},{2,1},{3,2},{4,3},{5,4},{6,5},{7,6},{8,7},{9,8},{10,9},{11,1... | collective-permute-start | bytes 20744 | tf_op jit(solution)/shard_map/ppermute | solution.py:86
  55.1 7.5 %collective-permute-start.6 = (f32[9,48]{1,0:T(8,128)S(1)}, f32[9,48]{1,0:T(8,128)S(1)}, u32[]{:S(2)}, u32[]{:S(2)}) collective-permute-start(f32[9,48]{1,0:T(8,128)S(1)} %get-tuple-element.27), channel_id=1, source_target_pairs={{0,32},{32,64},{64,96},{96,128},{128,160},{160,192},{192,224},{224... | collective-permute-start | bytes 5192 | tf_op jit(solution)/shard_map/ppermute | solution.py:86
  59.9 14.2 %collective-permute-start.7 = (f32[9,48]{1,0:T(8,128)S(1)}, f32[9,48]{1,0:T(8,128)S(1)}, u32[]{:S(2)}, u32[]{:S(2)}) collective-permute-start(f32[9,48]{1,0:T(8,128)S(1)} %get-tuple-element.28), channel_id=1, source_target_pairs={{32,0},{64,32},{96,64},{128,96},{160,128},{192,160},{224,192},{256... | collective-permute-start | bytes 5192 | tf_op jit(solution)/shard_map/ppermute | solution.py:86
  79.2 6.2 %collective-permute-start.8 = (f32[225,65]{0,1:T(8,128)S(1)}, f32[225,65]{0,1:T(8,128)S(1)}, u32[]{:S(2)}, u32[]{:S(2)}) collective-permute-start(f32[225,65]{0,1:T(8,128)S(1)} %dynamic_update_slice.5), channel_id=1, source_target_pairs={{0,1},{1,0},{2,3},{3,2},{4,5},{5,4},{6,7},{7,6},{8,9},{9,8},{10,11... | collective-permute-start | bytes 175508 | tf_op jit(solution)/shard_map/ppermute | solution.py:177
  85.5 7.2 %collective-permute-start.9 = (f32[225,65]{0,1:T(8,128)S(1)}, f32[225,65]{0,1:T(8,128)S(1)}, u32[]{:S(2)}, u32[]{:S(2)}) collective-permute-start(f32[225,65]{0,1:T(8,128)S(1)} %add.201), channel_id=1, source_target_pairs={{0,2},{1,3},{2,0},{3,1},{4,6},{5,7},{6,4},{7,5},{8,10},{9,11},{10,... | collective-permute-start | bytes 175508 | tf_op jit(solution)/shard_map/ppermute | solution.py:177
  92.8 8.6 %collective-permute-start.10 = (f32[225,65]{0,1:T(8,128)S(1)}, f32[225,65]{0,1:T(8,128)S(1)}, u32[]{:S(2)}, u32[]{:S(2)}) collective-permute-start(f32[225,65]{0,1:T(8,128)S(1)} %add.202), channel_id=1, source_target_pairs={{0,4},{1,5},{2,6},{3,7},{4,0},{5,1},{6,2},{7,3},{8,12},{9,13},{10,... | collective-permute-start | bytes 175508 | tf_op jit(solution)/shard_map/ppermute | solution.py:177
  101.4 6.4 %collective-permute-start.11 = (f32[225,65]{0,1:T(8,128)S(1)}, f32[225,65]{0,1:T(8,128)S(1)}, u32[]{:S(2)}, u32[]{:S(2)}) collective-permute-start(f32[225,65]{0,1:T(8,128)S(1)} %add.203), channel_id=1, source_target_pairs={{0,8},{1,9},{2,10},{3,11},{4,12},{5,13},{6,14},{7,15},{8,0},{9,1},... | collective-permute-start | bytes 175508 | tf_op jit(solution)/shard_map/ppermute | solution.py:177
  107.8 15.5 %collective-permute-start.12 = (f32[225,65]{0,1:T(8,128)S(1)}, f32[225,65]{0,1:T(8,128)S(1)}, u32[]{:S(2)}, u32[]{:S(2)}) collective-permute-start(f32[225,65]{0,1:T(8,128)S(1)} %add.204), channel_id=1, source_target_pairs={{0,16},{1,17},{2,18},{3,19},{4,20},{5,21},{6,22},{7,23},{8,24},{9,... | collective-permute-start | bytes 175508 | tf_op jit(solution)/shard_map/ppermute | solution.py:177
  128.7 21.7 %collective-permute-start.13 = (f32[9,192]{1,0:T(8,128)S(1)}, f32[9,192]{1,0:T(8,128)S(1)}, u32[]{:S(2)}, u32[]{:S(2)}) collective-permute-start(f32[9,192]{1,0:T(8,128)S(1)} %get-tuple-element.21), channel_id=1, source_target_pairs={{0,1},{1,2},{2,3},{3,4},{4,5},{5,6},{6,7},{7,8},{8,9},{9,10},{10,1... | collective-permute-start | bytes 20744 | tf_op jit(solution)/shard_map/ppermute | solution.py:86
  130.3 20.1 %collective-permute-start.14 = (f32[9,192]{1,0:T(8,128)S(1)}, f32[9,192]{1,0:T(8,128)S(1)}, u32[]{:S(2)}, u32[]{:S(2)}) collective-permute-start(f32[9,192]{1,0:T(8,128)S(1)} %get-tuple-element.22), channel_id=1, source_target_pairs={{1,0},{2,1},{3,2},{4,3},{5,4},{6,5},{7,6},{8,7},{9,8},{10,9},{11,1... | collective-permute-start | bytes 20744 | tf_op jit(solution)/shard_map/ppermute | solution.py:86
  131.9 7.3 %collective-permute-start.15 = (f32[9,48]{1,0:T(8,128)S(1)}, f32[9,48]{1,0:T(8,128)S(1)}, u32[]{:S(2)}, u32[]{:S(2)}) collective-permute-start(f32[9,48]{1,0:T(8,128)S(1)} %get-tuple-element.25), channel_id=1, source_target_pairs={{0,32},{32,64},{64,96},{96,128},{128,160},{160,192},{192,224},{224... | collective-permute-start | bytes 5192 | tf_op jit(solution)/shard_map/ppermute | solution.py:86
  136.7 13.7 %collective-permute-start.16 = (f32[9,48]{1,0:T(8,128)S(1)}, f32[9,48]{1,0:T(8,128)S(1)}, u32[]{:S(2)}, u32[]{:S(2)}) collective-permute-start(f32[9,48]{1,0:T(8,128)S(1)} %get-tuple-element.26), channel_id=1, source_target_pairs={{32,0},{64,32},{96,64},{128,96},{160,128},{192,160},{224,192},{256... | collective-permute-start | bytes 5192 | tf_op jit(solution)/shard_map/ppermute | solution.py:86
  156.0 26.8 %collective-permute-start.17 = (f32[36,192]{1,0:T(8,128)S(1)}, f32[36,192]{1,0:T(8,128)S(1)}, u32[]{:S(2)}, u32[]{:S(2)}) collective-permute-start(f32[36,192]{1,0:T(8,128)S(1)} %get-tuple-element.13), channel_id=1, source_target_pairs={{0,1},{1,2},{2,3},{3,4},{4,5},{5,6},{6,7},{7,8},{8,9},{9,10},{10,1... | collective-permute-start | bytes 82952 | tf_op jit(solution)/shard_map/ppermute | solution.py:86
  160.2 22.5 %collective-permute-start.18 = (f32[36,192]{1,0:T(8,128)S(1)}, f32[36,192]{1,0:T(8,128)S(1)}, u32[]{:S(2)}, u32[]{:S(2)}) collective-permute-start(f32[36,192]{1,0:T(8,128)S(1)} %get-tuple-element.14), channel_id=1, source_target_pairs={{1,0},{2,1},{3,2},{4,3},{5,4},{6,5},{7,6},{8,7},{9,8},{10,9},{11,1... | collective-permute-start | bytes 82952 | tf_op jit(solution)/shard_map/ppermute | solution.py:86
  161.9 10.2 %collective-permute-start.19 = (f32[36,48]{1,0:T(8,128)S(1)}, f32[36,48]{1,0:T(8,128)S(1)}, u32[]{:S(2)}, u32[]{:S(2)}) collective-permute-start(f32[36,48]{1,0:T(8,128)S(1)} %get-tuple-element.17), channel_id=1, source_target_pairs={{0,32},{32,64},{64,96},{96,128},{128,160},{160,192},{192,224},{224... | collective-permute-start | bytes 20744 | tf_op jit(solution)/shard_map/ppermute | solution.py:86
  168.5 14.2 %collective-permute-start.20 = (f32[36,48]{1,0:T(8,128)S(1)}, f32[36,48]{1,0:T(8,128)S(1)}, u32[]{:S(2)}, u32[]{:S(2)}) collective-permute-start(f32[36,48]{1,0:T(8,128)S(1)} %get-tuple-element.18), channel_id=1, source_target_pairs={{32,0},{64,32},{96,64},{128,96},{160,128},{192,160},{224,192},{256... | collective-permute-start | bytes 20744 | tf_op jit(solution)/shard_map/ppermute | solution.py:86
  (26 other events, 95.7 us)

commit v2 on v1

--- a/solution.py
+++ b/solution.py
@@ -68,7 +68,7 @@
     ghosts = 2 * group_count + 2 * region_count
     slots = jnp.arange(elements, dtype=jnp.int32)
     sources = jnp.arange(elements + ghosts, dtype=jnp.int32)
-    gather = (neighbor.T[:, None, :] == sources[None, :, None]).astype(jnp.float32)
+    gather = (neighbor.T[:, None, :] == sources[None, :, None]).astype(jnp.bfloat16)
     pick_group = (send_group[0][:, None, :] == slots[None, :, None]).astype(jnp.float32)
     pick_region = (send_region[0][:, None, :] == slots[None, :, None]).astype(jnp.float32)
     codes = (ghost_orient[0][None, :] == jnp.arange(8, dtype=jnp.int32)[:, None]).astype(
@@ -103,14 +103,12 @@
         "snj,sjk->snk", traces[2:4], pick_region, precision=HIGHEST,
         preferred_element_type=jnp.float32,
     )
+    from_region_low = shift(region_out[1], "region", 1)
+    from_region_high = shift(region_out[0], "region", -1)
+    from_group_low = shift(group_out[1], "group", 1)
+    from_group_high = shift(group_out[0], "group", -1)
     raw = jnp.concatenate(
-        [
-            shift(group_out[1], "group", 1),
-            shift(group_out[0], "group", -1),
-            shift(region_out[1], "region", 1),
-            shift(region_out[0], "region", -1),
-        ],
-        axis=1,
+        [from_group_low, from_group_high, from_region_low, from_region_high], axis=1
     )
     turned = mm(jnp.asarray(orient_matrix(points)), raw).reshape(8, plane, -1)
     ghosts = jnp.sum(turned * codes[:, None, :], axis=0)
@@ -119,7 +117,8 @@
         [swapped, jnp.broadcast_to(ghosts[None], (6,) + ghosts.shape)], axis=2
     )
     outside = jnp.einsum(
-        "fnq,fqe->fne", source, gather, precision=HIGHEST, preferred_element_type=jnp.float32
+        "fnq,fqe->fne", source, gather.astype(jnp.float32), precision=HIGHEST,
+        preferred_element_type=jnp.float32,
     )
     jumps = (traces - outside).reshape(6 * plane, elements)
     return product + mm(select.T, jumps)
@@ -167,15 +166,16 @@
 
 
 def gather_slab(local, width):
-    count = local.shape[0]
     index = lax.axis_index("group")
+    vert_x = BX * width + 1
     full = lax.dynamic_update_slice(
-        jnp.zeros((count, BX * width + 1), jnp.float32), local, (0, BX * index)
-    )
+        jnp.zeros((local.shape[0], vert_x), jnp.float32), local, (0, BX * index)
+    )
+    interior = full.reshape(BZ + 1, BY + 1, vert_x)[1:BZ, 1:BY, 1 : vert_x - 1]
     for bit in range(int(math.log2(width))):
         partner = [(i, i ^ (1 << bit)) for i in range(width)]
-        full = full + lax.ppermute(full, "group", partner)
-    return full
+        interior = interior + lax.ppermute(interior, "group", partner)
+    return interior
 
 
 def body(
@@ -207,14 +207,13 @@
     plane_ids = corner_ids // vert_x
     column = corner_ids - plane_ids * vert_x - BX * lax.axis_index("group")
     on_plane = (plane_ids[None, :] == jnp.arange(planes, dtype=jnp.int32)[:, None]).astype(
-        jnp.float32
-    )
+        jnp.bfloat16
+    ).astype(jnp.float32)
     on_column = (column[:, None] == jnp.arange(BX + 1, dtype=jnp.int32)[None, :]).astype(
         jnp.float32
     )
     local = mm(on_plane, corner_terms.reshape(-1)[:, None] * on_column)
-    assembled = gather_slab(local, width_group)
-    interior = assembled.reshape(BZ + 1, BY + 1, vert_x)[1:BZ, 1:BY, 1 : vert_x - 1]
+    interior = gather_slab(local, width_group)
     solved = coarse_solve(interior)
     padded = jnp.pad(solved, ((1, 1), (1, 1), (1, 1)))
     mine = lax.dynamic_slice_in_dim(padded, BX * lax.axis_index("group"), BX + 1, axis=2)

time: 193 us -> 196 us (1.016)
  no operation moved by 1% of the time
where the time goes in v2:
time: 196 us; the launch traced here: 193 us
  starting transfers between devices  94.7 us (48%)
  waiting for transfers between devices  53.5 us (27%)
  matrix products  30.4 us (16%)
  local copies, waits for them, and re-layouts  11.6 us (6%)
    ppermute x16, starting transfers between devices, shift(): return lax.ppermute(block, axis, pairs)  61.2 us
    ppermute x16, waiting for transfers between devices, shift(): return lax.ppermute(block, axis, pairs)  41.1 us
    ppermute x5, starting transfers between devices, gather_slab(): interior = interior + lax.ppermute(interior, 'group', partner)  33.6 us
    dot_general x22, matrix products, mm(): return jnp.dot(a, b, precision=HIGHEST, preferred_element_type=jnp.float32)  13.1 us
    ppermute x5, waiting for transfers between devices, gather_slab(): interior = interior + lax.ppermute(interior, 'group', partner)  12.4 us
    dot_general x4, matrix products, apply_level(): jnp.einsum('fnq,fqe->fne', source, gather.astype(jnp.float32), precision=...  11.7 us
    unnamed x59, local copies, waits for them, and re-layouts  4.8 us
  transfers between devices with their start and end apart: 21, of which 9 were waited for; matrix products, arithmetic and copies ran while one was open for 4% of the time, Pallas kernels for 0%

profile of v2, /device:TPU:1, one launch (start us, length us, event | category | flops | bytes accessed | tf_op | source)
XLA Modules:
  0.0 193.2 jit_solution(18154656890480682469)
XLA Ops:
  4.6 4.0 %collective-permute-start = (f32[36,192]{1,0:T(8,128)S(1)}, f32[36,192]{1,0:T(8,128)S(1)}, u32[]{:S(2)}, u32[]{:S(2)}) collective-permute-start(f32[36,192]{1,0:T(8,128)S(1)} %get-tuple-element.15), channel_id=1, source_target_pairs={{0,1},{1,2},{2,3},{3,4},{4,5},{5,6},{6,7},{7,8},{8,9},{9,10},{10,1... | collective-permute-start | bytes 82952 | tf_op jit(solution)/shard_map/ppermute | solution.py:86
  10.3 16.3 %collective-permute-start.2 = (f32[36,48]{1,0:T(8,128)S(1)}, f32[36,48]{1,0:T(8,128)S(1)}, u32[]{:S(2)}, u32[]{:S(2)}) collective-permute-start(f32[36,48]{1,0:T(8,128)S(1)} %get-tuple-element.19), channel_id=1, source_target_pairs={{0,32},{32,64},{64,96},{96,128},{128,160},{160,192},{192,224},{224... | collective-permute-start | bytes 20744 | tf_op jit(solution)/shard_map/ppermute | solution.py:86
  32.6 7.8 %collective-permute-done.3 = f32[36,48]{1,0:T(8,128)S(1)} collective-permute-done((f32[36,48]{1,0:T(8,128)S(1)}, f32[36,48]{1,0:T(8,128)S(1)}, u32[]{:S(2)}, u32[]{:S(2)}) %collective-permute-start.3) | collective-permute-done | bytes 6944 | tf_op jit(solution)/shard_map/ppermute | solution.py:86
  42.2 3.6 %fusion.11 = f32[6,36,384]{2,1,0:T(8,128)} fusion(f32[6,36,384]{2,1,0:T(8,128)S(1)} %reshape.280, s32[6,384]{1,0:T(8,128)S(1)} %bitcast.116, f32[6,36,480]{2,1,0:T(8,128)S(1)} %broadcast_in_dim.19, f32[6,36,384]{2,1,0:T(8,128)S(1)} %copy-done.9), kind=kOutput, calls=%fused_computation.18 | convolution fusion | flops 862223616 | bytes 1419264 | tf_op jit(solution)/shard_map/fnq,fqe->fne/dot_general | solution.py:119
  49.2 4.3 %collective-permute-start.4 = (f32[9,192]{1,0:T(8,128)S(1)}, f32[9,192]{1,0:T(8,128)S(1)}, u32[]{:S(2)}, u32[]{:S(2)}) collective-permute-start(f32[9,192]{1,0:T(8,128)S(1)} %get-tuple-element.23), channel_id=1, source_target_pairs={{0,1},{1,2},{2,3},{3,4},{4,5},{5,6},{6,7},{7,8},{8,9},{9,10},{10,1... | collective-permute-start | bytes 20744 | tf_op jit(solution)/shard_map/ppermute | solution.py:86
  55.1 4.9 %collective-permute-start.6 = (f32[9,48]{1,0:T(8,128)S(1)}, f32[9,48]{1,0:T(8,128)S(1)}, u32[]{:S(2)}, u32[]{:S(2)}) collective-permute-start(f32[9,48]{1,0:T(8,128)S(1)} %get-tuple-element.27), channel_id=1, source_target_pairs={{0,32},{32,64},{64,96},{96,128},{128,160},{160,192},{192,224},{224... | collective-permute-start | bytes 5192 | tf_op jit(solution)/shard_map/ppermute | solution.py:86
  62.7 11.4 %collective-permute-done.7 = f32[9,48]{1,0:T(8,128)S(1)} collective-permute-done((f32[9,48]{1,0:T(8,128)S(1)}, f32[9,48]{1,0:T(8,128)S(1)}, u32[]{:S(2)}, u32[]{:S(2)}) %collective-permute-start.7) | collective-permute-done | bytes 1760 | tf_op jit(solution)/shard_map/ppermute | solution.py:86
  74.6 2.7 %fusion.17 = f32[6,9,384]{2,1,0:T(8,128)S(1)} fusion(f32[6,9,384]{2,1,0:T(8,128)S(1)} %reshape.284, s32[6,384]{1,0:T(8,128)S(1)} %bitcast.117, f32[6,9,480]{2,1,0:T(8,128)S(1)} %broadcast_in_dim.22, f32[6,9,384]{2,1,0:T(8,128)S(1)} %gather_fusion.1), kind=kOutput, calls=%fused_computation.28 | convolution fusion | flops 217048896 | bytes 361728 | tf_op jit(solution)/shard_map/fnq,fqe->fne/dot_general | solution.py:119
  79.8 4.2 %collective-permute-start.8 = (f32[23,7,63]{2,1,0:T(8,128)S(1)}, f32[23,7,63]{2,1,0:T(8,128)S(1)}, u32[]{:S(2)}, u32[]{:S(2)}) collective-permute-start(f32[23,7,63]{2,1,0:T(8,128)S(1)} %slice.196), channel_id=1, source_target_pairs={{0,1},{1,0},{2,3},{3,2},{4,5},{5,4},{6,7},{7,6},{8,9},{9,8},{10,11... | collective-permute-start | bytes 121724 | tf_op jit(solution)/shard_map/ppermute | solution.py:177
  84.2 2.7 %collective-permute-done.8 = f32[23,7,63]{2,1,0:T(8,128)S(1)} collective-permute-done((f32[23,7,63]{2,1,0:T(8,128)S(1)}, f32[23,7,63]{2,1,0:T(8,128)S(1)}, u32[]{:S(2)}, u32[]{:S(2)}) %collective-permute-start.8) | collective-permute-done | bytes 40604 | tf_op jit(solution)/shard_map/ppermute | solution.py:177
  86.9 5.1 %collective-permute-start.9 = (f32[23,7,63]{2,1,0:T(8,128)S(1)}, f32[23,7,63]{2,1,0:T(8,128)S(1)}, u32[]{:S(2)}, u32[]{:S(2)}) collective-permute-start(f32[23,7,63]{2,1,0:T(8,128)S(1)} %slice_add_fusion), channel_id=1, source_target_pairs={{0,2},{1,3},{2,0},{3,1},{4,6},{5,7},{6,4},{7,5},{8,10},{9,11},{10,... | collective-permute-start | bytes 121724 | tf_op jit(solution)/shard_map/ppermute | solution.py:177
  94.0 6.6 %collective-permute-start.10 = (f32[23,7,63]{2,1,0:T(8,128)S(1)}, f32[23,7,63]{2,1,0:T(8,128)S(1)}, u32[]{:S(2)}, u32[]{:S(2)}) collective-permute-start(f32[23,7,63]{2,1,0:T(8,128)S(1)} %add.201), channel_id=1, source_target_pairs={{0,4},{1,5},{2,6},{3,7},{4,0},{5,1},{6,2},{7,3},{8,12},{9,13},{10,... | collective-permute-start | bytes 121724 | tf_op jit(solution)/shard_map/ppermute | solution.py:177
  100.6 2.7 %collective-permute-done.10 = f32[23,7,63]{2,1,0:T(8,128)S(1)} collective-permute-done((f32[23,7,63]{2,1,0:T(8,128)S(1)}, f32[23,7,63]{2,1,0:T(8,128)S(1)}, u32[]{:S(2)}, u32[]{:S(2)}) %collective-permute-start.10) | collective-permute-done | bytes 40604 | tf_op jit(solution)/shard_map/ppermute | solution.py:177
  103.3 4.5 %collective-permute-start.11 = (f32[23,7,63]{2,1,0:T(8,128)S(1)}, f32[23,7,63]{2,1,0:T(8,128)S(1)}, u32[]{:S(2)}, u32[]{:S(2)}) collective-permute-start(f32[23,7,63]{2,1,0:T(8,128)S(1)} %add.202), channel_id=1, source_target_pairs={{0,8},{1,9},{2,10},{3,11},{4,12},{5,13},{6,14},{7,15},{8,0},{9,1},... | collective-permute-start | bytes 121724 | tf_op jit(solution)/shard_map/ppermute | solution.py:177
  109.8 13.2 %collective-permute-start.12 = (f32[23,7,63]{2,1,0:T(8,128)S(1)}, f32[23,7,63]{2,1,0:T(8,128)S(1)}, u32[]{:S(2)}, u32[]{:S(2)}) collective-permute-start(f32[23,7,63]{2,1,0:T(8,128)S(1)} %add.203), channel_id=1, source_target_pairs={{0,16},{1,17},{2,18},{3,19},{4,20},{5,21},{6,22},{7,23},{8,24},{9,... | collective-permute-start | bytes 121724 | tf_op jit(solution)/shard_map/ppermute | solution.py:177
  122.9 3.2 %collective-permute-done.12 = f32[23,7,63]{2,1,0:T(8,128)S(1)} collective-permute-done((f32[23,7,63]{2,1,0:T(8,128)S(1)}, f32[23,7,63]{2,1,0:T(8,128)S(1)}, u32[]{:S(2)}, u32[]{:S(2)}) %collective-permute-start.12) | collective-permute-done | bytes 40604 | tf_op jit(solution)/shard_map/ppermute | solution.py:177
  134.8 6.2 %collective-permute-start.15 = (f32[9,48]{1,0:T(8,128)S(1)}, f32[9,48]{1,0:T(8,128)S(1)}, u32[]{:S(2)}, u32[]{:S(2)}) collective-permute-start(f32[9,48]{1,0:T(8,128)S(1)} %get-tuple-element.25), channel_id=1, source_target_pairs={{0,32},{32,64},{64,96},{96,128},{128,160},{160,192},{192,224},{224... | collective-permute-start | bytes 5192 | tf_op jit(solution)/shard_map/ppermute | solution.py:86
  141.1 2.1 %collective-permute-start.16 = (f32[9,48]{1,0:T(8,128)S(1)}, f32[9,48]{1,0:T(8,128)S(1)}, u32[]{:S(2)}, u32[]{:S(2)}) collective-permute-start(f32[9,48]{1,0:T(8,128)S(1)} %get-tuple-element.26), channel_id=1, source_target_pairs={{32,0},{64,32},{96,64},{128,96},{160,128},{192,160},{224,192},{256... | collective-permute-start | bytes 5192 | tf_op jit(solution)/shard_map/ppermute | solution.py:86
  143.8 10.9 %collective-permute-done.16 = f32[9,48]{1,0:T(8,128)S(1)} collective-permute-done((f32[9,48]{1,0:T(8,128)S(1)}, f32[9,48]{1,0:T(8,128)S(1)}, u32[]{:S(2)}, u32[]{:S(2)}) %collective-permute-start.16) | collective-permute-done | bytes 1760 | tf_op jit(solution)/shard_map/ppermute | solution.py:86
  155.2 2.7 %fusion.18 = f32[6,9,384]{2,1,0:T(8,128)S(1)} fusion(f32[6,9,384]{2,1,0:T(8,128)S(1)} %reshape.290, s32[6,384]{1,0:T(8,128)S(1)} %bitcast.118, f32[6,9,480]{2,1,0:T(8,128)S(1)} %broadcast_in_dim.24, f32[6,9,384]{2,1,0:T(8,128)S(1)} %gather_fusion.2), kind=kOutput, calls=%fused_computation.29 | convolution fusion | flops 217048896 | bytes 361728 | tf_op jit(solution)/shard_map/fnq,fqe->fne/dot_general | solution.py:119
  160.4 4.3 %collective-permute-start.17 = (f32[36,192]{1,0:T(8,128)S(1)}, f32[36,192]{1,0:T(8,128)S(1)}, u32[]{:S(2)}, u32[]{:S(2)}) collective-permute-start(f32[36,192]{1,0:T(8,128)S(1)} %get-tuple-element.13), channel_id=1, source_target_pairs={{0,1},{1,2},{2,3},{3,4},{4,5},{5,6},{6,7},{7,8},{8,9},{9,10},{10,1... | collective-permute-start | bytes 82952 | tf_op jit(solution)/shard_map/ppermute | solution.py:86
  166.3 6.0 %collective-permute-start.19 = (f32[36,48]{1,0:T(8,128)S(1)}, f32[36,48]{1,0:T(8,128)S(1)}, u32[]{:S(2)}, u32[]{:S(2)}) collective-permute-start(f32[36,48]{1,0:T(8,128)S(1)} %get-tuple-element.17), channel_id=1, source_target_pairs={{0,32},{32,64},{64,96},{96,128},{128,160},{160,192},{192,224},{224... | collective-permute-start | bytes 20744 | tf_op jit(solution)/shard_map/ppermute | solution.py:86
  175.7 10.9 %collective-permute-done.20 = f32[36,48]{1,0:T(8,128)S(1)} collective-permute-done((f32[36,48]{1,0:T(8,128)S(1)}, f32[36,48]{1,0:T(8,128)S(1)}, u32[]{:S(2)}, u32[]{:S(2)}) %collective-permute-start.20) | collective-permute-done | bytes 6944 | tf_op jit(solution)/shard_map/ppermute | solution.py:86
  188.4 2.8 %fusion.12 = f32[6,36,384]{2,1,0:T(8,128)S(1)} fusion(f32[6,36,384]{2,1,0:T(8,128)S(1)} %copy-done.4, s32[6,384]{1,0:T(8,128)S(1)} %bitcast.119, f32[6,36,480]{2,1,0:T(8,128)S(1)} %broadcast_in_dim.26, f32[6,36,384]{2,1,0:T(8,128)S(1)} %copy-done.8), kind=kOutput, calls=%fused_computation.19 | convolution fusion | flops 862223616 | bytes 1419264 | tf_op jit(solution)/shard_map/fnq,fqe->fne/dot_general | solution.py:119
  (190 shorter events, 49.0 us)
Async XLA Ops:
  3.4 25.2 %copy-start.24 = (s32[6]{0:T(128)S(1)}, s32[6]{0:T(128)}, u32[]{:S(2)}) copy-start(s32[6]{0:T(128)} %constant.126) | copy-start | bytes 76
  3.4 25.2 %copy-start.18 = (s32[384,8]{0,1:T(8,128)S(1)}, s32[384,8]{0,1:T(8,128)}, u32[]{:S(2)}) copy-start(s32[384,8]{0,1:T(8,128)} %param.39) | copy-start | bytes 36868
  4.6 35.8 %collective-permute-start = (f32[36,192]{1,0:T(8,128)S(1)}, f32[36,192]{1,0:T(8,128)S(1)}, u32[]{:S(2)}, u32[]{:S(2)}) collective-permute-start(f32[36,192]{1,0:T(8,128)S(1)} %get-tuple-element.15), channel_id=1, source_target_pairs={{0,1},{1,2},{2,3},{3,4},{4,5},{5,6},{6,7},{7,8},{8,9},{9,10},{10,1... | collective-permute-start | bytes 82952 | tf_op jit(solution)/shard_map/ppermute | solution.py:86
  8.6 31.8 %collective-permute-start.1 = (f32[36,192]{1,0:T(8,128)S(1)}, f32[36,192]{1,0:T(8,128)S(1)}, u32[]{:S(2)}, u32[]{:S(2)}) collective-permute-start(f32[36,192]{1,0:T(8,128)S(1)} %get-tuple-element.16), channel_id=1, source_target_pairs={{1,0},{2,1},{3,2},{4,3},{5,4},{6,5},{7,6},{8,7},{9,8},{10,9},{11,1... | collective-permute-start | bytes 82952 | tf_op jit(solution)/shard_map/ppermute | solution.py:86
  10.3 22.3 %collective-permute-start.2 = (f32[36,48]{1,0:T(8,128)S(1)}, f32[36,48]{1,0:T(8,128)S(1)}, u32[]{:S(2)}, u32[]{:S(2)}) collective-permute-start(f32[36,48]{1,0:T(8,128)S(1)} %get-tuple-element.19), channel_id=1, source_target_pairs={{0,32},{32,64},{64,96},{96,128},{128,160},{160,192},{192,224},{224... | collective-permute-start | bytes 20744 | tf_op jit(solution)/shard_map/ppermute | solution.py:86
  26.6 13.8 %collective-permute-start.3 = (f32[36,48]{1,0:T(8,128)S(1)}, f32[36,48]{1,0:T(8,128)S(1)}, u32[]{:S(2)}, u32[]{:S(2)}) collective-permute-start(f32[36,48]{1,0:T(8,128)S(1)} %get-tuple-element.20), channel_id=1, source_target_pairs={{32,0},{64,32},{96,64},{128,96},{160,128},{192,160},{224,192},{256... | collective-permute-start | bytes 20744 | tf_op jit(solution)/shard_map/ppermute | solution.py:86
  48.6 25.5 %copy-start.11 = (f32[72,9]{1,0:T(8,128)S(1)}, f32[72,9]{1,0:T(8,128)}, u32[]{:S(2)}) copy-start(f32[72,9]{1,0:T(8,128)} %constant.116.clone) | copy-start | bytes 7780
  49.2 24.9 %collective-permute-start.4 = (f32[9,192]{1,0:T(8,128)S(1)}, f32[9,192]{1,0:T(8,128)S(1)}, u32[]{:S(2)}, u32[]{:S(2)}) collective-permute-start(f32[9,192]{1,0:T(8,128)S(1)} %get-tuple-element.23), channel_id=1, source_target_pairs={{0,1},{1,2},{2,3},{3,4},{4,5},{5,6},{6,7},{7,8},{8,9},{9,10},{10,1... | collective-permute-start | bytes 20744 | tf_op jit(solution)/shard_map/ppermute | solution.py:86
  53.5 20.7 %collective-permute-start.5 = (f32[9,192]{1,0:T(8,128)S(1)}, f32[9,192]{1,0:T(8,128)S(1)}, u32[]{:S(2)}, u32[]{:S(2)}) collective-permute-start(f32[9,192]{1,0:T(8,128)S(1)} %get-tuple-element.24), channel_id=1, source_target_pairs={{1,0},{2,1},{3,2},{4,3},{5,4},{6,5},{7,6},{8,7},{9,8},{10,9},{11,1... | collective-permute-start | bytes 20744 | tf_op jit(solution)/shard_map/ppermute | solution.py:86
  55.1 7.7 %collective-permute-start.6 = (f32[9,48]{1,0:T(8,128)S(1)}, f32[9,48]{1,0:T(8,128)S(1)}, u32[]{:S(2)}, u32[]{:S(2)}) collective-permute-start(f32[9,48]{1,0:T(8,128)S(1)} %get-tuple-element.27), channel_id=1, source_target_pairs={{0,32},{32,64},{64,96},{96,128},{128,160},{160,192},{192,224},{224... | collective-permute-start | bytes 5192 | tf_op jit(solution)/shard_map/ppermute | solution.py:86
  59.9 14.2 %collective-permute-start.7 = (f32[9,48]{1,0:T(8,128)S(1)}, f32[9,48]{1,0:T(8,128)S(1)}, u32[]{:S(2)}, u32[]{:S(2)}) collective-permute-start(f32[9,48]{1,0:T(8,128)S(1)} %get-tuple-element.28), channel_id=1, source_target_pairs={{32,0},{64,32},{96,64},{128,96},{160,128},{192,160},{224,192},{256... | collective-permute-start | bytes 5192 | tf_op jit(solution)/shard_map/ppermute | solution.py:86
  79.8 7.0 %collective-permute-start.8 = (f32[23,7,63]{2,1,0:T(8,128)S(1)}, f32[23,7,63]{2,1,0:T(8,128)S(1)}, u32[]{:S(2)}, u32[]{:S(2)}) collective-permute-start(f32[23,7,63]{2,1,0:T(8,128)S(1)} %slice.196), channel_id=1, source_target_pairs={{0,1},{1,0},{2,3},{3,2},{4,5},{5,4},{6,7},{7,6},{8,9},{9,8},{10,11... | collective-permute-start | bytes 121724 | tf_op jit(solution)/shard_map/ppermute | solution.py:177
  86.9 7.0 %collective-permute-start.9 = (f32[23,7,63]{2,1,0:T(8,128)S(1)}, f32[23,7,63]{2,1,0:T(8,128)S(1)}, u32[]{:S(2)}, u32[]{:S(2)}) collective-permute-start(f32[23,7,63]{2,1,0:T(8,128)S(1)} %slice_add_fusion), channel_id=1, source_target_pairs={{0,2},{1,3},{2,0},{3,1},{4,6},{5,7},{6,4},{7,5},{8,10},{9,11},{10,... | collective-permute-start | bytes 121724 | tf_op jit(solution)/shard_map/ppermute | solution.py:177
  94.0 9.3 %collective-permute-start.10 = (f32[23,7,63]{2,1,0:T(8,128)S(1)}, f32[23,7,63]{2,1,0:T(8,128)S(1)}, u32[]{:S(2)}, u32[]{:S(2)}) collective-permute-start(f32[23,7,63]{2,1,0:T(8,128)S(1)} %add.201), channel_id=1, source_target_pairs={{0,4},{1,5},{2,6},{3,7},{4,0},{5,1},{6,2},{7,3},{8,12},{9,13},{10,... | collective-permute-start | bytes 121724 | tf_op jit(solution)/shard_map/ppermute | solution.py:177
  103.3 6.5 %collective-permute-start.11 = (f32[23,7,63]{2,1,0:T(8,128)S(1)}, f32[23,7,63]{2,1,0:T(8,128)S(1)}, u32[]{:S(2)}, u32[]{:S(2)}) collective-permute-start(f32[23,7,63]{2,1,0:T(8,128)S(1)} %add.202), channel_id=1, source_target_pairs={{0,8},{1,9},{2,10},{3,11},{4,12},{5,13},{6,14},{7,15},{8,0},{9,1},... | collective-permute-start | bytes 121724 | tf_op jit(solution)/shard_map/ppermute | solution.py:177
  109.8 16.4 %collective-permute-start.12 = (f32[23,7,63]{2,1,0:T(8,128)S(1)}, f32[23,7,63]{2,1,0:T(8,128)S(1)}, u32[]{:S(2)}, u32[]{:S(2)}) collective-permute-start(f32[23,7,63]{2,1,0:T(8,128)S(1)} %add.203), channel_id=1, source_target_pairs={{0,16},{1,17},{2,18},{3,19},{4,20},{5,21},{6,22},{7,23},{8,24},{9,... | collective-permute-start | bytes 121724 | tf_op jit(solution)/shard_map/ppermute | solution.py:177
  131.4 23.4 %collective-permute-start.13 = (f32[9,192]{1,0:T(8,128)S(1)}, f32[9,192]{1,0:T(8,128)S(1)}, u32[]{:S(2)}, u32[]{:S(2)}) collective-permute-start(f32[9,192]{1,0:T(8,128)S(1)} %get-tuple-element.21), channel_id=1, source_target_pairs={{0,1},{1,2},{2,3},{3,4},{4,5},{5,6},{6,7},{7,8},{8,9},{9,10},{10,1... | collective-permute-start | bytes 20744 | tf_op jit(solution)/shard_map/ppermute | solution.py:86
  133.2 21.5 %collective-permute-start.14 = (f32[9,192]{1,0:T(8,128)S(1)}, f32[9,192]{1,0:T(8,128)S(1)}, u32[]{:S(2)}, u32[]{:S(2)}) collective-permute-start(f32[9,192]{1,0:T(8,128)S(1)} %get-tuple-element.22), channel_id=1, source_target_pairs={{1,0},{2,1},{3,2},{4,3},{5,4},{6,5},{7,6},{8,7},{9,8},{10,9},{11,1... | collective-permute-start | bytes 20744 | tf_op jit(solution)/shard_map/ppermute | solution.py:86
  134.8 9.0 %collective-permute-start.15 = (f32[9,48]{1,0:T(8,128)S(1)}, f32[9,48]{1,0:T(8,128)S(1)}, u32[]{:S(2)}, u32[]{:S(2)}) collective-permute-start(f32[9,48]{1,0:T(8,128)S(1)} %get-tuple-element.25), channel_id=1, source_target_pairs={{0,32},{32,64},{64,96},{96,128},{128,160},{160,192},{192,224},{224... | collective-permute-start | bytes 5192 | tf_op jit(solution)/shard_map/ppermute | solution.py:86
  141.1 13.7 %collective-permute-start.16 = (f32[9,48]{1,0:T(8,128)S(1)}, f32[9,48]{1,0:T(8,128)S(1)}, u32[]{:S(2)}, u32[]{:S(2)}) collective-permute-start(f32[9,48]{1,0:T(8,128)S(1)} %get-tuple-element.26), channel_id=1, source_target_pairs={{32,0},{64,32},{96,64},{128,96},{160,128},{192,160},{224,192},{256... | collective-permute-start | bytes 5192 | tf_op jit(solution)/shard_map/ppermute | solution.py:86
  160.4 26.2 %collective-permute-start.17 = (f32[36,192]{1,0:T(8,128)S(1)}, f32[36,192]{1,0:T(8,128)S(1)}, u32[]{:S(2)}, u32[]{:S(2)}) collective-permute-start(f32[36,192]{1,0:T(8,128)S(1)} %get-tuple-element.13), channel_id=1, source_target_pairs={{0,1},{1,2},{2,3},{3,4},{4,5},{5,6},{6,7},{7,8},{8,9},{9,10},{10,1... | collective-permute-start | bytes 82952 | tf_op jit(solution)/shard_map/ppermute | solution.py:86
  164.6 21.9 %collective-permute-start.18 = (f32[36,192]{1,0:T(8,128)S(1)}, f32[36,192]{1,0:T(8,128)S(1)}, u32[]{:S(2)}, u32[]{:S(2)}) collective-permute-start(f32[36,192]{1,0:T(8,128)S(1)} %get-tuple-element.14), channel_id=1, source_target_pairs={{1,0},{2,1},{3,2},{4,3},{5,4},{6,5},{7,6},{8,7},{9,8},{10,9},{11,1... | collective-permute-start | bytes 82952 | tf_op jit(solution)/shard_map/ppermute | solution.py:86
  166.3 9.4 %collective-permute-start.19 = (f32[36,48]{1,0:T(8,128)S(1)}, f32[36,48]{1,0:T(8,128)S(1)}, u32[]{:S(2)}, u32[]{:S(2)}) collective-permute-start(f32[36,48]{1,0:T(8,128)S(1)} %get-tuple-element.17), channel_id=1, source_target_pairs={{0,32},{32,64},{64,96},{96,128},{128,160},{160,192},{192,224},{224... | collective-permute-start | bytes 20744 | tf_op jit(solution)/shard_map/ppermute | solution.py:86
  172.3 14.2 %collective-permute-start.20 = (f32[36,48]{1,0:T(8,128)S(1)}, f32[36,48]{1,0:T(8,128)S(1)}, u32[]{:S(2)}, u32[]{:S(2)}) collective-permute-start(f32[36,48]{1,0:T(8,128)S(1)} %get-tuple-element.18), channel_id=1, source_target_pairs={{32,0},{64,32},{96,64},{128,96},{160,128},{192,160},{224,192},{256... | collective-permute-start | bytes 20744 | tf_op jit(solution)/shard_map/ppermute | solution.py:86
  (26 other events, 93.6 us)

commit v3 on v2

--- a/solution.py
+++ b/solution.py
@@ -86,7 +86,7 @@
     return lax.ppermute(block, axis, pairs)
 
 
-def apply_level(current, stiffness, points, tables):
+def apply_level(current, stiffness, points, tables, extra=None, group_ghosts=None):
     gather, pick_group, pick_region, codes = tables
     plane = points * points
     cube = points**3
@@ -95,20 +95,26 @@
     both = mm(jnp.concatenate([stiffness, select], axis=0), current)
     product = both[:cube]
     traces = both[cube:].reshape(6, plane, elements)
-    group_out = jnp.einsum(
-        "snj,sjk->snk", traces[0:2], pick_group, precision=HIGHEST,
-        preferred_element_type=jnp.float32,
-    )
     region_out = jnp.einsum(
         "snj,sjk->snk", traces[2:4], pick_region, precision=HIGHEST,
         preferred_element_type=jnp.float32,
     )
     from_region_low = shift(region_out[1], "region", 1)
     from_region_high = shift(region_out[0], "region", -1)
-    from_group_low = shift(group_out[1], "group", 1)
-    from_group_high = shift(group_out[0], "group", -1)
+    received = None
+    if group_ghosts is None:
+        group_out = jnp.einsum(
+            "snj,sjk->snk", traces[0:2], pick_group, precision=HIGHEST,
+            preferred_element_type=jnp.float32,
+        )
+        if extra is not None:
+            group_out = jnp.concatenate([group_out, extra], axis=1)
+        from_group_low = shift(group_out[1], "group", 1)
+        from_group_high = shift(group_out[0], "group", -1)
+        received = (from_group_low[plane:], from_group_high[plane:])
+        group_ghosts = (from_group_low[:plane], from_group_high[:plane])
     raw = jnp.concatenate(
-        [from_group_low, from_group_high, from_region_low, from_region_high], axis=1
+        [group_ghosts[0], group_ghosts[1], from_region_low, from_region_high], axis=1
     )
     turned = mm(jnp.asarray(orient_matrix(points)), raw).reshape(8, plane, -1)
     ghosts = jnp.sum(turned * codes[:, None, :], axis=0)
@@ -121,7 +127,21 @@
         preferred_element_type=jnp.float32,
     )
     jumps = (traces - outside).reshape(6 * plane, elements)
-    return product + mm(select.T, jumps)
+    return product + mm(select.T, jumps), received
+
+
+def corner_values(window, ids, first_column, planes, vert_x):
+    flat = ids.reshape(-1)
+    plane_ids = flat // vert_x
+    column = flat - plane_ids * vert_x - first_column
+    on_plane = (plane_ids[None, :] == jnp.arange(planes, dtype=jnp.int32)[:, None]).astype(
+        jnp.float32
+    )
+    on_column = (
+        column[:, None] == jnp.arange(window.shape[1], dtype=jnp.int32)[None, :]
+    ).astype(jnp.float32)
+    picked = mm(window.T, on_plane)
+    return jnp.sum(picked * on_column.T, axis=0).reshape(ids.shape)
 
 
 def sine_basis(extent):
@@ -193,38 +213,60 @@
     corners,
 ):
     tables = make_tables(neighbor, send_group, send_region, ghost_orient)
+    width_group = lax.axis_size("group")
+    index = lax.axis_index("group")
+    vert_x = width_group * BX + 1
+    planes = (BZ + 1) * (BY + 1)
+    corner_ids = corners.T
+    sent_ids = jnp.einsum(
+        "nj,sjk->snk", corner_ids.astype(jnp.float32), tables[1], precision=HIGHEST,
+        preferred_element_type=jnp.float32,
+    )
+
     smoothed = mm(smooth_fine, right_side)
-    residual = right_side - apply_level(smoothed, stiff_fine, FINE_PTS, tables)
+    operated, received = apply_level(smoothed, stiff_fine, FINE_PTS, tables, extra=sent_ids)
+    residual = right_side - operated
+    neighbor_ids = jnp.round(jnp.concatenate(received, axis=1)).astype(jnp.int32)
     middle_rhs = mm(restrict_fine, residual)
     middle_fix = mm(smooth_middle, middle_rhs)
-    middle_res = middle_rhs - apply_level(middle_fix, stiff_middle, MID_PTS, tables)
+    middle_res = middle_rhs - apply_level(middle_fix, stiff_middle, MID_PTS, tables)[0]
     corner_terms = mm(restrict_middle, middle_res)
 
-    width_group = lax.axis_size("group")
-    vert_x = width_group * BX + 1
-    planes = (BZ + 1) * (BY + 1)
-    corner_ids = corners.T.reshape(-1)
-    plane_ids = corner_ids // vert_x
-    column = corner_ids - plane_ids * vert_x - BX * lax.axis_index("group")
+    plane_ids = corner_ids.reshape(-1) // vert_x
+    column = corner_ids.reshape(-1) - plane_ids * vert_x - BX * index
     on_plane = (plane_ids[None, :] == jnp.arange(planes, dtype=jnp.int32)[:, None]).astype(
-        jnp.bfloat16
-    ).astype(jnp.float32)
+        jnp.float32
+    )
     on_column = (column[:, None] == jnp.arange(BX + 1, dtype=jnp.int32)[None, :]).astype(
         jnp.float32
     )
     local = mm(on_plane, corner_terms.reshape(-1)[:, None] * on_column)
     interior = gather_slab(local, width_group)
     solved = coarse_solve(interior)
-    padded = jnp.pad(solved, ((1, 1), (1, 1), (1, 1)))
-    mine = lax.dynamic_slice_in_dim(padded, BX * lax.axis_index("group"), BX + 1, axis=2)
-    picked = mm(mine.reshape(planes, BX + 1).T, on_plane)
-    coarse_fix = jnp.sum(picked * on_column.T, axis=0).reshape(corners.shape[1], -1)
-
-    middle_corr = middle_fix + mm(restrict_middle.T, coarse_fix)
-    middle_left = middle_rhs - apply_level(middle_corr, stiff_middle, MID_PTS, tables)
+    padded = jnp.pad(solved, ((1, 1), (1, 1), (1 + BX, 1 + BX)))
+    window = lax.dynamic_slice_in_dim(padded, BX * index, 3 * BX + 1, axis=2)
+    window = window.reshape(planes, 3 * BX + 1)
+    mine = window[:, BX : 2 * BX + 1]
+    coarse_fix = corner_values(mine, corner_ids, BX * index, planes, vert_x)
+    neighbor_fix = corner_values(window, neighbor_ids, BX * (index - 1), planes, vert_x)
+    face_select = trace_matrix(MID_PTS).reshape(6, MID_PTS**2, MID_PTS**3)
+    neighbor_corr = mm(restrict_middle.T, neighbor_fix)
+    count = send_group.shape[2]
+    low_valid = (index > 0).astype(jnp.float32)
+    high_valid = (index < width_group - 1).astype(jnp.float32)
+    group_ghosts = (
+        mm(jnp.asarray(face_select[1]), neighbor_corr[:, :count]) * low_valid,
+        mm(jnp.asarray(face_select[0]), neighbor_corr[:, count:]) * high_valid,
+    )
+
+    correction = mm(restrict_middle.T, coarse_fix)
+    middle_corr = middle_fix + correction
+    middle_left = middle_res - apply_level(
+        correction, stiff_middle, MID_PTS, tables, group_ghosts=group_ghosts
+    )[0]
     middle_post = middle_corr + mm(smooth_middle, middle_left)
     current = smoothed + mm(restrict_fine.T, middle_post)
-    left_over = right_side - apply_level(current, stiff_fine, FINE_PTS, tables)
+    left_over = right_side - apply_level(current, stiff_fine, FINE_PTS, tables)[0]
     return current + mm(smooth_fine, left_over)
 
 

time: 196 us -> 190 us (0.969); the launches traced: 193 us -> 189 us
  starting transfers between devices: 94.7 us -> 89.9 us
  waiting for transfers between devices: 53.5 us -> 51.1 us
    ppermute x16 -> x14, starting transfers between devices: 61.2 us -> 55.9 us  [shift(): return lax.ppermute(block, axis, pairs)]
    dot_general x22 -> x26, matrix products: 13.1 us -> 14.7 us  [mm(): return jnp.dot(a, b, precision=HIGHEST, preferred_element_type=jnp.float32)]
    ppermute x16 -> x14, waiting for transfers between devices: 41.1 us -> 40 us  [shift(): return lax.ppermute(block, axis, pairs)]
    unnamed x59 -> x67, local copies, waits for them, and re-layouts: 4.8 us -> 4.79 us
  transfers between devices with their start and end apart: 21 -> 19, of which waited for: 9 -> 9; matrix products, arithmetic and copies ran while one was open for 4% -> 5% of each run, Pallas kernels for 0% -> 0%
where the time goes in v3:
time: 190 us; the launch traced here: 189 us
  starting transfers between devices  89.9 us (47%)
  waiting for transfers between devices  51.1 us (27%)
  matrix products  32 us (17%)
  local copies, waits for them, and re-layouts  13.1 us (7%)
  other arithmetic  1.94 us (1%)
    ppermute x14, starting transfers between devices, shift(): return lax.ppermute(block, axis, pairs)  55.9 us
    ppermute x14, waiting for transfers between devices, shift(): return lax.ppermute(block, axis, pairs)  40 us
    ppermute x5, starting transfers between devices, gather_slab(): interior = interior + lax.ppermute(interior, 'group', partner)  34 us
    dot_general x26, matrix products, mm(): return jnp.dot(a, b, precision=HIGHEST, preferred_element_type=jnp.float32)  14.7 us
    dot_general x4, matrix products, apply_level(): jnp.einsum('fnq,fqe->fne', source, gather.astype(jnp.float32), precision=...  11.7 us
    ppermute x5, waiting for transfers between devices, gather_slab(): interior = interior + lax.ppermute(interior, 'group', partner)  11.1 us
    unnamed x67, local copies, waits for them, and re-layouts  4.79 us
  transfers between devices with their start and end apart: 19, of which 9 were waited for; matrix products, arithmetic and copies ran while one was open for 5% of the time, Pallas kernels for 0%

profile of v3, /device:TPU:1, one launch (start us, length us, event | category | flops | bytes accessed | tf_op | source)
XLA Modules:
  0.0 189.4 jit_solution(9547601404748167419)
XLA Ops:
  5.2 4.0 %collective-permute-start = (f32[44,192]{1,0:T(8,128)S(1)}, f32[44,192]{1,0:T(8,128)S(1)}, u32[]{:S(2)}, u32[]{:S(2)}) collective-permute-start(f32[44,192]{1,0:T(8,128)S(1)} %get-tuple-element.11), channel_id=1, source_target_pairs={{0,1},{1,2},{2,3},{3,4},{4,5},{5,6},{6,7},{7,8},{8,9},{9,10},{10,1... | collective-permute-start | bytes 101384 | tf_op jit(solution)/shard_map/ppermute | solution.py:86
  10.8 16.3 %collective-permute-start.2 = (f32[36,48]{1,0:T(8,128)S(1)}, f32[36,48]{1,0:T(8,128)S(1)}, u32[]{:S(2)}, u32[]{:S(2)}) collective-permute-start(f32[36,48]{1,0:T(8,128)S(1)} %get-tuple-element.17), channel_id=1, source_target_pairs={{0,32},{32,64},{64,96},{96,128},{128,160},{160,192},{192,224},{224... | collective-permute-start | bytes 20744 | tf_op jit(solution)/shard_map/ppermute | solution.py:86
  33.3 7.7 %collective-permute-done.3 = f32[36,48]{1,0:T(8,128)S(1)} collective-permute-done((f32[36,48]{1,0:T(8,128)S(1)}, f32[36,48]{1,0:T(8,128)S(1)}, u32[]{:S(2)}, u32[]{:S(2)}) %collective-permute-start.3) | collective-permute-done | bytes 6944 | tf_op jit(solution)/shard_map/ppermute | solution.py:86
  42.7 3.6 %fusion.12 = f32[6,36,384]{2,1,0:T(8,128)} fusion(f32[6,36,384]{2,1,0:T(8,128)S(1)} %reshape.319, s32[6,384]{1,0:T(8,128)S(1)} %bitcast.129, f32[6,36,480]{2,1,0:T(8,128)S(1)} %broadcast_in_dim.19, f32[6,36,384]{2,1,0:T(8,128)S(1)} %copy-done.9), kind=kOutput, calls=%fused_computation.21 | convolution fusion | flops 862223616 | bytes 1419264 | tf_op jit(solution)/shard_map/fnq,fqe->fne/dot_general | solution.py:125
  49.7 4.3 %collective-permute-start.4 = (f32[9,192]{1,0:T(8,128)S(1)}, f32[9,192]{1,0:T(8,128)S(1)}, u32[]{:S(2)}, u32[]{:S(2)}) collective-permute-start(f32[9,192]{1,0:T(8,128)S(1)} %get-tuple-element.19), channel_id=1, source_target_pairs={{0,1},{1,2},{2,3},{3,4},{4,5},{5,6},{6,7},{7,8},{8,9},{9,10},{10,1... | collective-permute-start | bytes 20744 | tf_op jit(solution)/shard_map/ppermute | solution.py:86
  55.6 5.5 %collective-permute-start.6 = (f32[9,48]{1,0:T(8,128)S(1)}, f32[9,48]{1,0:T(8,128)S(1)}, u32[]{:S(2)}, u32[]{:S(2)}) collective-permute-start(f32[9,48]{1,0:T(8,128)S(1)} %get-tuple-element.23), channel_id=1, source_target_pairs={{0,32},{32,64},{64,96},{96,128},{128,160},{160,192},{192,224},{224... | collective-permute-start | bytes 5192 | tf_op jit(solution)/shard_map/ppermute | solution.py:86
  61.1 2.1 %collective-permute-start.7 = (f32[9,48]{1,0:T(8,128)S(1)}, f32[9,48]{1,0:T(8,128)S(1)}, u32[]{:S(2)}, u32[]{:S(2)}) collective-permute-start(f32[9,48]{1,0:T(8,128)S(1)} %get-tuple-element.24), channel_id=1, source_target_pairs={{32,0},{64,32},{96,64},{128,96},{160,128},{192,160},{224,192},{256... | collective-permute-start | bytes 5192 | tf_op jit(solution)/shard_map/ppermute | solution.py:86
  63.9 10.9 %collective-permute-done.7 = f32[9,48]{1,0:T(8,128)S(1)} collective-permute-done((f32[9,48]{1,0:T(8,128)S(1)}, f32[9,48]{1,0:T(8,128)S(1)}, u32[]{:S(2)}, u32[]{:S(2)}) %collective-permute-start.7) | collective-permute-done | bytes 1760 | tf_op jit(solution)/shard_map/ppermute | solution.py:86
  75.3 2.7 %fusion.18 = f32[6,9,384]{2,1,0:T(8,128)S(1)} fusion(f32[6,9,384]{2,1,0:T(8,128)S(1)} %reshape.323, s32[6,384]{1,0:T(8,128)S(1)} %bitcast.130, f32[6,9,480]{2,1,0:T(8,128)S(1)} %broadcast_in_dim.22, f32[6,9,384]{2,1,0:T(8,128)S(1)} %gather_fusion.1), kind=kOutput, calls=%fused_computation.31 | convolution fusion | flops 217048896 | bytes 361728 | tf_op jit(solution)/shard_map/fnq,fqe->fne/dot_general | solution.py:125
  80.5 4.5 %collective-permute-start.8 = (f32[23,7,63]{2,1,0:T(8,128)S(1)}, f32[23,7,63]{2,1,0:T(8,128)S(1)}, u32[]{:S(2)}, u32[]{:S(2)}) collective-permute-start(f32[23,7,63]{2,1,0:T(8,128)S(1)} %slice.209), channel_id=1, source_target_pairs={{0,1},{1,0},{2,3},{3,2},{4,5},{5,4},{6,7},{7,6},{8,9},{9,8},{10,11... | collective-permute-start | bytes 121724 | tf_op jit(solution)/shard_map/ppermute | solution.py:197
  85.0 2.8 %collective-permute-done.8 = f32[23,7,63]{2,1,0:T(8,128)S(1)} collective-permute-done((f32[23,7,63]{2,1,0:T(8,128)S(1)}, f32[23,7,63]{2,1,0:T(8,128)S(1)}, u32[]{:S(2)}, u32[]{:S(2)}) %collective-permute-start.8) | collective-permute-done | bytes 40604 | tf_op jit(solution)/shard_map/ppermute | solution.py:197
  88.0 5.3 %collective-permute-start.9 = (f32[23,7,63]{2,1,0:T(8,128)S(1)}, f32[23,7,63]{2,1,0:T(8,128)S(1)}, u32[]{:S(2)}, u32[]{:S(2)}) collective-permute-start(f32[23,7,63]{2,1,0:T(8,128)S(1)} %slice_add_fusion), channel_id=1, source_target_pairs={{0,2},{1,3},{2,0},{3,1},{4,6},{5,7},{6,4},{7,5},{8,10},{9,11},{10,... | collective-permute-start | bytes 121724 | tf_op jit(solution)/shard_map/ppermute | solution.py:197
  95.2 6.6 %collective-permute-start.10 = (f32[23,7,63]{2,1,0:T(8,128)S(1)}, f32[23,7,63]{2,1,0:T(8,128)S(1)}, u32[]{:S(2)}, u32[]{:S(2)}) collective-permute-start(f32[23,7,63]{2,1,0:T(8,128)S(1)} %add.213), channel_id=1, source_target_pairs={{0,4},{1,5},{2,6},{3,7},{4,0},{5,1},{6,2},{7,3},{8,12},{9,13},{10,... | collective-permute-start | bytes 121724 | tf_op jit(solution)/shard_map/ppermute | solution.py:197
  104.5 4.5 %collective-permute-start.11 = (f32[23,7,63]{2,1,0:T(8,128)S(1)}, f32[23,7,63]{2,1,0:T(8,128)S(1)}, u32[]{:S(2)}, u32[]{:S(2)}) collective-permute-start(f32[23,7,63]{2,1,0:T(8,128)S(1)} %add.214), channel_id=1, source_target_pairs={{0,8},{1,9},{2,10},{3,11},{4,12},{5,13},{6,14},{7,15},{8,0},{9,1},... | collective-permute-start | bytes 121724 | tf_op jit(solution)/shard_map/ppermute | solution.py:197
  111.0 13.2 %collective-permute-start.12 = (f32[23,7,63]{2,1,0:T(8,128)S(1)}, f32[23,7,63]{2,1,0:T(8,128)S(1)}, u32[]{:S(2)}, u32[]{:S(2)}) collective-permute-start(f32[23,7,63]{2,1,0:T(8,128)S(1)} %add.215), channel_id=1, source_target_pairs={{0,16},{1,17},{2,18},{3,19},{4,20},{5,21},{6,22},{7,23},{8,24},{9,... | collective-permute-start | bytes 121724 | tf_op jit(solution)/shard_map/ppermute | solution.py:197
  124.2 3.2 %collective-permute-done.12 = f32[23,7,63]{2,1,0:T(8,128)S(1)} collective-permute-done((f32[23,7,63]{2,1,0:T(8,128)S(1)}, f32[23,7,63]{2,1,0:T(8,128)S(1)}, u32[]{:S(2)}, u32[]{:S(2)}) %collective-permute-start.12) | collective-permute-done | bytes 40604 | tf_op jit(solution)/shard_map/ppermute | solution.py:197
  133.7 5.6 %collective-permute-start.13 = (f32[9,48]{1,0:T(8,128)S(1)}, f32[9,48]{1,0:T(8,128)S(1)}, u32[]{:S(2)}, u32[]{:S(2)}) collective-permute-start(f32[9,48]{1,0:T(8,128)S(1)} %get-tuple-element.21), channel_id=1, source_target_pairs={{0,32},{32,64},{64,96},{96,128},{128,160},{160,192},{192,224},{224... | collective-permute-start | bytes 5192 | tf_op jit(solution)/shard_map/ppermute | solution.py:86
  139.3 2.1 %collective-permute-start.14 = (f32[9,48]{1,0:T(8,128)S(1)}, f32[9,48]{1,0:T(8,128)S(1)}, u32[]{:S(2)}, u32[]{:S(2)}) collective-permute-start(f32[9,48]{1,0:T(8,128)S(1)} %get-tuple-element.22), channel_id=1, source_target_pairs={{32,0},{64,32},{96,64},{128,96},{160,128},{192,160},{224,192},{256... | collective-permute-start | bytes 5192 | tf_op jit(solution)/shard_map/ppermute | solution.py:86
  142.5 10.5 %collective-permute-done.14 = f32[9,48]{1,0:T(8,128)S(1)} collective-permute-done((f32[9,48]{1,0:T(8,128)S(1)}, f32[9,48]{1,0:T(8,128)S(1)}, u32[]{:S(2)}, u32[]{:S(2)}) %collective-permute-start.14) | collective-permute-done | bytes 1760 | tf_op jit(solution)/shard_map/ppermute | solution.py:86
  153.4 2.7 %fusion.19 = f32[6,9,384]{2,1,0:T(8,128)S(1)} fusion(f32[6,9,384]{2,1,0:T(8,128)S(1)} %reshape.329, s32[6,384]{1,0:T(8,128)S(1)} %bitcast.131, f32[6,9,480]{2,1,0:T(8,128)S(1)} %broadcast_in_dim.24, f32[6,9,384]{2,1,0:T(8,128)S(1)} %gather_fusion.2), kind=kOutput, calls=%fused_computation.32 | convolution fusion | flops 217048896 | bytes 361728 | tf_op jit(solution)/shard_map/fnq,fqe->fne/dot_general | solution.py:125
  158.6 2.2 %collective-permute-start.15 = (f32[36,192]{1,0:T(8,128)S(1)}, f32[36,192]{1,0:T(8,128)S(1)}, u32[]{:S(2)}, u32[]{:S(2)}) collective-permute-start(f32[36,192]{1,0:T(8,128)S(1)} %get-tuple-element.13), channel_id=1, source_target_pairs={{0,1},{1,2},{2,3},{3,4},{4,5},{5,6},{6,7},{7,8},{8,9},{9,10},{10,1... | collective-permute-start | bytes 82952 | tf_op jit(solution)/shard_map/ppermute | solution.py:86
  162.4 6.0 %collective-permute-start.17 = (f32[36,48]{1,0:T(8,128)S(1)}, f32[36,48]{1,0:T(8,128)S(1)}, u32[]{:S(2)}, u32[]{:S(2)}) collective-permute-start(f32[36,48]{1,0:T(8,128)S(1)} %get-tuple-element.15), channel_id=1, source_target_pairs={{0,32},{32,64},{64,96},{96,128},{128,160},{160,192},{192,224},{224... | collective-permute-start | bytes 20744 | tf_op jit(solution)/shard_map/ppermute | solution.py:86
  171.8 10.8 %collective-permute-done.18 = f32[36,48]{1,0:T(8,128)S(1)} collective-permute-done((f32[36,48]{1,0:T(8,128)S(1)}, f32[36,48]{1,0:T(8,128)S(1)}, u32[]{:S(2)}, u32[]{:S(2)}) %collective-permute-start.18) | collective-permute-done | bytes 6944 | tf_op jit(solution)/shard_map/ppermute | solution.py:86
  184.5 2.8 %fusion.13 = f32[6,36,384]{2,1,0:T(8,128)S(1)} fusion(f32[6,36,384]{2,1,0:T(8,128)S(1)} %copy-done.4, s32[6,384]{1,0:T(8,128)S(1)} %bitcast.132, f32[6,36,480]{2,1,0:T(8,128)S(1)} %broadcast_in_dim.26, f32[6,36,384]{2,1,0:T(8,128)S(1)} %copy-done.8), kind=kOutput, calls=%fused_computation.22 | convolution fusion | flops 862223616 | bytes 1419264 | tf_op jit(solution)/shard_map/fnq,fqe->fne/dot_general | solution.py:125
  (204 shorter events, 48.1 us)
Async XLA Ops:
  3.4 25.8 %copy-start.27 = (s32[1,480]{1,0:T(1,128)S(1)}, s32[1,480]{1,0:T(1,128)}, u32[]{:S(2)}) copy-start(s32[1,480]{1,0:T(1,128)} %param.40) | copy-start | bytes 5764
  3.4 27.1 %copy-start.28 = (s32[6]{0:T(128)S(1)}, s32[6]{0:T(128)}, u32[]{:S(2)}) copy-start(s32[6]{0:T(128)} %constant.144) | copy-start | bytes 76
  5.2 28.0 %collective-permute-start = (f32[44,192]{1,0:T(8,128)S(1)}, f32[44,192]{1,0:T(8,128)S(1)}, u32[]{:S(2)}, u32[]{:S(2)}) collective-permute-start(f32[44,192]{1,0:T(8,128)S(1)} %get-tuple-element.11), channel_id=1, source_target_pairs={{0,1},{1,2},{2,3},{3,4},{4,5},{5,6},{6,7},{7,8},{8,9},{9,10},{10,1... | collective-permute-start | bytes 101384 | tf_op jit(solution)/shard_map/ppermute | solution.py:86
  9.2 24.0 %collective-permute-start.1 = (f32[44,192]{1,0:T(8,128)S(1)}, f32[44,192]{1,0:T(8,128)S(1)}, u32[]{:S(2)}, u32[]{:S(2)}) collective-permute-start(f32[44,192]{1,0:T(8,128)S(1)} %get-tuple-element.12), channel_id=1, source_target_pairs={{1,0},{2,1},{3,2},{4,3},{5,4},{6,5},{7,6},{8,7},{9,8},{10,9},{11,1... | collective-permute-start | bytes 101384 | tf_op jit(solution)/shard_map/ppermute | solution.py:86
  10.8 22.4 %collective-permute-start.2 = (f32[36,48]{1,0:T(8,128)S(1)}, f32[36,48]{1,0:T(8,128)S(1)}, u32[]{:S(2)}, u32[]{:S(2)}) collective-permute-start(f32[36,48]{1,0:T(8,128)S(1)} %get-tuple-element.17), channel_id=1, source_target_pairs={{0,32},{32,64},{64,96},{96,128},{128,160},{160,192},{192,224},{224... | collective-permute-start | bytes 20744 | tf_op jit(solution)/shard_map/ppermute | solution.py:86
  27.1 13.8 %collective-permute-start.3 = (f32[36,48]{1,0:T(8,128)S(1)}, f32[36,48]{1,0:T(8,128)S(1)}, u32[]{:S(2)}, u32[]{:S(2)}) collective-permute-start(f32[36,48]{1,0:T(8,128)S(1)} %get-tuple-element.18), channel_id=1, source_target_pairs={{32,0},{64,32},{96,64},{128,96},{160,128},{192,160},{224,192},{256... | collective-permute-start | bytes 20744 | tf_op jit(solution)/shard_map/ppermute | solution.py:86
  49.1 25.7 %copy-start.11 = (f32[72,9]{1,0:T(8,128)S(1)}, f32[72,9]{1,0:T(8,128)}, u32[]{:S(2)}) copy-start(f32[72,9]{1,0:T(8,128)} %constant.132.clone) | copy-start | bytes 7780
  49.7 25.1 %collective-permute-start.4 = (f32[9,192]{1,0:T(8,128)S(1)}, f32[9,192]{1,0:T(8,128)S(1)}, u32[]{:S(2)}, u32[]{:S(2)}) collective-permute-start(f32[9,192]{1,0:T(8,128)S(1)} %get-tuple-element.19), channel_id=1, source_target_pairs={{0,1},{1,2},{2,3},{3,4},{4,5},{5,6},{6,7},{7,8},{8,9},{9,10},{10,1... | collective-permute-start | bytes 20744 | tf_op jit(solution)/shard_map/ppermute | solution.py:86
  54.0 20.8 %collective-permute-start.5 = (f32[9,192]{1,0:T(8,128)S(1)}, f32[9,192]{1,0:T(8,128)S(1)}, u32[]{:S(2)}, u32[]{:S(2)}) collective-permute-start(f32[9,192]{1,0:T(8,128)S(1)} %get-tuple-element.20), channel_id=1, source_target_pairs={{1,0},{2,1},{3,2},{4,3},{5,4},{6,5},{7,6},{8,7},{9,8},{10,9},{11,1... | collective-permute-start | bytes 20744 | tf_op jit(solution)/shard_map/ppermute | solution.py:86
  55.6 8.3 %collective-permute-start.6 = (f32[9,48]{1,0:T(8,128)S(1)}, f32[9,48]{1,0:T(8,128)S(1)}, u32[]{:S(2)}, u32[]{:S(2)}) collective-permute-start(f32[9,48]{1,0:T(8,128)S(1)} %get-tuple-element.23), channel_id=1, source_target_pairs={{0,32},{32,64},{64,96},{96,128},{128,160},{160,192},{192,224},{224... | collective-permute-start | bytes 5192 | tf_op jit(solution)/shard_map/ppermute | solution.py:86
  61.1 13.7 %collective-permute-start.7 = (f32[9,48]{1,0:T(8,128)S(1)}, f32[9,48]{1,0:T(8,128)S(1)}, u32[]{:S(2)}, u32[]{:S(2)}) collective-permute-start(f32[9,48]{1,0:T(8,128)S(1)} %get-tuple-element.24), channel_id=1, source_target_pairs={{32,0},{64,32},{96,64},{128,96},{160,128},{192,160},{224,192},{256... | collective-permute-start | bytes 5192 | tf_op jit(solution)/shard_map/ppermute | solution.py:86
  80.5 7.4 %collective-permute-start.8 = (f32[23,7,63]{2,1,0:T(8,128)S(1)}, f32[23,7,63]{2,1,0:T(8,128)S(1)}, u32[]{:S(2)}, u32[]{:S(2)}) collective-permute-start(f32[23,7,63]{2,1,0:T(8,128)S(1)} %slice.209), channel_id=1, source_target_pairs={{0,1},{1,0},{2,3},{3,2},{4,5},{5,4},{6,7},{7,6},{8,9},{9,8},{10,11... | collective-permute-start | bytes 121724 | tf_op jit(solution)/shard_map/ppermute | solution.py:197
  88.0 7.2 %collective-permute-start.9 = (f32[23,7,63]{2,1,0:T(8,128)S(1)}, f32[23,7,63]{2,1,0:T(8,128)S(1)}, u32[]{:S(2)}, u32[]{:S(2)}) collective-permute-start(f32[23,7,63]{2,1,0:T(8,128)S(1)} %slice_add_fusion), channel_id=1, source_target_pairs={{0,2},{1,3},{2,0},{3,1},{4,6},{5,7},{6,4},{7,5},{8,10},{9,11},{10,... | collective-permute-start | bytes 121724 | tf_op jit(solution)/shard_map/ppermute | solution.py:197
  95.2 9.3 %collective-permute-start.10 = (f32[23,7,63]{2,1,0:T(8,128)S(1)}, f32[23,7,63]{2,1,0:T(8,128)S(1)}, u32[]{:S(2)}, u32[]{:S(2)}) collective-permute-start(f32[23,7,63]{2,1,0:T(8,128)S(1)} %add.213), channel_id=1, source_target_pairs={{0,4},{1,5},{2,6},{3,7},{4,0},{5,1},{6,2},{7,3},{8,12},{9,13},{10,... | collective-permute-start | bytes 121724 | tf_op jit(solution)/shard_map/ppermute | solution.py:197
  102.6 25.7 %copy-start.25 = (f32[23,7]{0,1:T(8,128)S(1)}, f32[23,7]{0,1:T(8,128)}, u32[]{:S(2)}) copy-start(f32[23,7]{0,1:T(8,128)} %get-tuple-element.29) | copy-start | bytes 1936
  102.6 25.7 %copy-start.26 = (f32[23,7]{0,1:T(8,128)S(1)}, f32[23,7]{0,1:T(8,128)}, u32[]{:S(2)}) copy-start(f32[23,7]{0,1:T(8,128)} %get-tuple-element.30) | copy-start | bytes 1936
  104.5 6.5 %collective-permute-start.11 = (f32[23,7,63]{2,1,0:T(8,128)S(1)}, f32[23,7,63]{2,1,0:T(8,128)S(1)}, u32[]{:S(2)}, u32[]{:S(2)}) collective-permute-start(f32[23,7,63]{2,1,0:T(8,128)S(1)} %add.214), channel_id=1, source_target_pairs={{0,8},{1,9},{2,10},{3,11},{4,12},{5,13},{6,14},{7,15},{8,0},{9,1},... | collective-permute-start | bytes 121724 | tf_op jit(solution)/shard_map/ppermute | solution.py:197
  111.0 16.4 %collective-permute-start.12 = (f32[23,7,63]{2,1,0:T(8,128)S(1)}, f32[23,7,63]{2,1,0:T(8,128)S(1)}, u32[]{:S(2)}, u32[]{:S(2)}) collective-permute-start(f32[23,7,63]{2,1,0:T(8,128)S(1)} %add.215), channel_id=1, source_target_pairs={{0,16},{1,17},{2,18},{3,19},{4,20},{5,21},{6,22},{7,23},{8,24},{9,... | collective-permute-start | bytes 121724 | tf_op jit(solution)/shard_map/ppermute | solution.py:197
  133.7 8.8 %collective-permute-start.13 = (f32[9,48]{1,0:T(8,128)S(1)}, f32[9,48]{1,0:T(8,128)S(1)}, u32[]{:S(2)}, u32[]{:S(2)}) collective-permute-start(f32[9,48]{1,0:T(8,128)S(1)} %get-tuple-element.21), channel_id=1, source_target_pairs={{0,32},{32,64},{64,96},{96,128},{128,160},{160,192},{192,224},{224... | collective-permute-start | bytes 5192 | tf_op jit(solution)/shard_map/ppermute | solution.py:86
  139.3 13.7 %collective-permute-start.14 = (f32[9,48]{1,0:T(8,128)S(1)}, f32[9,48]{1,0:T(8,128)S(1)}, u32[]{:S(2)}, u32[]{:S(2)}) collective-permute-start(f32[9,48]{1,0:T(8,128)S(1)} %get-tuple-element.22), channel_id=1, source_target_pairs={{32,0},{64,32},{96,64},{128,96},{160,128},{192,160},{224,192},{256... | collective-permute-start | bytes 5192 | tf_op jit(solution)/shard_map/ppermute | solution.py:86
  158.6 24.0 %collective-permute-start.15 = (f32[36,192]{1,0:T(8,128)S(1)}, f32[36,192]{1,0:T(8,128)S(1)}, u32[]{:S(2)}, u32[]{:S(2)}) collective-permute-start(f32[36,192]{1,0:T(8,128)S(1)} %get-tuple-element.13), channel_id=1, source_target_pairs={{0,1},{1,2},{2,3},{3,4},{4,5},{5,6},{6,7},{7,8},{8,9},{9,10},{10,1... | collective-permute-start | bytes 82952 | tf_op jit(solution)/shard_map/ppermute | solution.py:86
  160.8 21.9 %collective-permute-start.16 = (f32[36,192]{1,0:T(8,128)S(1)}, f32[36,192]{1,0:T(8,128)S(1)}, u32[]{:S(2)}, u32[]{:S(2)}) collective-permute-start(f32[36,192]{1,0:T(8,128)S(1)} %get-tuple-element.14), channel_id=1, source_target_pairs={{1,0},{2,1},{3,2},{4,3},{5,4},{6,5},{7,6},{8,7},{9,8},{10,9},{11,1... | collective-permute-start | bytes 82952 | tf_op jit(solution)/shard_map/ppermute | solution.py:86
  162.4 9.4 %collective-permute-start.17 = (f32[36,48]{1,0:T(8,128)S(1)}, f32[36,48]{1,0:T(8,128)S(1)}, u32[]{:S(2)}, u32[]{:S(2)}) collective-permute-start(f32[36,48]{1,0:T(8,128)S(1)} %get-tuple-element.15), channel_id=1, source_target_pairs={{0,32},{32,64},{64,96},{96,128},{128,160},{160,192},{192,224},{224... | collective-permute-start | bytes 20744 | tf_op jit(solution)/shard_map/ppermute | solution.py:86
  168.4 14.2 %collective-permute-start.18 = (f32[36,48]{1,0:T(8,128)S(1)}, f32[36,48]{1,0:T(8,128)S(1)}, u32[]{:S(2)}, u32[]{:S(2)}) collective-permute-start(f32[36,48]{1,0:T(8,128)S(1)} %get-tuple-element.16), channel_id=1, source_target_pairs={{32,0},{64,32},{96,64},{128,96},{160,128},{192,160},{224,192},{256... | collective-permute-start | bytes 20744 | tf_op jit(solution)/shard_map/ppermute | solution.py:86
  (28 other events, 95.8 us)

commit v4 on v3

--- a/solution.py
+++ b/solution.py
@@ -122,12 +122,23 @@
     source = jnp.concatenate(
         [swapped, jnp.broadcast_to(ghosts[None], (6,) + ghosts.shape)], axis=2
     )
-    outside = jnp.einsum(
-        "fnq,fqe->fne", source, gather.astype(jnp.float32), precision=HIGHEST,
-        preferred_element_type=jnp.float32,
-    )
+    outside = exact_select("fnq,fqe->fne", source, gather, axis=1)
     jumps = (traces - outside).reshape(6 * plane, elements)
     return product + mm(select.T, jumps), received
+
+
+def exact_select(spec, values, picks, axis):
+    high = lax.reduce_precision(values, exponent_bits=8, mantissa_bits=7)
+    rest = values - high
+    middle = lax.reduce_precision(rest, exponent_bits=8, mantissa_bits=7)
+    low = rest - middle
+    parts = jnp.concatenate([high, middle, low], axis=axis).astype(jnp.bfloat16)
+    out = jnp.einsum(spec, parts, picks, preferred_element_type=jnp.float32)
+    size = values.shape[axis]
+    first = lax.slice_in_dim(out, 0, size, axis=axis)
+    second = lax.slice_in_dim(out, size, 2 * size, axis=axis)
+    third = lax.slice_in_dim(out, 2 * size, 3 * size, axis=axis)
+    return first + second + third
 
 
 def corner_values(window, ids, first_column, planes, vert_x):
@@ -157,12 +168,6 @@
         jnp.arange(1, extent + 1, dtype=jnp.int32).astype(jnp.float32) * (math.pi / (extent + 1))
     )
     return (2.0 - 2.0 * cosine, (4.0 + 2.0 * cosine) / 6.0)
-
-
-def transform(volume, basis_z, basis_y, basis_x):
-    turned = jnp.einsum("zyx,xk->zyk", volume, basis_x, precision=HIGHEST)
-    turned = jnp.einsum("zyk,yj->zjk", turned, basis_y, precision=HIGHEST)
-    return jnp.einsum("zjk,zi->ijk", turned, basis_z, precision=HIGHEST)
 
 
 def coarse_solve(interior):
@@ -179,10 +184,13 @@
         stiff_z[:, None, None] * mass_y[None, :, None] * mass_x[None, None, :]
         + mass_z[:, None, None] * stiff_y[None, :, None] * mass_x[None, None, :]
         + mass_z[:, None, None] * mass_y[None, :, None] * stiff_x[None, None, :]
-    )
-    return transform(
-        transform(interior, basis_z, basis_y, basis_x) / eigen_sum, basis_z, basis_y, basis_x
-    )
+    ).reshape(depth_count * height_count, breadth_count)
+    basis_zy = (basis_z[:, None, :, None] * basis_y[None, :, None, :]).reshape(
+        depth_count * height_count, depth_count * height_count
+    )
+    volume = interior.reshape(depth_count * height_count, breadth_count)
+    spectral = mm(basis_zy.T, mm(volume, basis_x)) / eigen_sum
+    return mm(basis_zy.T, mm(spectral, basis_x)).reshape(interior.shape)
 
 
 def gather_slab(local, width):

time: 190 us -> 205 us (1.079)
  local copies, waits for them, and re-layouts: 13.1 us -> 21.5 us
  waiting for transfers between devices: 51.1 us -> 43.2 us
  starting transfers between devices: 89.9 us -> 97.6 us
  other arithmetic: 1.94 us -> 7.87 us
    ppermute x14, starting transfers between devices: 55.9 us -> 64.1 us  [shift(): return lax.ppermute(block, axis, pairs)]
    ppermute x14, waiting for transfers between devices: 40 us -> 32.3 us  [shift(): return lax.ppermute(block, axis, pairs)]
    dot_general x10 -> x4, matrix products: 14.1 us -> 7.78 us  [exact_select(): out = jnp.einsum(spec, parts, picks, preferred_element_type=jnp.float32)]
    mul x0 -> x9, local copies, waits for them, and re-layouts: none -> 5.35 us  [the longest x4 2.75 us: coarse_solve(): stiff_z[:, None, None] * mass_y[None, :, None] * mass_x[None, None, :]]
    dot_general x26 -> x30, matrix products: 14.7 us -> 19.7 us  [mm(): return jnp.dot(a, b, precision=HIGHEST, preferred_element_type=jnp.float32)]
    unnamed x67 -> x73, local copies, waits for them, and re-layouts: 4.79 us -> 3.16 us
  transfers between devices with their start and end apart: 19 -> 19, of which waited for: 9 -> 9; matrix products, arithmetic and copies ran while one was open for 5% -> 9% of each run, Pallas kernels for 0% -> 0%
where the time goes in v4:
time: 205 us; the launch traced here: 203 us
  starting transfers between devices  97.6 us (48%)
  waiting for transfers between devices  43.2 us (21%)
  matrix products  31.5 us (15%)
  local copies, waits for them, and re-layouts  21.5 us (10%)
  other arithmetic  7.87 us (4%)
    ppermute x14, starting transfers between devices, shift(): return lax.ppermute(block, axis, pairs)  64.1 us
    ppermute x5, starting transfers between devices, gather_slab(): interior = interior + lax.ppermute(interior, 'group', partner)  33.5 us
    ppermute x14, waiting for transfers between devices, shift(): return lax.ppermute(block, axis, pairs)  32.3 us
    dot_general x30, matrix products, mm(): return jnp.dot(a, b, precision=HIGHEST, preferred_element_type=jnp.float32)  19.7 us
    ppermute x5, waiting for transfers between devices, gather_slab(): interior = interior + lax.ppermute(interior, 'group', partner)  10.9 us
    dot_general x4, matrix products, exact_select(): out = jnp.einsum(spec, parts, picks, preferred_element_type=jnp.float32)  7.78 us
  transfers between devices with their start and end apart: 19, of which 9 were waited for; matrix products, arithmetic and copies ran while one was open for 9% of the time, Pallas kernels for 0%

profile of v4, /device:TPU:1, one launch (start us, length us, event | category | flops | bytes accessed | tf_op | source)
XLA Modules:
  0.0 203.1 jit_solution(14094980445753953347)
XLA Ops:
  7.0 4.0 %collective-permute-start = (f32[44,192]{1,0:T(8,128)}, f32[44,192]{1,0:T(8,128)S(1)}, u32[]{:S(2)}, u32[]{:S(2)}) collective-permute-start(f32[44,192]{1,0:T(8,128)} %get-tuple-element.23), channel_id=1, source_target_pairs={{0,1},{1,2},{2,3},{3,4},{4,5},{5,6},{6,7},{7,8},{8,9},{9,10},{10,1... | collective-permute-start | bytes 101384 | tf_op jit(solution)/shard_map/ppermute | solution.py:86
  13.2 16.3 %collective-permute-start.2 = (f32[36,48]{1,0:T(8,128)}, f32[36,48]{1,0:T(8,128)}, u32[]{:S(2)}, u32[]{:S(2)}) collective-permute-start(f32[36,48]{1,0:T(8,128)} %get-tuple-element.29), channel_id=1, source_target_pairs={{0,32},{32,64},{64,96},{96,128},{128,160},{160,192},{192,224},{224... | collective-permute-start | bytes 20744 | tf_op jit(solution)/shard_map/ppermute | solution.py:86
  38.5 4.9 %collective-permute-done.3 = f32[36,48]{1,0:T(8,128)} collective-permute-done((f32[36,48]{1,0:T(8,128)S(1)}, f32[36,48]{1,0:T(8,128)}, u32[]{:S(2)}, u32[]{:S(2)}) %collective-permute-start.3) | collective-permute-done | bytes 6944 | tf_op jit(solution)/shard_map/ppermute | solution.py:86
  43.4 2.2 %fusion.65 = f32[288,480]{1,0:T(8,128)} fusion(f32[288,36]{1,0:T(8,128)S(1)} %copy-done.6, f32[36,48]{1,0:T(8,128)} %collective-permute-done.3, f32[36,48]{1,0:T(8,128)} %collective-permute-done.2, f32[36,192]{1,0:T(8,128)S(1)} %slice.245, f32[36,192]{1,0:T(8,128)S(1)} %slice.244), kind=kOutput, calls=%fused_computation.128 | convolution fusion | flops 59771520 | bytes 663552 | tf_op jit(solution)/shard_map/dot_general | solution.py:22
  45.7 2.0 reshape.400
  57.8 4.3 %collective-permute-start.4 = (f32[9,192]{1,0:T(8,128)S(1)}, f32[9,192]{1,0:T(8,128)S(1)}, u32[]{:S(2)}, u32[]{:S(2)}) collective-permute-start(f32[9,192]{1,0:T(8,128)S(1)} %get-tuple-element.31), channel_id=1, source_target_pairs={{0,1},{1,2},{2,3},{3,4},{4,5},{5,6},{6,7},{7,8},{8,9},{9,10},{10,1... | collective-permute-start | bytes 20744 | tf_op jit(solution)/shard_map/ppermute | solution.py:86
  63.7 7.7 %collective-permute-start.6 = (f32[9,48]{1,0:T(8,128)S(1)}, f32[9,48]{1,0:T(8,128)S(1)}, u32[]{:S(2)}, u32[]{:S(2)}) collective-permute-start(f32[9,48]{1,0:T(8,128)S(1)} %get-tuple-element.35), channel_id=1, source_target_pairs={{0,32},{32,64},{64,96},{96,128},{128,160},{160,192},{192,224},{224... | collective-permute-start | bytes 5192 | tf_op jit(solution)/shard_map/ppermute | solution.py:86
  71.5 2.1 %collective-permute-start.7 = (f32[9,48]{1,0:T(8,128)S(1)}, f32[9,48]{1,0:T(8,128)S(1)}, u32[]{:S(2)}, u32[]{:S(2)}) collective-permute-start(f32[9,48]{1,0:T(8,128)S(1)} %get-tuple-element.36), channel_id=1, source_target_pairs={{32,0},{64,32},{96,64},{128,96},{160,128},{192,160},{224,192},{256... | collective-permute-start | bytes 5192 | tf_op jit(solution)/shard_map/ppermute | solution.py:86
  79.1 6.0 %collective-permute-done.7 = f32[9,48]{1,0:T(8,128)S(1)} collective-permute-done((f32[9,48]{1,0:T(8,128)S(1)}, f32[9,48]{1,0:T(8,128)S(1)}, u32[]{:S(2)}, u32[]{:S(2)}) %collective-permute-start.7) | collective-permute-done | bytes 1760 | tf_op jit(solution)/shard_map/ppermute | solution.py:86
  85.7 2.4 %fusion.2 = f32[6,27,384]{2,1,0:T(8,128)S(1)} fusion(s32[6,384]{1,0:T(8,128)} %bitcast.125, bf16[6,9,864]{2,1,0:T(8,128)(2,1)S(1)} %get-tuple-element.19, bf16[6,9,864]{2,1,0:T(8,128)(2,1)S(1)} %get-tuple-element.20, bf16[6,9,864]{2,1,0:T(8,128)(2,1)S(1)} %get-tuple-element.18), kind=kOutput, calls=%fused_computation.7 | convolution fusion | flops 110325888 | bytes 537984 | tf_op jit(solution)/shard_map/fnq,fqe->fne/dot_general | solution.py:136
  90.7 4.5 %collective-permute-start.8 = (f32[23,7,63]{2,1,0:T(8,128)S(1)}, f32[23,7,63]{2,1,0:T(8,128)S(1)}, u32[]{:S(2)}, u32[]{:S(2)}) collective-permute-start(f32[23,7,63]{2,1,0:T(8,128)S(1)} %slice.263), channel_id=1, source_target_pairs={{0,1},{1,0},{2,3},{3,2},{4,5},{5,4},{6,7},{7,6},{8,9},{9,8},{10,11... | collective-permute-start | bytes 121724 | tf_op jit(solution)/shard_map/ppermute | solution.py:205
  95.3 2.8 %collective-permute-done.8 = f32[23,7,63]{2,1,0:T(8,128)S(1)} collective-permute-done((f32[23,7,63]{2,1,0:T(8,128)S(1)}, f32[23,7,63]{2,1,0:T(8,128)S(1)}, u32[]{:S(2)}, u32[]{:S(2)}) %collective-permute-start.8) | collective-permute-done | bytes 40604 | tf_op jit(solution)/shard_map/ppermute | solution.py:205
  98.2 5.3 %collective-permute-start.9 = (f32[23,7,63]{2,1,0:T(8,128)S(1)}, f32[23,7,63]{2,1,0:T(8,128)S(1)}, u32[]{:S(2)}, u32[]{:S(2)}) collective-permute-start(f32[23,7,63]{2,1,0:T(8,128)S(1)} %slice_add_fusion.8), channel_id=1, source_target_pairs={{0,2},{1,3},{2,0},{3,1},{4,6},{5,7},{6,4},{7,5},{8,10},{9,11},{10,... | collective-permute-start | bytes 121724 | tf_op jit(solution)/shard_map/ppermute | solution.py:205
  105.4 6.6 %collective-permute-start.10 = (f32[23,7,63]{2,1,0:T(8,128)S(1)}, f32[23,7,63]{2,1,0:T(8,128)S(1)}, u32[]{:S(2)}, u32[]{:S(2)}) collective-permute-start(f32[23,7,63]{2,1,0:T(8,128)S(1)} %add.251), channel_id=1, source_target_pairs={{0,4},{1,5},{2,6},{3,7},{4,0},{5,1},{6,2},{7,3},{8,12},{9,13},{10,... | collective-permute-start | bytes 121724 | tf_op jit(solution)/shard_map/ppermute | solution.py:205
  114.7 4.5 %collective-permute-start.11 = (f32[23,7,63]{2,1,0:T(8,128)S(1)}, f32[23,7,63]{2,1,0:T(8,128)S(1)}, u32[]{:S(2)}, u32[]{:S(2)}) collective-permute-start(f32[23,7,63]{2,1,0:T(8,128)S(1)} %add.252), channel_id=1, source_target_pairs={{0,8},{1,9},{2,10},{3,11},{4,12},{5,13},{6,14},{7,15},{8,0},{9,1},... | collective-permute-start | bytes 121724 | tf_op jit(solution)/shard_map/ppermute | solution.py:205
  121.2 12.6 %collective-permute-start.12 = (f32[23,7,63]{2,1,0:T(8,128)S(1)}, f32[23,7,63]{2,1,0:T(8,128)S(1)}, u32[]{:S(2)}, u32[]{:S(2)}) collective-permute-start(f32[23,7,63]{2,1,0:T(8,128)S(1)} %add.253), channel_id=1, source_target_pairs={{0,16},{1,17},{2,18},{3,19},{4,20},{5,21},{6,22},{7,23},{8,24},{9,... | collective-permute-start | bytes 121724 | tf_op jit(solution)/shard_map/ppermute | solution.py:205
  133.9 3.9 %collective-permute-done.12 = f32[23,7,63]{2,1,0:T(8,128)S(1)} collective-permute-done((f32[23,7,63]{2,1,0:T(8,128)S(1)}, f32[23,7,63]{2,1,0:T(8,128)S(1)}, u32[]{:S(2)}, u32[]{:S(2)}) %collective-permute-start.12) | collective-permute-done | bytes 40604 | tf_op jit(solution)/shard_map/ppermute | solution.py:205
  143.2 15.5 %collective-permute-start.13 = (f32[9,48]{1,0:T(8,128)S(1)}, f32[9,48]{1,0:T(8,128)S(1)}, u32[]{:S(2)}, u32[]{:S(2)}) collective-permute-start(f32[9,48]{1,0:T(8,128)S(1)} %get-tuple-element.33), channel_id=1, source_target_pairs={{0,32},{32,64},{64,96},{96,128},{128,160},{160,192},{192,224},{224... | collective-permute-start | bytes 5192 | tf_op jit(solution)/shard_map/ppermute | solution.py:86
  158.7 2.1 %collective-permute-start.14 = (f32[9,48]{1,0:T(8,128)S(1)}, f32[9,48]{1,0:T(8,128)S(1)}, u32[]{:S(2)}, u32[]{:S(2)}) collective-permute-start(f32[9,48]{1,0:T(8,128)S(1)} %get-tuple-element.34), channel_id=1, source_target_pairs={{32,0},{64,32},{96,64},{128,96},{160,128},{192,160},{224,192},{256... | collective-permute-start | bytes 5192 | tf_op jit(solution)/shard_map/ppermute | solution.py:86
  161.9 10.4 %collective-permute-done.14 = f32[9,48]{1,0:T(8,128)S(1)} collective-permute-done((f32[9,48]{1,0:T(8,128)S(1)}, f32[9,48]{1,0:T(8,128)S(1)}, u32[]{:S(2)}, u32[]{:S(2)}) %collective-permute-start.14) | collective-permute-done | bytes 1760 | tf_op jit(solution)/shard_map/ppermute | solution.py:86
  177.2 1.9 collective-permute-start.15
  180.8 2.2 %collective-permute-start.17 = (f32[36,48]{1,0:T(8,128)S(1)}, f32[36,48]{1,0:T(8,128)S(1)}, u32[]{:S(2)}, u32[]{:S(2)}) collective-permute-start(f32[36,48]{1,0:T(8,128)S(1)} %get-tuple-element.27), channel_id=1, source_target_pairs={{0,32},{32,64},{64,96},{96,128},{128,160},{160,192},{192,224},{224... | collective-permute-start | bytes 20744 | tf_op jit(solution)/shard_map/ppermute | solution.py:86
  183.0 2.1 %collective-permute-start.18 = (f32[36,48]{1,0:T(8,128)S(1)}, f32[36,48]{1,0:T(8,128)S(1)}, u32[]{:S(2)}, u32[]{:S(2)}) collective-permute-start(f32[36,48]{1,0:T(8,128)S(1)} %get-tuple-element.28), channel_id=1, source_target_pairs={{32,0},{64,32},{96,64},{128,96},{160,128},{192,160},{224,192},{256... | collective-permute-start | bytes 20744 | tf_op jit(solution)/shard_map/ppermute | solution.py:86
  185.9 10.9 %collective-permute-done.18 = f32[36,48]{1,0:T(8,128)S(1)} collective-permute-done((f32[36,48]{1,0:T(8,128)S(1)}, f32[36,48]{1,0:T(8,128)S(1)}, u32[]{:S(2)}, u32[]{:S(2)}) %collective-permute-start.18) | collective-permute-done | bytes 6944 | tf_op jit(solution)/shard_map/ppermute | solution.py:86
  (233 shorter events, 64.3 us)
Async XLA Ops:
  0.0 32.8 %copy-start.30 = (s32[6]{0:T(128)S(1)}, s32[6]{0:T(128)}, u32[]{:S(2)}) copy-start(s32[6]{0:T(128)} %constant.144) | copy-start | bytes 76
  0.0 32.7 %copy-start.29 = (s32[1,480]{1,0:T(1,128)S(1)}, s32[1,480]{1,0:T(1,128)}, u32[]{:S(2)}) copy-start(s32[1,480]{1,0:T(1,128)} %param.40) | copy-start | bytes 5764
  7.0 30.7 %collective-permute-start = (f32[44,192]{1,0:T(8,128)}, f32[44,192]{1,0:T(8,128)S(1)}, u32[]{:S(2)}, u32[]{:S(2)}) collective-permute-start(f32[44,192]{1,0:T(8,128)} %get-tuple-element.23), channel_id=1, source_target_pairs={{0,1},{1,2},{2,3},{3,4},{4,5},{5,6},{6,7},{7,8},{8,9},{9,10},{10,1... | collective-permute-start | bytes 101384 | tf_op jit(solution)/shard_map/ppermute | solution.py:86
  11.0 26.7 %collective-permute-start.1 = (f32[44,192]{1,0:T(8,128)}, f32[44,192]{1,0:T(8,128)}, u32[]{:S(2)}, u32[]{:S(2)}) collective-permute-start(f32[44,192]{1,0:T(8,128)} %get-tuple-element.24), channel_id=1, source_target_pairs={{1,0},{2,1},{3,2},{4,3},{5,4},{6,5},{7,6},{8,7},{9,8},{10,9},{11,1... | collective-permute-start | bytes 101384 | tf_op jit(solution)/shard_map/ppermute | solution.py:86
  12.3 24.0 %copy-start.18 = (f32[27,27]{1,0:T(8,128)S(1)}, f32[27,27]{1,0:T(8,128)}, u32[]{:S(2)}) copy-start(f32[27,27]{1,0:T(8,128)} %param.34) | copy-start | bytes 8752
  13.2 25.3 %collective-permute-start.2 = (f32[36,48]{1,0:T(8,128)}, f32[36,48]{1,0:T(8,128)}, u32[]{:S(2)}, u32[]{:S(2)}) collective-permute-start(f32[36,48]{1,0:T(8,128)} %get-tuple-element.29), channel_id=1, source_target_pairs={{0,32},{32,64},{64,96},{96,128},{128,160},{160,192},{192,224},{224... | collective-permute-start | bytes 20744 | tf_op jit(solution)/shard_map/ppermute | solution.py:86
  29.5 13.9 %collective-permute-start.3 = (f32[36,48]{1,0:T(8,128)S(1)}, f32[36,48]{1,0:T(8,128)}, u32[]{:S(2)}, u32[]{:S(2)}) collective-permute-start(f32[36,48]{1,0:T(8,128)S(1)} %get-tuple-element.30), channel_id=1, source_target_pairs={{32,0},{64,32},{96,64},{128,96},{160,128},{192,160},{224,192},{256... | collective-permute-start | bytes 20744 | tf_op jit(solution)/shard_map/ppermute | solution.py:86
  53.9 31.2 %copy-start.9 = (f32[72,9]{1,0:T(8,128)S(1)}, f32[72,9]{1,0:T(8,128)}, u32[]{:S(2)}) copy-start(f32[72,9]{1,0:T(8,128)} %constant.132.clone) | copy-start | bytes 7780
  57.8 27.3 %collective-permute-start.4 = (f32[9,192]{1,0:T(8,128)S(1)}, f32[9,192]{1,0:T(8,128)S(1)}, u32[]{:S(2)}, u32[]{:S(2)}) collective-permute-start(f32[9,192]{1,0:T(8,128)S(1)} %get-tuple-element.31), channel_id=1, source_target_pairs={{0,1},{1,2},{2,3},{3,4},{4,5},{5,6},{6,7},{7,8},{8,9},{9,10},{10,1... | collective-permute-start | bytes 20744 | tf_op jit(solution)/shard_map/ppermute | solution.py:86
  62.1 23.0 %collective-permute-start.5 = (f32[9,192]{1,0:T(8,128)S(1)}, f32[9,192]{1,0:T(8,128)S(1)}, u32[]{:S(2)}, u32[]{:S(2)}) collective-permute-start(f32[9,192]{1,0:T(8,128)S(1)} %get-tuple-element.32), channel_id=1, source_target_pairs={{1,0},{2,1},{3,2},{4,3},{5,4},{6,5},{7,6},{8,7},{9,8},{10,9},{11,1... | collective-permute-start | bytes 20744 | tf_op jit(solution)/shard_map/ppermute | solution.py:86
  63.7 15.4 %collective-permute-start.6 = (f32[9,48]{1,0:T(8,128)S(1)}, f32[9,48]{1,0:T(8,128)S(1)}, u32[]{:S(2)}, u32[]{:S(2)}) collective-permute-start(f32[9,48]{1,0:T(8,128)S(1)} %get-tuple-element.35), channel_id=1, source_target_pairs={{0,32},{32,64},{64,96},{96,128},{128,160},{160,192},{192,224},{224... | collective-permute-start | bytes 5192 | tf_op jit(solution)/shard_map/ppermute | solution.py:86
  71.5 13.7 %collective-permute-start.7 = (f32[9,48]{1,0:T(8,128)S(1)}, f32[9,48]{1,0:T(8,128)S(1)}, u32[]{:S(2)}, u32[]{:S(2)}) collective-permute-start(f32[9,48]{1,0:T(8,128)S(1)} %get-tuple-element.36), channel_id=1, source_target_pairs={{32,0},{64,32},{96,64},{128,96},{160,128},{192,160},{224,192},{256... | collective-permute-start | bytes 5192 | tf_op jit(solution)/shard_map/ppermute | solution.py:86
  90.7 7.4 %collective-permute-start.8 = (f32[23,7,63]{2,1,0:T(8,128)S(1)}, f32[23,7,63]{2,1,0:T(8,128)S(1)}, u32[]{:S(2)}, u32[]{:S(2)}) collective-permute-start(f32[23,7,63]{2,1,0:T(8,128)S(1)} %slice.263), channel_id=1, source_target_pairs={{0,1},{1,0},{2,3},{3,2},{4,5},{5,4},{6,7},{7,6},{8,9},{9,8},{10,11... | collective-permute-start | bytes 121724 | tf_op jit(solution)/shard_map/ppermute | solution.py:205
  98.2 7.2 %collective-permute-start.9 = (f32[23,7,63]{2,1,0:T(8,128)S(1)}, f32[23,7,63]{2,1,0:T(8,128)S(1)}, u32[]{:S(2)}, u32[]{:S(2)}) collective-permute-start(f32[23,7,63]{2,1,0:T(8,128)S(1)} %slice_add_fusion.8), channel_id=1, source_target_pairs={{0,2},{1,3},{2,0},{3,1},{4,6},{5,7},{6,4},{7,5},{8,10},{9,11},{10,... | collective-permute-start | bytes 121724 | tf_op jit(solution)/shard_map/ppermute | solution.py:205
  105.4 9.3 %collective-permute-start.10 = (f32[23,7,63]{2,1,0:T(8,128)S(1)}, f32[23,7,63]{2,1,0:T(8,128)S(1)}, u32[]{:S(2)}, u32[]{:S(2)}) collective-permute-start(f32[23,7,63]{2,1,0:T(8,128)S(1)} %add.251), channel_id=1, source_target_pairs={{0,4},{1,5},{2,6},{3,7},{4,0},{5,1},{6,2},{7,3},{8,12},{9,13},{10,... | collective-permute-start | bytes 121724 | tf_op jit(solution)/shard_map/ppermute | solution.py:205
  114.7 6.5 %collective-permute-start.11 = (f32[23,7,63]{2,1,0:T(8,128)S(1)}, f32[23,7,63]{2,1,0:T(8,128)S(1)}, u32[]{:S(2)}, u32[]{:S(2)}) collective-permute-start(f32[23,7,63]{2,1,0:T(8,128)S(1)} %add.252), channel_id=1, source_target_pairs={{0,8},{1,9},{2,10},{3,11},{4,12},{5,13},{6,14},{7,15},{8,0},{9,1},... | collective-permute-start | bytes 121724 | tf_op jit(solution)/shard_map/ppermute | solution.py:205
  121.2 16.5 %collective-permute-start.12 = (f32[23,7,63]{2,1,0:T(8,128)S(1)}, f32[23,7,63]{2,1,0:T(8,128)S(1)}, u32[]{:S(2)}, u32[]{:S(2)}) collective-permute-start(f32[23,7,63]{2,1,0:T(8,128)S(1)} %add.253), channel_id=1, source_target_pairs={{0,16},{1,17},{2,18},{3,19},{4,20},{5,21},{6,22},{7,23},{8,24},{9,... | collective-permute-start | bytes 121724 | tf_op jit(solution)/shard_map/ppermute | solution.py:205
  140.9 32.0 %copy-start.32 = (s32[384,6]{0,1:T(8,128)S(1)}, s32[384,6]{0,1:T(8,128)}, u32[]{:S(2)}) copy-start(s32[384,6]{0,1:T(8,128)} %param.37) | copy-start | bytes 27652
  143.2 18.7 %collective-permute-start.13 = (f32[9,48]{1,0:T(8,128)S(1)}, f32[9,48]{1,0:T(8,128)S(1)}, u32[]{:S(2)}, u32[]{:S(2)}) collective-permute-start(f32[9,48]{1,0:T(8,128)S(1)} %get-tuple-element.33), channel_id=1, source_target_pairs={{0,32},{32,64},{64,96},{96,128},{128,160},{160,192},{192,224},{224... | collective-permute-start | bytes 5192 | tf_op jit(solution)/shard_map/ppermute | solution.py:86
  158.7 13.7 %collective-permute-start.14 = (f32[9,48]{1,0:T(8,128)S(1)}, f32[9,48]{1,0:T(8,128)S(1)}, u32[]{:S(2)}, u32[]{:S(2)}) collective-permute-start(f32[9,48]{1,0:T(8,128)S(1)} %get-tuple-element.34), channel_id=1, source_target_pairs={{32,0},{64,32},{96,64},{128,96},{160,128},{192,160},{224,192},{256... | collective-permute-start | bytes 5192 | tf_op jit(solution)/shard_map/ppermute | solution.py:86
  177.2 19.6 %collective-permute-start.15 = (f32[36,192]{1,0:T(8,128)S(1)}, f32[36,192]{1,0:T(8,128)S(1)}, u32[]{:S(2)}, u32[]{:S(2)}) collective-permute-start(f32[36,192]{1,0:T(8,128)S(1)} %get-tuple-element.25), channel_id=1, source_target_pairs={{0,1},{1,2},{2,3},{3,4},{4,5},{5,6},{6,7},{7,8},{8,9},{9,10},{10,1... | collective-permute-start | bytes 82952 | tf_op jit(solution)/shard_map/ppermute | solution.py:86
  179.1 17.7 %collective-permute-start.16 = (f32[36,192]{1,0:T(8,128)S(1)}, f32[36,192]{1,0:T(8,128)S(1)}, u32[]{:S(2)}, u32[]{:S(2)}) collective-permute-start(f32[36,192]{1,0:T(8,128)S(1)} %get-tuple-element.26), channel_id=1, source_target_pairs={{1,0},{2,1},{3,2},{4,3},{5,4},{6,5},{7,6},{8,7},{9,8},{10,9},{11,1... | collective-permute-start | bytes 82952 | tf_op jit(solution)/shard_map/ppermute | solution.py:86
  180.8 5.1 %collective-permute-start.17 = (f32[36,48]{1,0:T(8,128)S(1)}, f32[36,48]{1,0:T(8,128)S(1)}, u32[]{:S(2)}, u32[]{:S(2)}) collective-permute-start(f32[36,48]{1,0:T(8,128)S(1)} %get-tuple-element.27), channel_id=1, source_target_pairs={{0,32},{32,64},{64,96},{96,128},{128,160},{160,192},{192,224},{224... | collective-permute-start | bytes 20744 | tf_op jit(solution)/shard_map/ppermute | solution.py:86
  183.0 13.8 %collective-permute-start.18 = (f32[36,48]{1,0:T(8,128)S(1)}, f32[36,48]{1,0:T(8,128)S(1)}, u32[]{:S(2)}, u32[]{:S(2)}) collective-permute-start(f32[36,48]{1,0:T(8,128)S(1)} %get-tuple-element.28), channel_id=1, source_target_pairs={{32,0},{64,32},{96,64},{128,96},{160,128},{192,160},{224,192},{256... | collective-permute-start | bytes 20744 | tf_op jit(solution)/shard_map/ppermute | solution.py:86
  (31 other events, 197.2 us)

commit v5 on v3

--- a/solution.py
+++ b/solution.py
@@ -86,6 +86,22 @@
     return lax.ppermute(block, axis, pairs)
 
 
+def region_exchange(region_out):
+    count = lax.axis_size("region")
+    odd = (lax.axis_index("region") % 2) == 1
+    far_pairs = [(i, i + 1) for i in range(1, count - 1, 2)]
+    far_pairs += [(i, i - 1) for i in range(2, count, 2)]
+    near_pairs = [(i, i + 1) for i in range(0, count - 1, 2)]
+    near_pairs += [(i + 1, i) for i in range(0, count - 1, 2)]
+    far_recv = lax.ppermute(
+        jnp.where(odd, region_out[1], region_out[0]), "region", far_pairs
+    )
+    near_recv = lax.ppermute(
+        jnp.where(odd, region_out[0], region_out[1]), "region", near_pairs
+    )
+    return jnp.where(odd, near_recv, far_recv), jnp.where(odd, far_recv, near_recv)
+
+
 def apply_level(current, stiffness, points, tables, extra=None, group_ghosts=None):
     gather, pick_group, pick_region, codes = tables
     plane = points * points
@@ -99,8 +115,7 @@
         "snj,sjk->snk", traces[2:4], pick_region, precision=HIGHEST,
         preferred_element_type=jnp.float32,
     )
-    from_region_low = shift(region_out[1], "region", 1)
-    from_region_high = shift(region_out[0], "region", -1)
+    from_region_low, from_region_high = region_exchange(region_out)
     received = None
     if group_ghosts is None:
         group_out = jnp.einsum(

time: 190 us -> 175 us (0.921); the launches traced: 189 us -> 172 us
  waiting for transfers between devices: 51.1 us -> 20.3 us
  starting transfers between devices: 89.9 us -> 103 us
    ppermute x0 -> x8, starting transfers between devices: none -> 65.4 us  [the longest x4 43.6 us: region_exchange(): lax.ppermute(jnp.where(odd, region_out[1], region_out[0]), 'region', far_...]
    ppermute x14 -> x6, starting transfers between devices: 55.9 us -> 13.7 us  [shift(): return lax.ppermute(block, axis, pairs)]
    ppermute x14 -> x6, waiting for transfers between devices: 40 us -> 4.41 us  [shift(): return lax.ppermute(block, axis, pairs)]
    ppermute x5, starting transfers between devices: 34 us -> 24.1 us  [gather_slab(): interior = interior + lax.ppermute(interior, 'group', partner)]
    ppermute x5, waiting for transfers between devices: 11.1 us -> 15.2 us  [gather_slab(): interior = interior + lax.ppermute(interior, 'group', partner)]
    unnamed x67 -> x69, local copies, waits for them, and re-layouts: 4.79 us -> 5.74 us
  transfers between devices with their start and end apart: 19 -> 19, of which waited for: 9 -> 9; matrix products, arithmetic and copies ran while one was open for 5% -> 6% of each run, Pallas kernels for 0% -> 0%
where the time goes in v5:
time: 175 us; the launch traced here: 172 us
  starting transfers between devices  103 us (59%)
  matrix products  31.3 us (18%)
  waiting for transfers between devices  20.3 us (12%)
  local copies, waits for them, and re-layouts  13 us (7%)
  other arithmetic  2.59 us (1%)
    ppermute x4, starting transfers between devices, region_exchange(): lax.ppermute(jnp.where(odd, region_out[1], region_out[0]), 'region', far_...  43.6 us
    ppermute x5, starting transfers between devices, gather_slab(): interior = interior + lax.ppermute(interior, 'group', partner)  24.1 us
    ppermute x4, starting transfers between devices, region_exchange(): lax.ppermute(jnp.where(odd, region_out[0], region_out[1]), 'region', near...  21.8 us
    ppermute x5, waiting for transfers between devices, gather_slab(): interior = interior + lax.ppermute(interior, 'group', partner)  15.2 us
    dot_general x26, matrix products, mm(): return jnp.dot(a, b, precision=HIGHEST, preferred_element_type=jnp.float32)  14.7 us
    ppermute x6, starting transfers between devices, shift(): return lax.ppermute(block, axis, pairs)  13.7 us
    dot_general x4, matrix products, apply_level(): jnp.einsum('fnq,fqe->fne', source, gather.astype(jnp.float32), precision=...  11 us
    unnamed x69, local copies, waits for them, and re-layouts  5.74 us
  transfers between devices with their start and end apart: 19, of which 9 were waited for; matrix products, arithmetic and copies ran while one was open for 6% of the time, Pallas kernels for 0%

profile of v5, /device:TPU:1, one launch (start us, length us, event | category | flops | bytes accessed | tf_op | source)
XLA Modules:
  0.0 171.8 jit_solution(4100118348771248002)
XLA Ops:
  4.3 16.1 %collective-permute-start.2 = (f32[36,48]{1,0:T(8,128)S(1)}, f32[36,48]{1,0:T(8,128)S(1)}, u32[]{:S(2)}, u32[]{:S(2)}) collective-permute-start(f32[36,48]{1,0:T(8,128)S(1)} %get-tuple-element.21), channel_id=1, source_target_pairs={{0,32},{64,96},{128,160},{192,224},{256,288},{320,352},{384,416},{... | collective-permute-start | bytes 20744 | tf_op jit(solution)/shard_map/ppermute | solution.py:99
  20.4 2.7 %collective-permute-start.3 = (f32[36,48]{1,0:T(8,128)S(1)}, f32[36,48]{1,0:T(8,128)S(1)}, u32[]{:S(2)}, u32[]{:S(2)}) collective-permute-start(f32[36,48]{1,0:T(8,128)S(1)} %get-tuple-element.22), channel_id=1, source_target_pairs={{32,64},{96,128},{160,192},{224,256},{288,320},{352,384},{416,448}... | collective-permute-start | bytes 20744 | tf_op jit(solution)/shard_map/ppermute | solution.py:96
  24.3 3.2 %collective-permute-start = (f32[44,192]{1,0:T(8,128)S(1)}, f32[44,192]{1,0:T(8,128)S(1)}, u32[]{:S(2)}, u32[]{:S(2)}) collective-permute-start(f32[44,192]{1,0:T(8,128)S(1)} %get-tuple-element.11), channel_id=1, source_target_pairs={{0,1},{1,2},{2,3},{3,4},{4,5},{5,6},{6,7},{7,8},{8,9},{9,10},{10,1... | collective-permute-start | bytes 101384 | tf_op jit(solution)/shard_map/ppermute | solution.py:86
  36.1 2.8 %fusion.12 = f32[6,36,384]{2,1,0:T(8,128)S(1)} fusion(f32[6,36,384]{2,1,0:T(8,128)S(1)} %reshape.335, s32[6,384]{1,0:T(8,128)S(1)} %bitcast.129, f32[6,36,480]{2,1,0:T(8,128)S(1)} %broadcast_in_dim.19, f32[6,36,384]{2,1,0:T(8,128)S(1)} %copy-done.8), kind=kOutput, calls=%fused_computation.21 | convolution fusion | flops 862223616 | bytes 1419264 | tf_op jit(solution)/shard_map/fnq,fqe->fne/dot_general | solution.py:140
  42.0 1.9 %collective-permute-start.6 = (f32[9,48]{1,0:T(8,128)S(1)}, f32[9,48]{1,0:T(8,128)S(1)}, u32[]{:S(2)}, u32[]{:S(2)}) collective-permute-start(f32[9,48]{1,0:T(8,128)S(1)} %get-tuple-element.31), channel_id=1, source_target_pairs={{0,32},{64,96},{128,160},{192,224},{256,288},{320,352},{384,416},{... | collective-permute-start | bytes 5192 | tf_op jit(solution)/shard_map/ppermute | solution.py:99
  43.9 15.2 %collective-permute-start.7 = (f32[9,48]{1,0:T(8,128)S(1)}, f32[9,48]{1,0:T(8,128)S(1)}, u32[]{:S(2)}, u32[]{:S(2)}) collective-permute-start(f32[9,48]{1,0:T(8,128)S(1)} %get-tuple-element.32), channel_id=1, source_target_pairs={{32,64},{96,128},{160,192},{224,256},{288,320},{352,384},{416,448}... | collective-permute-start | bytes 5192 | tf_op jit(solution)/shard_map/ppermute | solution.py:96
  59.7 4.0 %collective-permute-start.4 = (f32[9,192]{1,0:T(8,128)S(1)}, f32[9,192]{1,0:T(8,128)S(1)}, u32[]{:S(2)}, u32[]{:S(2)}) collective-permute-start(f32[9,192]{1,0:T(8,128)S(1)} %get-tuple-element.23), channel_id=1, source_target_pairs={{0,1},{1,2},{2,3},{3,4},{4,5},{5,6},{6,7},{7,8},{8,9},{9,10},{10,1... | collective-permute-start | bytes 20744 | tf_op jit(solution)/shard_map/ppermute | solution.py:86
  65.8 2.4 %collective-permute-done.5 = f32[9,192]{1,0:T(8,128)S(1)} collective-permute-done((f32[9,192]{1,0:T(8,128)S(1)}, f32[9,192]{1,0:T(8,128)S(1)}, u32[]{:S(2)}, u32[]{:S(2)}) %collective-permute-start.5) | collective-permute-done | bytes 6944 | tf_op jit(solution)/shard_map/ppermute | solution.py:86
  68.7 2.7 %fusion.18 = f32[6,9,384]{2,1,0:T(8,128)S(1)} fusion(f32[6,9,384]{2,1,0:T(8,128)S(1)} %reshape.339, s32[6,384]{1,0:T(8,128)S(1)} %bitcast.130, f32[6,9,480]{2,1,0:T(8,128)S(1)} %broadcast_in_dim.22, f32[6,9,384]{2,1,0:T(8,128)S(1)} %gather_fusion.1), kind=kOutput, calls=%fused_computation.31 | convolution fusion | flops 217048896 | bytes 361728 | tf_op jit(solution)/shard_map/fnq,fqe->fne/dot_general | solution.py:140
  73.9 3.4 %collective-permute-start.8 = (f32[23,7,63]{2,1,0:T(8,128)S(1)}, f32[23,7,63]{2,1,0:T(8,128)S(1)}, u32[]{:S(2)}, u32[]{:S(2)}) collective-permute-start(f32[23,7,63]{2,1,0:T(8,128)S(1)} %slice.217), channel_id=1, source_target_pairs={{0,1},{1,0},{2,3},{3,2},{4,5},{5,4},{6,7},{7,6},{8,9},{9,8},{10,11... | collective-permute-start | bytes 121724 | tf_op jit(solution)/shard_map/ppermute | solution.py:212
  77.3 2.9 %collective-permute-done.8 = f32[23,7,63]{2,1,0:T(8,128)S(1)} collective-permute-done((f32[23,7,63]{2,1,0:T(8,128)S(1)}, f32[23,7,63]{2,1,0:T(8,128)S(1)}, u32[]{:S(2)}, u32[]{:S(2)}) %collective-permute-start.8) | collective-permute-done | bytes 40604 | tf_op jit(solution)/shard_map/ppermute | solution.py:212
  80.4 6.9 %collective-permute-start.9 = (f32[23,7,63]{2,1,0:T(8,128)S(1)}, f32[23,7,63]{2,1,0:T(8,128)S(1)}, u32[]{:S(2)}, u32[]{:S(2)}) collective-permute-start(f32[23,7,63]{2,1,0:T(8,128)S(1)} %slice_add_fusion), channel_id=1, source_target_pairs={{0,2},{1,3},{2,0},{3,1},{4,6},{5,7},{6,4},{7,5},{8,10},{9,11},{10,... | collective-permute-start | bytes 121724 | tf_op jit(solution)/shard_map/ppermute | solution.py:212
  87.2 1.9 %collective-permute-done.9 = f32[23,7,63]{2,1,0:T(8,128)S(1)} collective-permute-done((f32[23,7,63]{2,1,0:T(8,128)S(1)}, f32[23,7,63]{2,1,0:T(8,128)S(1)}, u32[]{:S(2)}, u32[]{:S(2)}) %collective-permute-start.9) | collective-permute-done | bytes 40604 | tf_op jit(solution)/shard_map/ppermute | solution.py:212
  89.2 2.7 %collective-permute-start.10 = (f32[23,7,63]{2,1,0:T(8,128)S(1)}, f32[23,7,63]{2,1,0:T(8,128)S(1)}, u32[]{:S(2)}, u32[]{:S(2)}) collective-permute-start(f32[23,7,63]{2,1,0:T(8,128)S(1)} %add.221), channel_id=1, source_target_pairs={{0,4},{1,5},{2,6},{3,7},{4,0},{5,1},{6,2},{7,3},{8,12},{9,13},{10,... | collective-permute-start | bytes 121724 | tf_op jit(solution)/shard_map/ppermute | solution.py:212
  94.5 6.0 %collective-permute-start.11 = (f32[23,7,63]{2,1,0:T(8,128)S(1)}, f32[23,7,63]{2,1,0:T(8,128)S(1)}, u32[]{:S(2)}, u32[]{:S(2)}) collective-permute-start(f32[23,7,63]{2,1,0:T(8,128)S(1)} %add.222), channel_id=1, source_target_pairs={{0,8},{1,9},{2,10},{3,11},{4,12},{5,13},{6,14},{7,15},{8,0},{9,1},... | collective-permute-start | bytes 121724 | tf_op jit(solution)/shard_map/ppermute | solution.py:212
  100.6 2.9 %collective-permute-done.11 = f32[23,7,63]{2,1,0:T(8,128)S(1)} collective-permute-done((f32[23,7,63]{2,1,0:T(8,128)S(1)}, f32[23,7,63]{2,1,0:T(8,128)S(1)}, u32[]{:S(2)}, u32[]{:S(2)}) %collective-permute-start.11) | collective-permute-done | bytes 40604 | tf_op jit(solution)/shard_map/ppermute | solution.py:212
  103.5 5.1 %collective-permute-start.12 = (f32[23,7,63]{2,1,0:T(8,128)S(1)}, f32[23,7,63]{2,1,0:T(8,128)S(1)}, u32[]{:S(2)}, u32[]{:S(2)}) collective-permute-start(f32[23,7,63]{2,1,0:T(8,128)S(1)} %add.223), channel_id=1, source_target_pairs={{0,16},{1,17},{2,18},{3,19},{4,20},{5,21},{6,22},{7,23},{8,24},{9,... | collective-permute-start | bytes 121724 | tf_op jit(solution)/shard_map/ppermute | solution.py:212
  108.7 6.3 %collective-permute-done.12 = f32[23,7,63]{2,1,0:T(8,128)S(1)} collective-permute-done((f32[23,7,63]{2,1,0:T(8,128)S(1)}, f32[23,7,63]{2,1,0:T(8,128)S(1)}, u32[]{:S(2)}, u32[]{:S(2)}) %collective-permute-start.12) | collective-permute-done | bytes 40604 | tf_op jit(solution)/shard_map/ppermute | solution.py:212
  123.2 12.8 %collective-permute-start.14 = (f32[9,48]{1,0:T(8,128)S(1)}, f32[9,48]{1,0:T(8,128)S(1)}, u32[]{:S(2)}, u32[]{:S(2)}) collective-permute-start(f32[9,48]{1,0:T(8,128)S(1)} %get-tuple-element.28), channel_id=1, source_target_pairs={{32,64},{96,128},{160,192},{224,256},{288,320},{352,384},{416,448}... | collective-permute-start | bytes 5192 | tf_op jit(solution)/shard_map/ppermute | solution.py:96
  137.5 2.7 %fusion.19 = f32[6,9,384]{2,1,0:T(8,128)S(1)} fusion(f32[6,9,384]{2,1,0:T(8,128)S(1)} %reshape.345, s32[6,384]{1,0:T(8,128)S(1)} %bitcast.131, f32[6,9,480]{2,1,0:T(8,128)S(1)} %broadcast_in_dim.24, f32[6,9,384]{2,1,0:T(8,128)S(1)} %gather_fusion.2), kind=kOutput, calls=%fused_computation.32 | convolution fusion | flops 217048896 | bytes 361728 | tf_op jit(solution)/shard_map/fnq,fqe->fne/dot_general | solution.py:140
  144.3 12.8 %collective-permute-start.18 = (f32[36,48]{1,0:T(8,128)S(1)}, f32[36,48]{1,0:T(8,128)S(1)}, u32[]{:S(2)}, u32[]{:S(2)}) collective-permute-start(f32[36,48]{1,0:T(8,128)S(1)} %get-tuple-element.18), channel_id=1, source_target_pairs={{32,64},{96,128},{160,192},{224,256},{288,320},{352,384},{416,448}... | collective-permute-start | bytes 20744 | tf_op jit(solution)/shard_map/ppermute | solution.py:96
  157.8 2.4 %collective-permute-start.15 = (f32[36,192]{1,0:T(8,128)S(1)}, f32[36,192]{1,0:T(8,128)S(1)}, u32[]{:S(2)}, u32[]{:S(2)}) collective-permute-start(f32[36,192]{1,0:T(8,128)S(1)} %get-tuple-element.13), channel_id=1, source_target_pairs={{0,1},{1,2},{2,3},{3,4},{4,5},{5,6},{6,7},{7,8},{8,9},{9,10},{10,1... | collective-permute-start | bytes 82952 | tf_op jit(solution)/shard_map/ppermute | solution.py:86
  163.0 2.0 %collective-permute-done.16 = f32[36,192]{1,0:T(8,128)S(1)} collective-permute-done((f32[36,192]{1,0:T(8,128)S(1)}, f32[36,192]{1,0:T(8,128)S(1)}, u32[]{:S(2)}, u32[]{:S(2)}) %collective-permute-start.16) | collective-permute-done | bytes 27680 | tf_op jit(solution)/shard_map/ppermute | solution.py:86
  166.9 2.8 %fusion.13 = f32[6,36,384]{2,1,0:T(8,128)S(1)} fusion(f32[6,36,384]{2,1,0:T(8,128)S(1)} %copy-done.4, s32[6,384]{1,0:T(8,128)S(1)} %bitcast.132, f32[6,36,480]{2,1,0:T(8,128)S(1)} %broadcast_in_dim.26, f32[6,36,384]{2,1,0:T(8,128)S(1)} %copy-done.9), kind=kOutput, calls=%fused_computation.22 | convolution fusion | flops 862223616 | bytes 1419264 | tf_op jit(solution)/shard_map/fnq,fqe->fne/dot_general | solution.py:140
  (210 shorter events, 45.7 us)
Async XLA Ops:
  3.4 25.5 %copy-start.27 = (s32[1,480]{1,0:T(1,128)S(1)}, s32[1,480]{1,0:T(1,128)}, u32[]{:S(2)}) copy-start(s32[1,480]{1,0:T(1,128)} %param.40) | copy-start | bytes 5764
  3.4 25.5 %copy-start.28 = (s32[6]{0:T(128)S(1)}, s32[6]{0:T(128)}, u32[]{:S(2)}) copy-start(s32[6]{0:T(128)} %constant.162) | copy-start | bytes 76
  4.3 29.3 %collective-permute-start.2 = (f32[36,48]{1,0:T(8,128)S(1)}, f32[36,48]{1,0:T(8,128)S(1)}, u32[]{:S(2)}, u32[]{:S(2)}) collective-permute-start(f32[36,48]{1,0:T(8,128)S(1)} %get-tuple-element.21), channel_id=1, source_target_pairs={{0,32},{64,96},{128,160},{192,224},{256,288},{320,352},{384,416},{... | collective-permute-start | bytes 20744 | tf_op jit(solution)/shard_map/ppermute | solution.py:99
  20.4 13.8 %collective-permute-start.3 = (f32[36,48]{1,0:T(8,128)S(1)}, f32[36,48]{1,0:T(8,128)S(1)}, u32[]{:S(2)}, u32[]{:S(2)}) collective-permute-start(f32[36,48]{1,0:T(8,128)S(1)} %get-tuple-element.22), channel_id=1, source_target_pairs={{32,64},{96,128},{160,192},{224,256},{288,320},{352,384},{416,448}... | collective-permute-start | bytes 20744 | tf_op jit(solution)/shard_map/ppermute | solution.py:96
  24.3 10.0 %collective-permute-start = (f32[44,192]{1,0:T(8,128)S(1)}, f32[44,192]{1,0:T(8,128)S(1)}, u32[]{:S(2)}, u32[]{:S(2)}) collective-permute-start(f32[44,192]{1,0:T(8,128)S(1)} %get-tuple-element.11), channel_id=1, source_target_pairs={{0,1},{1,2},{2,3},{3,4},{4,5},{5,6},{6,7},{7,8},{8,9},{9,10},{10,1... | collective-permute-start | bytes 101384 | tf_op jit(solution)/shard_map/ppermute | solution.py:86
  27.5 6.8 %collective-permute-start.1 = (f32[44,192]{1,0:T(8,128)S(1)}, f32[44,192]{1,0:T(8,128)S(1)}, u32[]{:S(2)}, u32[]{:S(2)}) collective-permute-start(f32[44,192]{1,0:T(8,128)S(1)} %get-tuple-element.12), channel_id=1, source_target_pairs={{1,0},{2,1},{3,2},{4,3},{5,4},{6,5},{7,6},{8,7},{9,8},{10,9},{11,1... | collective-permute-start | bytes 101384 | tf_op jit(solution)/shard_map/ppermute | solution.py:86
  41.7 26.5 %copy-start.11 = (f32[72,9]{1,0:T(8,128)S(1)}, f32[72,9]{1,0:T(8,128)}, u32[]{:S(2)}) copy-start(f32[72,9]{1,0:T(8,128)} %constant.150.clone) | copy-start | bytes 7780
  42.0 23.8 %collective-permute-start.6 = (f32[9,48]{1,0:T(8,128)S(1)}, f32[9,48]{1,0:T(8,128)S(1)}, u32[]{:S(2)}, u32[]{:S(2)}) collective-permute-start(f32[9,48]{1,0:T(8,128)S(1)} %get-tuple-element.31), channel_id=1, source_target_pairs={{0,32},{64,96},{128,160},{192,224},{256,288},{320,352},{384,416},{... | collective-permute-start | bytes 5192 | tf_op jit(solution)/shard_map/ppermute | solution.py:99
  43.9 21.9 %collective-permute-start.7 = (f32[9,48]{1,0:T(8,128)S(1)}, f32[9,48]{1,0:T(8,128)S(1)}, u32[]{:S(2)}, u32[]{:S(2)}) collective-permute-start(f32[9,48]{1,0:T(8,128)S(1)} %get-tuple-element.32), channel_id=1, source_target_pairs={{32,64},{96,128},{160,192},{224,256},{288,320},{352,384},{416,448}... | collective-permute-start | bytes 5192 | tf_op jit(solution)/shard_map/ppermute | solution.py:96
  59.7 6.1 %collective-permute-start.4 = (f32[9,192]{1,0:T(8,128)S(1)}, f32[9,192]{1,0:T(8,128)S(1)}, u32[]{:S(2)}, u32[]{:S(2)}) collective-permute-start(f32[9,192]{1,0:T(8,128)S(1)} %get-tuple-element.23), channel_id=1, source_target_pairs={{0,1},{1,2},{2,3},{3,4},{4,5},{5,6},{6,7},{7,8},{8,9},{9,10},{10,1... | collective-permute-start | bytes 20744 | tf_op jit(solution)/shard_map/ppermute | solution.py:86
  63.7 4.5 %collective-permute-start.5 = (f32[9,192]{1,0:T(8,128)S(1)}, f32[9,192]{1,0:T(8,128)S(1)}, u32[]{:S(2)}, u32[]{:S(2)}) collective-permute-start(f32[9,192]{1,0:T(8,128)S(1)} %get-tuple-element.24), channel_id=1, source_target_pairs={{1,0},{2,1},{3,2},{4,3},{5,4},{6,5},{7,6},{8,7},{9,8},{10,9},{11,1... | collective-permute-start | bytes 20744 | tf_op jit(solution)/shard_map/ppermute | solution.py:86
  73.9 6.4 %collective-permute-start.8 = (f32[23,7,63]{2,1,0:T(8,128)S(1)}, f32[23,7,63]{2,1,0:T(8,128)S(1)}, u32[]{:S(2)}, u32[]{:S(2)}) collective-permute-start(f32[23,7,63]{2,1,0:T(8,128)S(1)} %slice.217), channel_id=1, source_target_pairs={{0,1},{1,0},{2,3},{3,2},{4,5},{5,4},{6,7},{7,6},{8,9},{9,8},{10,11... | collective-permute-start | bytes 121724 | tf_op jit(solution)/shard_map/ppermute | solution.py:212
  80.4 8.8 %collective-permute-start.9 = (f32[23,7,63]{2,1,0:T(8,128)S(1)}, f32[23,7,63]{2,1,0:T(8,128)S(1)}, u32[]{:S(2)}, u32[]{:S(2)}) collective-permute-start(f32[23,7,63]{2,1,0:T(8,128)S(1)} %slice_add_fusion), channel_id=1, source_target_pairs={{0,2},{1,3},{2,0},{3,1},{4,6},{5,7},{6,4},{7,5},{8,10},{9,11},{10,... | collective-permute-start | bytes 121724 | tf_op jit(solution)/shard_map/ppermute | solution.py:212
  89.2 5.3 %collective-permute-start.10 = (f32[23,7,63]{2,1,0:T(8,128)S(1)}, f32[23,7,63]{2,1,0:T(8,128)S(1)}, u32[]{:S(2)}, u32[]{:S(2)}) collective-permute-start(f32[23,7,63]{2,1,0:T(8,128)S(1)} %add.221), channel_id=1, source_target_pairs={{0,4},{1,5},{2,6},{3,7},{4,0},{5,1},{6,2},{7,3},{8,12},{9,13},{10,... | collective-permute-start | bytes 121724 | tf_op jit(solution)/shard_map/ppermute | solution.py:212
  92.6 23.2 %copy-start.32 = (f32[63]{0:T(128)S(1)}, f32[63]{0:T(128)}, u32[]{:S(2)}) copy-start(f32[63]{0:T(128)} %get-tuple-element.43) | copy-start | bytes 760
  92.6 23.2 %copy-start.33 = (f32[63]{0:T(128)S(1)}, f32[63]{0:T(128)}, u32[]{:S(2)}) copy-start(f32[63]{0:T(128)} %get-tuple-element.44) | copy-start | bytes 760
  94.5 8.9 %collective-permute-start.11 = (f32[23,7,63]{2,1,0:T(8,128)S(1)}, f32[23,7,63]{2,1,0:T(8,128)S(1)}, u32[]{:S(2)}, u32[]{:S(2)}) collective-permute-start(f32[23,7,63]{2,1,0:T(8,128)S(1)} %add.222), channel_id=1, source_target_pairs={{0,8},{1,9},{2,10},{3,11},{4,12},{5,13},{6,14},{7,15},{8,0},{9,1},... | collective-permute-start | bytes 121724 | tf_op jit(solution)/shard_map/ppermute | solution.py:212
  103.5 11.5 %collective-permute-start.12 = (f32[23,7,63]{2,1,0:T(8,128)S(1)}, f32[23,7,63]{2,1,0:T(8,128)S(1)}, u32[]{:S(2)}, u32[]{:S(2)}) collective-permute-start(f32[23,7,63]{2,1,0:T(8,128)S(1)} %add.223), channel_id=1, source_target_pairs={{0,16},{1,17},{2,18},{3,19},{4,20},{5,21},{6,22},{7,23},{8,24},{9,... | collective-permute-start | bytes 121724 | tf_op jit(solution)/shard_map/ppermute | solution.py:212
  121.3 15.7 %collective-permute-start.13 = (f32[9,48]{1,0:T(8,128)S(1)}, f32[9,48]{1,0:T(8,128)S(1)}, u32[]{:S(2)}, u32[]{:S(2)}) collective-permute-start(f32[9,48]{1,0:T(8,128)S(1)} %get-tuple-element.27), channel_id=1, source_target_pairs={{0,32},{64,96},{128,160},{192,224},{256,288},{320,352},{384,416},{... | collective-permute-start | bytes 5192 | tf_op jit(solution)/shard_map/ppermute | solution.py:99
  123.2 13.9 %collective-permute-start.14 = (f32[9,48]{1,0:T(8,128)S(1)}, f32[9,48]{1,0:T(8,128)S(1)}, u32[]{:S(2)}, u32[]{:S(2)}) collective-permute-start(f32[9,48]{1,0:T(8,128)S(1)} %get-tuple-element.28), channel_id=1, source_target_pairs={{32,64},{96,128},{160,192},{224,256},{288,320},{352,384},{416,448}... | collective-permute-start | bytes 5192 | tf_op jit(solution)/shard_map/ppermute | solution.py:96
  142.4 20.6 %collective-permute-start.17 = (f32[36,48]{1,0:T(8,128)S(1)}, f32[36,48]{1,0:T(8,128)S(1)}, u32[]{:S(2)}, u32[]{:S(2)}) collective-permute-start(f32[36,48]{1,0:T(8,128)S(1)} %get-tuple-element.17), channel_id=1, source_target_pairs={{0,32},{64,96},{128,160},{192,224},{256,288},{320,352},{384,416},{... | collective-permute-start | bytes 20744 | tf_op jit(solution)/shard_map/ppermute | solution.py:99
  144.3 18.7 %collective-permute-start.18 = (f32[36,48]{1,0:T(8,128)S(1)}, f32[36,48]{1,0:T(8,128)S(1)}, u32[]{:S(2)}, u32[]{:S(2)}) collective-permute-start(f32[36,48]{1,0:T(8,128)S(1)} %get-tuple-element.18), channel_id=1, source_target_pairs={{32,64},{96,128},{160,192},{224,256},{288,320},{352,384},{416,448}... | collective-permute-start | bytes 20744 | tf_op jit(solution)/shard_map/ppermute | solution.py:96
  157.8 5.2 %collective-permute-start.15 = (f32[36,192]{1,0:T(8,128)S(1)}, f32[36,192]{1,0:T(8,128)S(1)}, u32[]{:S(2)}, u32[]{:S(2)}) collective-permute-start(f32[36,192]{1,0:T(8,128)S(1)} %get-tuple-element.13), channel_id=1, source_target_pairs={{0,1},{1,2},{2,3},{3,4},{4,5},{5,6},{6,7},{7,8},{8,9},{9,10},{10,1... | collective-permute-start | bytes 82952 | tf_op jit(solution)/shard_map/ppermute | solution.py:86
  160.3 4.7 %collective-permute-start.16 = (f32[36,192]{1,0:T(8,128)S(1)}, f32[36,192]{1,0:T(8,128)S(1)}, u32[]{:S(2)}, u32[]{:S(2)}) collective-permute-start(f32[36,192]{1,0:T(8,128)S(1)} %get-tuple-element.14), channel_id=1, source_target_pairs={{1,0},{2,1},{3,2},{4,3},{5,4},{6,5},{7,6},{8,7},{9,8},{10,9},{11,1... | collective-permute-start | bytes 82952 | tf_op jit(solution)/shard_map/ppermute | solution.py:86
  (29 other events, 173.8 us)

commit v6 on v5

--- a/solution.py
+++ b/solution.py
@@ -14,12 +14,17 @@
 
 
 HIGHEST = lax.Precision.HIGHEST
+HIGH = lax.Precision.HIGH
 penalty_fine = 1.0
 penalty_middle = 1.0
 
 
 def mm(a, b):
     return jnp.dot(a, b, precision=HIGHEST, preferred_element_type=jnp.float32)
+
+
+def pick(a, b):
+    return jnp.dot(a, b, precision=HIGH, preferred_element_type=jnp.float32)
 
 
 def orient_lookup(points):
@@ -112,14 +117,14 @@
     product = both[:cube]
     traces = both[cube:].reshape(6, plane, elements)
     region_out = jnp.einsum(
-        "snj,sjk->snk", traces[2:4], pick_region, precision=HIGHEST,
+        "snj,sjk->snk", traces[2:4], pick_region, precision=HIGH,
         preferred_element_type=jnp.float32,
     )
     from_region_low, from_region_high = region_exchange(region_out)
     received = None
     if group_ghosts is None:
         group_out = jnp.einsum(
-            "snj,sjk->snk", traces[0:2], pick_group, precision=HIGHEST,
+            "snj,sjk->snk", traces[0:2], pick_group, precision=HIGH,
             preferred_element_type=jnp.float32,
         )
         if extra is not None:
@@ -131,18 +136,18 @@
     raw = jnp.concatenate(
         [group_ghosts[0], group_ghosts[1], from_region_low, from_region_high], axis=1
     )
-    turned = mm(jnp.asarray(orient_matrix(points)), raw).reshape(8, plane, -1)
+    turned = pick(jnp.asarray(orient_matrix(points)), raw).reshape(8, plane, -1)
     ghosts = jnp.sum(turned * codes[:, None, :], axis=0)
     swapped = traces[np.array([1, 0, 3, 2, 5, 4])]
     source = jnp.concatenate(
         [swapped, jnp.broadcast_to(ghosts[None], (6,) + ghosts.shape)], axis=2
     )
     outside = jnp.einsum(
-        "fnq,fqe->fne", source, gather.astype(jnp.float32), precision=HIGHEST,
+        "fnq,fqe->fne", source, gather.astype(jnp.float32), precision=HIGH,
         preferred_element_type=jnp.float32,
     )
     jumps = (traces - outside).reshape(6 * plane, elements)
-    return product + mm(select.T, jumps), received
+    return product + pick(select.T, jumps), received
 
 
 def corner_values(window, ids, first_column, planes, vert_x):
@@ -155,7 +160,7 @@
     on_column = (
         column[:, None] == jnp.arange(window.shape[1], dtype=jnp.int32)[None, :]
     ).astype(jnp.float32)
-    picked = mm(window.T, on_plane)
+    picked = pick(window.T, on_plane)
     return jnp.sum(picked * on_column.T, axis=0).reshape(ids.shape)
 
 
@@ -255,7 +260,7 @@
     on_column = (column[:, None] == jnp.arange(BX + 1, dtype=jnp.int32)[None, :]).astype(
         jnp.float32
     )
-    local = mm(on_plane, corner_terms.reshape(-1)[:, None] * on_column)
+    local = pick(on_plane, corner_terms.reshape(-1)[:, None] * on_column)
     interior = gather_slab(local, width_group)
     solved = coarse_solve(interior)
     padded = jnp.pad(solved, ((1, 1), (1, 1), (1 + BX, 1 + BX)))

time: 175 us -> 170 us (0.971)
  matrix products: 31.3 us -> 26.5 us
    dot_general x26 -> x15, matrix products: 14.7 us -> 7.6 us  [mm(): return jnp.dot(a, b, precision=HIGHEST, preferred_element_type=jnp.float32)]
    dot_general x7 -> x18, matrix products: 2.76 us -> 7.49 us  [the longest x11 5.18 us: pick(): return jnp.dot(a, b, precision=HIGH, preferred_element_type=jnp.float32)]
    dot_general x4, matrix products: 11 us -> 8.58 us  [apply_level(): jnp.einsum('fnq,fqe->fne', source, gather.astype(jnp.float32), precision=...]
where the time goes in v6:
time: 170 us; the launch traced here: 167 us
  starting transfers between devices  103 us (61%)
  matrix products  26.5 us (16%)
  waiting for transfers between devices  20.7 us (12%)
  local copies, waits for them, and re-layouts  13.3 us (8%)
  other arithmetic  2.59 us (2%)
    ppermute x4, starting transfers between devices, region_exchange(): lax.ppermute(jnp.where(odd, region_out[1], region_out[0]), 'region', far_...  43.2 us
    ppermute x5, starting transfers between devices, gather_slab(): interior = interior + lax.ppermute(interior, 'group', partner)  24.2 us
    ppermute x4, starting transfers between devices, region_exchange(): lax.ppermute(jnp.where(odd, region_out[0], region_out[1]), 'region', near...  21.8 us
    ppermute x5, waiting for transfers between devices, gather_slab(): interior = interior + lax.ppermute(interior, 'group', partner)  15 us
    ppermute x6, starting transfers between devices, shift(): return lax.ppermute(block, axis, pairs)  13.5 us
    dot_general x4, matrix products, apply_level(): jnp.einsum('fnq,fqe->fne', source, gather.astype(jnp.float32), precision=...  8.58 us
    dot_general x15, matrix products, mm(): return jnp.dot(a, b, precision=HIGHEST, preferred_element_type=jnp.float32)  7.6 us
    unnamed x69, local copies, waits for them, and re-layouts  6.01 us
  transfers between devices with their start and end apart: 19, of which 9 were waited for; matrix products, arithmetic and copies ran while one was open for 6% of the time, Pallas kernels for 0%

profile of v6, /device:TPU:1, one launch (start us, length us, event | category | flops | bytes accessed | tf_op | source)
XLA Modules:
  0.0 167.2 jit_solution(14362662986196042417)
XLA Ops:
  4.3 16.1 %collective-permute-start.2 = (f32[36,48]{1,0:T(8,128)S(1)}, f32[36,48]{1,0:T(8,128)S(1)}, u32[]{:S(2)}, u32[]{:S(2)}) collective-permute-start(f32[36,48]{1,0:T(8,128)S(1)} %get-tuple-element.21), channel_id=1, source_target_pairs={{0,32},{64,96},{128,160},{192,224},{256,288},{320,352},{384,416},{... | collective-permute-start | bytes 20744 | tf_op jit(solution)/shard_map/ppermute | solution.py:104
  20.4 2.7 %collective-permute-start.3 = (f32[36,48]{1,0:T(8,128)S(1)}, f32[36,48]{1,0:T(8,128)S(1)}, u32[]{:S(2)}, u32[]{:S(2)}) collective-permute-start(f32[36,48]{1,0:T(8,128)S(1)} %get-tuple-element.22), channel_id=1, source_target_pairs={{32,64},{96,128},{160,192},{224,256},{288,320},{352,384},{416,448}... | collective-permute-start | bytes 20744 | tf_op jit(solution)/shard_map/ppermute | solution.py:101
  24.1 3.2 %collective-permute-start = (f32[44,192]{1,0:T(8,128)S(1)}, f32[44,192]{1,0:T(8,128)S(1)}, u32[]{:S(2)}, u32[]{:S(2)}) collective-permute-start(f32[44,192]{1,0:T(8,128)S(1)} %get-tuple-element.11), channel_id=1, source_target_pairs={{0,1},{1,2},{2,3},{3,4},{4,5},{5,6},{6,7},{7,8},{8,9},{9,10},{10,1... | collective-permute-start | bytes 101384 | tf_op jit(solution)/shard_map/ppermute | solution.py:91
  35.8 2.2 %fusion.12 = f32[6,36,384]{2,1,0:T(8,128)S(1)} fusion(f32[6,36,384]{2,1,0:T(8,128)S(1)} %reshape.335, s32[6,384]{1,0:T(8,128)S(1)} %bitcast.129, f32[6,36,480]{2,1,0:T(8,128)S(1)} %broadcast_in_dim.19, f32[6,36,384]{2,1,0:T(8,128)S(1)} %copy-done.8), kind=kOutput, calls=%fused_computation.21 | convolution fusion | flops 432241920 | bytes 1419264 | tf_op jit(solution)/shard_map/fnq,fqe->fne/dot_general | solution.py:145
  43.0 15.1 %collective-permute-start.7 = (f32[9,48]{1,0:T(8,128)S(1)}, f32[9,48]{1,0:T(8,128)S(1)}, u32[]{:S(2)}, u32[]{:S(2)}) collective-permute-start(f32[9,48]{1,0:T(8,128)S(1)} %get-tuple-element.32), channel_id=1, source_target_pairs={{32,64},{96,128},{160,192},{224,256},{288,320},{352,384},{416,448}... | collective-permute-start | bytes 5192 | tf_op jit(solution)/shard_map/ppermute | solution.py:101
  58.6 4.0 %collective-permute-start.4 = (f32[9,192]{1,0:T(8,128)S(1)}, f32[9,192]{1,0:T(8,128)S(1)}, u32[]{:S(2)}, u32[]{:S(2)}) collective-permute-start(f32[9,192]{1,0:T(8,128)S(1)} %get-tuple-element.23), channel_id=1, source_target_pairs={{0,1},{1,2},{2,3},{3,4},{4,5},{5,6},{6,7},{7,8},{8,9},{9,10},{10,1... | collective-permute-start | bytes 20744 | tf_op jit(solution)/shard_map/ppermute | solution.py:91
  64.5 2.5 %collective-permute-done.5 = f32[9,192]{1,0:T(8,128)S(1)} collective-permute-done((f32[9,192]{1,0:T(8,128)S(1)}, f32[9,192]{1,0:T(8,128)S(1)}, u32[]{:S(2)}, u32[]{:S(2)}) %collective-permute-start.5) | collective-permute-done | bytes 6944 | tf_op jit(solution)/shard_map/ppermute | solution.py:91
  67.5 2.1 %fusion.18 = f32[6,9,384]{2,1,0:T(8,128)S(1)} fusion(f32[6,9,384]{2,1,0:T(8,128)S(1)} %reshape.339, s32[6,384]{1,0:T(8,128)S(1)} %bitcast.130, f32[6,9,480]{2,1,0:T(8,128)S(1)} %broadcast_in_dim.22, f32[6,9,384]{2,1,0:T(8,128)S(1)} %gather_fusion.1), kind=kOutput, calls=%fused_computation.31 | convolution fusion | flops 109553472 | bytes 361728 | tf_op jit(solution)/shard_map/fnq,fqe->fne/dot_general | solution.py:145
  71.6 3.5 %collective-permute-start.8 = (f32[23,7,63]{2,1,0:T(8,128)S(1)}, f32[23,7,63]{2,1,0:T(8,128)S(1)}, u32[]{:S(2)}, u32[]{:S(2)}) collective-permute-start(f32[23,7,63]{2,1,0:T(8,128)S(1)} %slice.217), channel_id=1, source_target_pairs={{0,1},{1,0},{2,3},{3,2},{4,5},{5,4},{6,7},{7,6},{8,9},{9,8},{10,11... | collective-permute-start | bytes 121724 | tf_op jit(solution)/shard_map/ppermute | solution.py:217
  75.1 2.9 %collective-permute-done.8 = f32[23,7,63]{2,1,0:T(8,128)S(1)} collective-permute-done((f32[23,7,63]{2,1,0:T(8,128)S(1)}, f32[23,7,63]{2,1,0:T(8,128)S(1)}, u32[]{:S(2)}, u32[]{:S(2)}) %collective-permute-start.8) | collective-permute-done | bytes 40604 | tf_op jit(solution)/shard_map/ppermute | solution.py:217
  78.1 6.8 %collective-permute-start.9 = (f32[23,7,63]{2,1,0:T(8,128)S(1)}, f32[23,7,63]{2,1,0:T(8,128)S(1)}, u32[]{:S(2)}, u32[]{:S(2)}) collective-permute-start(f32[23,7,63]{2,1,0:T(8,128)S(1)} %slice_add_fusion), channel_id=1, source_target_pairs={{0,2},{1,3},{2,0},{3,1},{4,6},{5,7},{6,4},{7,5},{8,10},{9,11},{10,... | collective-permute-start | bytes 121724 | tf_op jit(solution)/shard_map/ppermute | solution.py:217
  85.0 1.9 %collective-permute-done.9 = f32[23,7,63]{2,1,0:T(8,128)S(1)} collective-permute-done((f32[23,7,63]{2,1,0:T(8,128)S(1)}, f32[23,7,63]{2,1,0:T(8,128)S(1)}, u32[]{:S(2)}, u32[]{:S(2)}) %collective-permute-start.9) | collective-permute-done | bytes 40604 | tf_op jit(solution)/shard_map/ppermute | solution.py:217
  86.9 2.6 %collective-permute-start.10 = (f32[23,7,63]{2,1,0:T(8,128)S(1)}, f32[23,7,63]{2,1,0:T(8,128)S(1)}, u32[]{:S(2)}, u32[]{:S(2)}) collective-permute-start(f32[23,7,63]{2,1,0:T(8,128)S(1)} %add.221), channel_id=1, source_target_pairs={{0,4},{1,5},{2,6},{3,7},{4,0},{5,1},{6,2},{7,3},{8,12},{9,13},{10,... | collective-permute-start | bytes 121724 | tf_op jit(solution)/shard_map/ppermute | solution.py:217
  92.3 6.0 %collective-permute-start.11 = (f32[23,7,63]{2,1,0:T(8,128)S(1)}, f32[23,7,63]{2,1,0:T(8,128)S(1)}, u32[]{:S(2)}, u32[]{:S(2)}) collective-permute-start(f32[23,7,63]{2,1,0:T(8,128)S(1)} %add.222), channel_id=1, source_target_pairs={{0,8},{1,9},{2,10},{3,11},{4,12},{5,13},{6,14},{7,15},{8,0},{9,1},... | collective-permute-start | bytes 121724 | tf_op jit(solution)/shard_map/ppermute | solution.py:217
  98.3 2.9 %collective-permute-done.11 = f32[23,7,63]{2,1,0:T(8,128)S(1)} collective-permute-done((f32[23,7,63]{2,1,0:T(8,128)S(1)}, f32[23,7,63]{2,1,0:T(8,128)S(1)}, u32[]{:S(2)}, u32[]{:S(2)}) %collective-permute-start.11) | collective-permute-done | bytes 40604 | tf_op jit(solution)/shard_map/ppermute | solution.py:217
  101.2 5.3 %collective-permute-start.12 = (f32[23,7,63]{2,1,0:T(8,128)S(1)}, f32[23,7,63]{2,1,0:T(8,128)S(1)}, u32[]{:S(2)}, u32[]{:S(2)}) collective-permute-start(f32[23,7,63]{2,1,0:T(8,128)S(1)} %add.223), channel_id=1, source_target_pairs={{0,16},{1,17},{2,18},{3,19},{4,20},{5,21},{6,22},{7,23},{8,24},{9,... | collective-permute-start | bytes 121724 | tf_op jit(solution)/shard_map/ppermute | solution.py:217
  106.6 6.1 %collective-permute-done.12 = f32[23,7,63]{2,1,0:T(8,128)S(1)} collective-permute-done((f32[23,7,63]{2,1,0:T(8,128)S(1)}, f32[23,7,63]{2,1,0:T(8,128)S(1)}, u32[]{:S(2)}, u32[]{:S(2)}) %collective-permute-start.12) | collective-permute-done | bytes 40604 | tf_op jit(solution)/shard_map/ppermute | solution.py:217
  118.6 1.9 %collective-permute-start.13 = (f32[9,48]{1,0:T(8,128)S(1)}, f32[9,48]{1,0:T(8,128)S(1)}, u32[]{:S(2)}, u32[]{:S(2)}) collective-permute-start(f32[9,48]{1,0:T(8,128)S(1)} %get-tuple-element.27), channel_id=1, source_target_pairs={{0,32},{64,96},{128,160},{192,224},{256,288},{320,352},{384,416},{... | collective-permute-start | bytes 5192 | tf_op jit(solution)/shard_map/ppermute | solution.py:104
  120.6 12.6 %collective-permute-start.14 = (f32[9,48]{1,0:T(8,128)S(1)}, f32[9,48]{1,0:T(8,128)S(1)}, u32[]{:S(2)}, u32[]{:S(2)}) collective-permute-start(f32[9,48]{1,0:T(8,128)S(1)} %get-tuple-element.28), channel_id=1, source_target_pairs={{32,64},{96,128},{160,192},{224,256},{288,320},{352,384},{416,448}... | collective-permute-start | bytes 5192 | tf_op jit(solution)/shard_map/ppermute | solution.py:101
  134.8 2.1 %fusion.19 = f32[6,9,384]{2,1,0:T(8,128)S(1)} fusion(f32[6,9,384]{2,1,0:T(8,128)S(1)} %reshape.345, s32[6,384]{1,0:T(8,128)S(1)} %bitcast.131, f32[6,9,480]{2,1,0:T(8,128)S(1)} %broadcast_in_dim.24, f32[6,9,384]{2,1,0:T(8,128)S(1)} %gather_fusion.2), kind=kOutput, calls=%fused_computation.32 | convolution fusion | flops 109553472 | bytes 361728 | tf_op jit(solution)/shard_map/fnq,fqe->fne/dot_general | solution.py:145
  141.0 12.8 %collective-permute-start.18 = (f32[36,48]{1,0:T(8,128)S(1)}, f32[36,48]{1,0:T(8,128)S(1)}, u32[]{:S(2)}, u32[]{:S(2)}) collective-permute-start(f32[36,48]{1,0:T(8,128)S(1)} %get-tuple-element.18), channel_id=1, source_target_pairs={{32,64},{96,128},{160,192},{224,256},{288,320},{352,384},{416,448}... | collective-permute-start | bytes 20744 | tf_op jit(solution)/shard_map/ppermute | solution.py:101
  154.4 2.5 %collective-permute-start.15 = (f32[36,192]{1,0:T(8,128)S(1)}, f32[36,192]{1,0:T(8,128)S(1)}, u32[]{:S(2)}, u32[]{:S(2)}) collective-permute-start(f32[36,192]{1,0:T(8,128)S(1)} %get-tuple-element.13), channel_id=1, source_target_pairs={{0,1},{1,2},{2,3},{3,4},{4,5},{5,6},{6,7},{7,8},{8,9},{9,10},{10,1... | collective-permute-start | bytes 82952 | tf_op jit(solution)/shard_map/ppermute | solution.py:91
  159.6 2.0 %collective-permute-done.16 = f32[36,192]{1,0:T(8,128)S(1)} collective-permute-done((f32[36,192]{1,0:T(8,128)S(1)}, f32[36,192]{1,0:T(8,128)S(1)}, u32[]{:S(2)}, u32[]{:S(2)}) %collective-permute-start.16) | collective-permute-done | bytes 27680 | tf_op jit(solution)/shard_map/ppermute | solution.py:91
  163.3 2.2 %fusion.13 = f32[6,36,384]{2,1,0:T(8,128)S(1)} fusion(f32[6,36,384]{2,1,0:T(8,128)S(1)} %copy-done.4, s32[6,384]{1,0:T(8,128)S(1)} %bitcast.132, f32[6,36,480]{2,1,0:T(8,128)S(1)} %broadcast_in_dim.26, f32[6,36,384]{2,1,0:T(8,128)S(1)} %copy-done.9), kind=kOutput, calls=%fused_computation.22 | convolution fusion | flops 432241920 | bytes 1419264 | tf_op jit(solution)/shard_map/fnq,fqe->fne/dot_general | solution.py:145
  (210 shorter events, 43.8 us)
Async XLA Ops:
  3.4 25.4 %copy-start.27 = (s32[1,480]{1,0:T(1,128)S(1)}, s32[1,480]{1,0:T(1,128)}, u32[]{:S(2)}) copy-start(s32[1,480]{1,0:T(1,128)} %param.40) | copy-start | bytes 5764
  3.4 25.4 %copy-start.28 = (s32[6]{0:T(128)S(1)}, s32[6]{0:T(128)}, u32[]{:S(2)}) copy-start(s32[6]{0:T(128)} %constant.162) | copy-start | bytes 76
  4.3 29.2 %collective-permute-start.2 = (f32[36,48]{1,0:T(8,128)S(1)}, f32[36,48]{1,0:T(8,128)S(1)}, u32[]{:S(2)}, u32[]{:S(2)}) collective-permute-start(f32[36,48]{1,0:T(8,128)S(1)} %get-tuple-element.21), channel_id=1, source_target_pairs={{0,32},{64,96},{128,160},{192,224},{256,288},{320,352},{384,416},{... | collective-permute-start | bytes 20744 | tf_op jit(solution)/shard_map/ppermute | solution.py:104
  20.4 13.8 %collective-permute-start.3 = (f32[36,48]{1,0:T(8,128)S(1)}, f32[36,48]{1,0:T(8,128)S(1)}, u32[]{:S(2)}, u32[]{:S(2)}) collective-permute-start(f32[36,48]{1,0:T(8,128)S(1)} %get-tuple-element.22), channel_id=1, source_target_pairs={{32,64},{96,128},{160,192},{224,256},{288,320},{352,384},{416,448}... | collective-permute-start | bytes 20744 | tf_op jit(solution)/shard_map/ppermute | solution.py:101
  24.1 10.1 %collective-permute-start = (f32[44,192]{1,0:T(8,128)S(1)}, f32[44,192]{1,0:T(8,128)S(1)}, u32[]{:S(2)}, u32[]{:S(2)}) collective-permute-start(f32[44,192]{1,0:T(8,128)S(1)} %get-tuple-element.11), channel_id=1, source_target_pairs={{0,1},{1,2},{2,3},{3,4},{4,5},{5,6},{6,7},{7,8},{8,9},{9,10},{10,1... | collective-permute-start | bytes 101384 | tf_op jit(solution)/shard_map/ppermute | solution.py:91
  27.3 6.9 %collective-permute-start.1 = (f32[44,192]{1,0:T(8,128)S(1)}, f32[44,192]{1,0:T(8,128)S(1)}, u32[]{:S(2)}, u32[]{:S(2)}) collective-permute-start(f32[44,192]{1,0:T(8,128)S(1)} %get-tuple-element.12), channel_id=1, source_target_pairs={{1,0},{2,1},{3,2},{4,3},{5,4},{6,5},{7,6},{8,7},{9,8},{10,9},{11,1... | collective-permute-start | bytes 101384 | tf_op jit(solution)/shard_map/ppermute | solution.py:91
  40.8 26.3 %copy-start.11 = (f32[72,9]{1,0:T(8,128)S(1)}, f32[72,9]{1,0:T(8,128)}, u32[]{:S(2)}) copy-start(f32[72,9]{1,0:T(8,128)} %constant.150.clone) | copy-start | bytes 7780
  41.1 23.4 %collective-permute-start.6 = (f32[9,48]{1,0:T(8,128)S(1)}, f32[9,48]{1,0:T(8,128)S(1)}, u32[]{:S(2)}, u32[]{:S(2)}) collective-permute-start(f32[9,48]{1,0:T(8,128)S(1)} %get-tuple-element.31), channel_id=1, source_target_pairs={{0,32},{64,96},{128,160},{192,224},{256,288},{320,352},{384,416},{... | collective-permute-start | bytes 5192 | tf_op jit(solution)/shard_map/ppermute | solution.py:104
  43.0 21.5 %collective-permute-start.7 = (f32[9,48]{1,0:T(8,128)S(1)}, f32[9,48]{1,0:T(8,128)S(1)}, u32[]{:S(2)}, u32[]{:S(2)}) collective-permute-start(f32[9,48]{1,0:T(8,128)S(1)} %get-tuple-element.32), channel_id=1, source_target_pairs={{32,64},{96,128},{160,192},{224,256},{288,320},{352,384},{416,448}... | collective-permute-start | bytes 5192 | tf_op jit(solution)/shard_map/ppermute | solution.py:101
  58.6 5.9 %collective-permute-start.4 = (f32[9,192]{1,0:T(8,128)S(1)}, f32[9,192]{1,0:T(8,128)S(1)}, u32[]{:S(2)}, u32[]{:S(2)}) collective-permute-start(f32[9,192]{1,0:T(8,128)S(1)} %get-tuple-element.23), channel_id=1, source_target_pairs={{0,1},{1,2},{2,3},{3,4},{4,5},{5,6},{6,7},{7,8},{8,9},{9,10},{10,1... | collective-permute-start | bytes 20744 | tf_op jit(solution)/shard_map/ppermute | solution.py:91
  62.6 4.5 %collective-permute-start.5 = (f32[9,192]{1,0:T(8,128)S(1)}, f32[9,192]{1,0:T(8,128)S(1)}, u32[]{:S(2)}, u32[]{:S(2)}) collective-permute-start(f32[9,192]{1,0:T(8,128)S(1)} %get-tuple-element.24), channel_id=1, source_target_pairs={{1,0},{2,1},{3,2},{4,3},{5,4},{6,5},{7,6},{8,7},{9,8},{10,9},{11,1... | collective-permute-start | bytes 20744 | tf_op jit(solution)/shard_map/ppermute | solution.py:91
  71.6 6.4 %collective-permute-start.8 = (f32[23,7,63]{2,1,0:T(8,128)S(1)}, f32[23,7,63]{2,1,0:T(8,128)S(1)}, u32[]{:S(2)}, u32[]{:S(2)}) collective-permute-start(f32[23,7,63]{2,1,0:T(8,128)S(1)} %slice.217), channel_id=1, source_target_pairs={{0,1},{1,0},{2,3},{3,2},{4,5},{5,4},{6,7},{7,6},{8,9},{9,8},{10,11... | collective-permute-start | bytes 121724 | tf_op jit(solution)/shard_map/ppermute | solution.py:217
  78.1 8.8 %collective-permute-start.9 = (f32[23,7,63]{2,1,0:T(8,128)S(1)}, f32[23,7,63]{2,1,0:T(8,128)S(1)}, u32[]{:S(2)}, u32[]{:S(2)}) collective-permute-start(f32[23,7,63]{2,1,0:T(8,128)S(1)} %slice_add_fusion), channel_id=1, source_target_pairs={{0,2},{1,3},{2,0},{3,1},{4,6},{5,7},{6,4},{7,5},{8,10},{9,11},{10,... | collective-permute-start | bytes 121724 | tf_op jit(solution)/shard_map/ppermute | solution.py:217
  86.9 5.3 %collective-permute-start.10 = (f32[23,7,63]{2,1,0:T(8,128)S(1)}, f32[23,7,63]{2,1,0:T(8,128)S(1)}, u32[]{:S(2)}, u32[]{:S(2)}) collective-permute-start(f32[23,7,63]{2,1,0:T(8,128)S(1)} %add.221), channel_id=1, source_target_pairs={{0,4},{1,5},{2,6},{3,7},{4,0},{5,1},{6,2},{7,3},{8,12},{9,13},{10,... | collective-permute-start | bytes 121724 | tf_op jit(solution)/shard_map/ppermute | solution.py:217
  90.3 23.2 %copy-start.32 = (f32[63]{0:T(128)S(1)}, f32[63]{0:T(128)}, u32[]{:S(2)}) copy-start(f32[63]{0:T(128)} %get-tuple-element.43) | copy-start | bytes 760
  90.3 23.2 %copy-start.33 = (f32[63]{0:T(128)S(1)}, f32[63]{0:T(128)}, u32[]{:S(2)}) copy-start(f32[63]{0:T(128)} %get-tuple-element.44) | copy-start | bytes 760
  92.3 8.9 %collective-permute-start.11 = (f32[23,7,63]{2,1,0:T(8,128)S(1)}, f32[23,7,63]{2,1,0:T(8,128)S(1)}, u32[]{:S(2)}, u32[]{:S(2)}) collective-permute-start(f32[23,7,63]{2,1,0:T(8,128)S(1)} %add.222), channel_id=1, source_target_pairs={{0,8},{1,9},{2,10},{3,11},{4,12},{5,13},{6,14},{7,15},{8,0},{9,1},... | collective-permute-start | bytes 121724 | tf_op jit(solution)/shard_map/ppermute | solution.py:217
  101.2 11.5 %collective-permute-start.12 = (f32[23,7,63]{2,1,0:T(8,128)S(1)}, f32[23,7,63]{2,1,0:T(8,128)S(1)}, u32[]{:S(2)}, u32[]{:S(2)}) collective-permute-start(f32[23,7,63]{2,1,0:T(8,128)S(1)} %add.223), channel_id=1, source_target_pairs={{0,16},{1,17},{2,18},{3,19},{4,20},{5,21},{6,22},{7,23},{8,24},{9,... | collective-permute-start | bytes 121724 | tf_op jit(solution)/shard_map/ppermute | solution.py:217
  118.6 15.5 %collective-permute-start.13 = (f32[9,48]{1,0:T(8,128)S(1)}, f32[9,48]{1,0:T(8,128)S(1)}, u32[]{:S(2)}, u32[]{:S(2)}) collective-permute-start(f32[9,48]{1,0:T(8,128)S(1)} %get-tuple-element.27), channel_id=1, source_target_pairs={{0,32},{64,96},{128,160},{192,224},{256,288},{320,352},{384,416},{... | collective-permute-start | bytes 5192 | tf_op jit(solution)/shard_map/ppermute | solution.py:104
  120.6 13.9 %collective-permute-start.14 = (f32[9,48]{1,0:T(8,128)S(1)}, f32[9,48]{1,0:T(8,128)S(1)}, u32[]{:S(2)}, u32[]{:S(2)}) collective-permute-start(f32[9,48]{1,0:T(8,128)S(1)} %get-tuple-element.28), channel_id=1, source_target_pairs={{32,64},{96,128},{160,192},{224,256},{288,320},{352,384},{416,448}... | collective-permute-start | bytes 5192 | tf_op jit(solution)/shard_map/ppermute | solution.py:101
  139.1 20.5 %collective-permute-start.17 = (f32[36,48]{1,0:T(8,128)S(1)}, f32[36,48]{1,0:T(8,128)S(1)}, u32[]{:S(2)}, u32[]{:S(2)}) collective-permute-start(f32[36,48]{1,0:T(8,128)S(1)} %get-tuple-element.17), channel_id=1, source_target_pairs={{0,32},{64,96},{128,160},{192,224},{256,288},{320,352},{384,416},{... | collective-permute-start | bytes 20744 | tf_op jit(solution)/shard_map/ppermute | solution.py:104
  141.0 18.5 %collective-permute-start.18 = (f32[36,48]{1,0:T(8,128)S(1)}, f32[36,48]{1,0:T(8,128)S(1)}, u32[]{:S(2)}, u32[]{:S(2)}) collective-permute-start(f32[36,48]{1,0:T(8,128)S(1)} %get-tuple-element.18), channel_id=1, source_target_pairs={{32,64},{96,128},{160,192},{224,256},{288,320},{352,384},{416,448}... | collective-permute-start | bytes 20744 | tf_op jit(solution)/shard_map/ppermute | solution.py:101
  154.4 5.2 %collective-permute-start.15 = (f32[36,192]{1,0:T(8,128)S(1)}, f32[36,192]{1,0:T(8,128)S(1)}, u32[]{:S(2)}, u32[]{:S(2)}) collective-permute-start(f32[36,192]{1,0:T(8,128)S(1)} %get-tuple-element.13), channel_id=1, source_target_pairs={{0,1},{1,2},{2,3},{3,4},{4,5},{5,6},{6,7},{7,8},{8,9},{9,10},{10,1... | collective-permute-start | bytes 82952 | tf_op jit(solution)/shard_map/ppermute | solution.py:91
  156.9 4.7 %collective-permute-start.16 = (f32[36,192]{1,0:T(8,128)S(1)}, f32[36,192]{1,0:T(8,128)S(1)}, u32[]{:S(2)}, u32[]{:S(2)}) collective-permute-start(f32[36,192]{1,0:T(8,128)S(1)} %get-tuple-element.14), channel_id=1, source_target_pairs={{1,0},{2,1},{3,2},{4,3},{5,4},{6,5},{7,6},{8,7},{9,8},{10,9},{11,1... | collective-permute-start | bytes 82952 | tf_op jit(solution)/shard_map/ppermute | solution.py:91
  (29 other events, 170.6 us)

commit v7 on v6

--- a/solution.py
+++ b/solution.py
@@ -98,11 +98,11 @@
     far_pairs += [(i, i - 1) for i in range(2, count, 2)]
     near_pairs = [(i, i + 1) for i in range(0, count - 1, 2)]
     near_pairs += [(i + 1, i) for i in range(0, count - 1, 2)]
+    near_recv = lax.ppermute(
+        jnp.where(odd, region_out[0], region_out[1]), "region", near_pairs
+    )
     far_recv = lax.ppermute(
         jnp.where(odd, region_out[1], region_out[0]), "region", far_pairs
-    )
-    near_recv = lax.ppermute(
-        jnp.where(odd, region_out[0], region_out[1]), "region", near_pairs
     )
     return jnp.where(odd, near_recv, far_recv), jnp.where(odd, far_recv, near_recv)
 

time: 170 us -> 170 us (level)
  no operation moved by 1% of the time
where the time goes in v7:
time: 170 us; the launch traced here: 167 us
  starting transfers between devices  103 us (61%)
  matrix products  26.5 us (16%)
  waiting for transfers between devices  20.7 us (12%)
  local copies, waits for them, and re-layouts  13.3 us (8%)
  other arithmetic  2.59 us (2%)
    ppermute x4, starting transfers between devices, region_exchange(): lax.ppermute(jnp.where(odd, region_out[1], region_out[0]), 'region', far_...  43.2 us
    ppermute x5, starting transfers between devices, gather_slab(): interior = interior + lax.ppermute(interior, 'group', partner)  24.2 us
    ppermute x4, starting transfers between devices, region_exchange(): lax.ppermute(jnp.where(odd, region_out[0], region_out[1]), 'region', near...  21.8 us
    ppermute x5, waiting for transfers between devices, gather_slab(): interior = interior + lax.ppermute(interior, 'group', partner)  15 us
    ppermute x6, starting transfers between devices, shift(): return lax.ppermute(block, axis, pairs)  13.5 us
    dot_general x4, matrix products, apply_level(): jnp.einsum('fnq,fqe->fne', source, gather.astype(jnp.float32), precision=...  8.58 us
    dot_general x15, matrix products, mm(): return jnp.dot(a, b, precision=HIGHEST, preferred_element_type=jnp.float32)  7.6 us
    unnamed x69, local copies, waits for them, and re-layouts  6.01 us
  transfers between devices with their start and end apart: 19, of which 9 were waited for; matrix products, arithmetic and copies ran while one was open for 6% of the time, Pallas kernels for 0%

profile of v7, /device:TPU:1, one launch (start us, length us, event | category | flops | bytes accessed | tf_op | source)
XLA Modules:
  0.0 167.2 jit_solution(14362662986196042417)
XLA Ops:
  4.3 16.1 %collective-permute-start.2 = (f32[36,48]{1,0:T(8,128)S(1)}, f32[36,48]{1,0:T(8,128)S(1)}, u32[]{:S(2)}, u32[]{:S(2)}) collective-permute-start(f32[36,48]{1,0:T(8,128)S(1)} %get-tuple-element.21), channel_id=1, source_target_pairs={{0,32},{64,96},{128,160},{192,224},{256,288},{320,352},{384,416},{... | collective-permute-start | bytes 20744 | tf_op jit(solution)/shard_map/ppermute | solution.py:101
  20.4 2.7 %collective-permute-start.3 = (f32[36,48]{1,0:T(8,128)S(1)}, f32[36,48]{1,0:T(8,128)S(1)}, u32[]{:S(2)}, u32[]{:S(2)}) collective-permute-start(f32[36,48]{1,0:T(8,128)S(1)} %get-tuple-element.22), channel_id=1, source_target_pairs={{32,64},{96,128},{160,192},{224,256},{288,320},{352,384},{416,448}... | collective-permute-start | bytes 20744 | tf_op jit(solution)/shard_map/ppermute | solution.py:104
  24.1 3.2 %collective-permute-start = (f32[44,192]{1,0:T(8,128)S(1)}, f32[44,192]{1,0:T(8,128)S(1)}, u32[]{:S(2)}, u32[]{:S(2)}) collective-permute-start(f32[44,192]{1,0:T(8,128)S(1)} %get-tuple-element.11), channel_id=1, source_target_pairs={{0,1},{1,2},{2,3},{3,4},{4,5},{5,6},{6,7},{7,8},{8,9},{9,10},{10,1... | collective-permute-start | bytes 101384 | tf_op jit(solution)/shard_map/ppermute | solution.py:91
  35.8 2.2 %fusion.12 = f32[6,36,384]{2,1,0:T(8,128)S(1)} fusion(f32[6,36,384]{2,1,0:T(8,128)S(1)} %reshape.335, s32[6,384]{1,0:T(8,128)S(1)} %bitcast.129, f32[6,36,480]{2,1,0:T(8,128)S(1)} %broadcast_in_dim.19, f32[6,36,384]{2,1,0:T(8,128)S(1)} %copy-done.8), kind=kOutput, calls=%fused_computation.21 | convolution fusion | flops 432241920 | bytes 1419264 | tf_op jit(solution)/shard_map/fnq,fqe->fne/dot_general | solution.py:145
  41.1 1.9 %collective-permute-start.6 = (f32[9,48]{1,0:T(8,128)S(1)}, f32[9,48]{1,0:T(8,128)S(1)}, u32[]{:S(2)}, u32[]{:S(2)}) collective-permute-start(f32[9,48]{1,0:T(8,128)S(1)} %get-tuple-element.31), channel_id=1, source_target_pairs={{0,32},{64,96},{128,160},{192,224},{256,288},{320,352},{384,416},{... | collective-permute-start | bytes 5192 | tf_op jit(solution)/shard_map/ppermute | solution.py:101
  43.0 15.1 %collective-permute-start.7 = (f32[9,48]{1,0:T(8,128)S(1)}, f32[9,48]{1,0:T(8,128)S(1)}, u32[]{:S(2)}, u32[]{:S(2)}) collective-permute-start(f32[9,48]{1,0:T(8,128)S(1)} %get-tuple-element.32), channel_id=1, source_target_pairs={{32,64},{96,128},{160,192},{224,256},{288,320},{352,384},{416,448}... | collective-permute-start | bytes 5192 | tf_op jit(solution)/shard_map/ppermute | solution.py:104
  58.6 4.0 %collective-permute-start.4 = (f32[9,192]{1,0:T(8,128)S(1)}, f32[9,192]{1,0:T(8,128)S(1)}, u32[]{:S(2)}, u32[]{:S(2)}) collective-permute-start(f32[9,192]{1,0:T(8,128)S(1)} %get-tuple-element.23), channel_id=1, source_target_pairs={{0,1},{1,2},{2,3},{3,4},{4,5},{5,6},{6,7},{7,8},{8,9},{9,10},{10,1... | collective-permute-start | bytes 20744 | tf_op jit(solution)/shard_map/ppermute | solution.py:91
  64.5 2.5 %collective-permute-done.5 = f32[9,192]{1,0:T(8,128)S(1)} collective-permute-done((f32[9,192]{1,0:T(8,128)S(1)}, f32[9,192]{1,0:T(8,128)S(1)}, u32[]{:S(2)}, u32[]{:S(2)}) %collective-permute-start.5) | collective-permute-done | bytes 6944 | tf_op jit(solution)/shard_map/ppermute | solution.py:91
  67.5 2.1 %fusion.18 = f32[6,9,384]{2,1,0:T(8,128)S(1)} fusion(f32[6,9,384]{2,1,0:T(8,128)S(1)} %reshape.339, s32[6,384]{1,0:T(8,128)S(1)} %bitcast.130, f32[6,9,480]{2,1,0:T(8,128)S(1)} %broadcast_in_dim.22, f32[6,9,384]{2,1,0:T(8,128)S(1)} %gather_fusion.1), kind=kOutput, calls=%fused_computation.31 | convolution fusion | flops 109553472 | bytes 361728 | tf_op jit(solution)/shard_map/fnq,fqe->fne/dot_general | solution.py:145
  71.6 3.5 %collective-permute-start.8 = (f32[23,7,63]{2,1,0:T(8,128)S(1)}, f32[23,7,63]{2,1,0:T(8,128)S(1)}, u32[]{:S(2)}, u32[]{:S(2)}) collective-permute-start(f32[23,7,63]{2,1,0:T(8,128)S(1)} %slice.217), channel_id=1, source_target_pairs={{0,1},{1,0},{2,3},{3,2},{4,5},{5,4},{6,7},{7,6},{8,9},{9,8},{10,11... | collective-permute-start | bytes 121724 | tf_op jit(solution)/shard_map/ppermute | solution.py:217
  75.1 2.9 %collective-permute-done.8 = f32[23,7,63]{2,1,0:T(8,128)S(1)} collective-permute-done((f32[23,7,63]{2,1,0:T(8,128)S(1)}, f32[23,7,63]{2,1,0:T(8,128)S(1)}, u32[]{:S(2)}, u32[]{:S(2)}) %collective-permute-start.8) | collective-permute-done | bytes 40604 | tf_op jit(solution)/shard_map/ppermute | solution.py:217
  78.1 6.8 %collective-permute-start.9 = (f32[23,7,63]{2,1,0:T(8,128)S(1)}, f32[23,7,63]{2,1,0:T(8,128)S(1)}, u32[]{:S(2)}, u32[]{:S(2)}) collective-permute-start(f32[23,7,63]{2,1,0:T(8,128)S(1)} %slice_add_fusion), channel_id=1, source_target_pairs={{0,2},{1,3},{2,0},{3,1},{4,6},{5,7},{6,4},{7,5},{8,10},{9,11},{10,... | collective-permute-start | bytes 121724 | tf_op jit(solution)/shard_map/ppermute | solution.py:217
  85.0 1.9 %collective-permute-done.9 = f32[23,7,63]{2,1,0:T(8,128)S(1)} collective-permute-done((f32[23,7,63]{2,1,0:T(8,128)S(1)}, f32[23,7,63]{2,1,0:T(8,128)S(1)}, u32[]{:S(2)}, u32[]{:S(2)}) %collective-permute-start.9) | collective-permute-done | bytes 40604 | tf_op jit(solution)/shard_map/ppermute | solution.py:217
  86.9 2.6 %collective-permute-start.10 = (f32[23,7,63]{2,1,0:T(8,128)S(1)}, f32[23,7,63]{2,1,0:T(8,128)S(1)}, u32[]{:S(2)}, u32[]{:S(2)}) collective-permute-start(f32[23,7,63]{2,1,0:T(8,128)S(1)} %add.221), channel_id=1, source_target_pairs={{0,4},{1,5},{2,6},{3,7},{4,0},{5,1},{6,2},{7,3},{8,12},{9,13},{10,... | collective-permute-start | bytes 121724 | tf_op jit(solution)/shard_map/ppermute | solution.py:217
  92.3 6.0 %collective-permute-start.11 = (f32[23,7,63]{2,1,0:T(8,128)S(1)}, f32[23,7,63]{2,1,0:T(8,128)S(1)}, u32[]{:S(2)}, u32[]{:S(2)}) collective-permute-start(f32[23,7,63]{2,1,0:T(8,128)S(1)} %add.222), channel_id=1, source_target_pairs={{0,8},{1,9},{2,10},{3,11},{4,12},{5,13},{6,14},{7,15},{8,0},{9,1},... | collective-permute-start | bytes 121724 | tf_op jit(solution)/shard_map/ppermute | solution.py:217
  98.3 2.9 %collective-permute-done.11 = f32[23,7,63]{2,1,0:T(8,128)S(1)} collective-permute-done((f32[23,7,63]{2,1,0:T(8,128)S(1)}, f32[23,7,63]{2,1,0:T(8,128)S(1)}, u32[]{:S(2)}, u32[]{:S(2)}) %collective-permute-start.11) | collective-permute-done | bytes 40604 | tf_op jit(solution)/shard_map/ppermute | solution.py:217
  101.2 5.3 %collective-permute-start.12 = (f32[23,7,63]{2,1,0:T(8,128)S(1)}, f32[23,7,63]{2,1,0:T(8,128)S(1)}, u32[]{:S(2)}, u32[]{:S(2)}) collective-permute-start(f32[23,7,63]{2,1,0:T(8,128)S(1)} %add.223), channel_id=1, source_target_pairs={{0,16},{1,17},{2,18},{3,19},{4,20},{5,21},{6,22},{7,23},{8,24},{9,... | collective-permute-start | bytes 121724 | tf_op jit(solution)/shard_map/ppermute | solution.py:217
  106.6 6.1 %collective-permute-done.12 = f32[23,7,63]{2,1,0:T(8,128)S(1)} collective-permute-done((f32[23,7,63]{2,1,0:T(8,128)S(1)}, f32[23,7,63]{2,1,0:T(8,128)S(1)}, u32[]{:S(2)}, u32[]{:S(2)}) %collective-permute-start.12) | collective-permute-done | bytes 40604 | tf_op jit(solution)/shard_map/ppermute | solution.py:217
  120.6 12.6 %collective-permute-start.14 = (f32[9,48]{1,0:T(8,128)S(1)}, f32[9,48]{1,0:T(8,128)S(1)}, u32[]{:S(2)}, u32[]{:S(2)}) collective-permute-start(f32[9,48]{1,0:T(8,128)S(1)} %get-tuple-element.28), channel_id=1, source_target_pairs={{32,64},{96,128},{160,192},{224,256},{288,320},{352,384},{416,448}... | collective-permute-start | bytes 5192 | tf_op jit(solution)/shard_map/ppermute | solution.py:104
  134.8 2.1 %fusion.19 = f32[6,9,384]{2,1,0:T(8,128)S(1)} fusion(f32[6,9,384]{2,1,0:T(8,128)S(1)} %reshape.345, s32[6,384]{1,0:T(8,128)S(1)} %bitcast.131, f32[6,9,480]{2,1,0:T(8,128)S(1)} %broadcast_in_dim.24, f32[6,9,384]{2,1,0:T(8,128)S(1)} %gather_fusion.2), kind=kOutput, calls=%fused_computation.32 | convolution fusion | flops 109553472 | bytes 361728 | tf_op jit(solution)/shard_map/fnq,fqe->fne/dot_general | solution.py:145
  141.0 12.8 %collective-permute-start.18 = (f32[36,48]{1,0:T(8,128)S(1)}, f32[36,48]{1,0:T(8,128)S(1)}, u32[]{:S(2)}, u32[]{:S(2)}) collective-permute-start(f32[36,48]{1,0:T(8,128)S(1)} %get-tuple-element.18), channel_id=1, source_target_pairs={{32,64},{96,128},{160,192},{224,256},{288,320},{352,384},{416,448}... | collective-permute-start | bytes 20744 | tf_op jit(solution)/shard_map/ppermute | solution.py:104
  154.4 2.5 %collective-permute-start.15 = (f32[36,192]{1,0:T(8,128)S(1)}, f32[36,192]{1,0:T(8,128)S(1)}, u32[]{:S(2)}, u32[]{:S(2)}) collective-permute-start(f32[36,192]{1,0:T(8,128)S(1)} %get-tuple-element.13), channel_id=1, source_target_pairs={{0,1},{1,2},{2,3},{3,4},{4,5},{5,6},{6,7},{7,8},{8,9},{9,10},{10,1... | collective-permute-start | bytes 82952 | tf_op jit(solution)/shard_map/ppermute | solution.py:91
  159.6 2.0 %collective-permute-done.16 = f32[36,192]{1,0:T(8,128)S(1)} collective-permute-done((f32[36,192]{1,0:T(8,128)S(1)}, f32[36,192]{1,0:T(8,128)S(1)}, u32[]{:S(2)}, u32[]{:S(2)}) %collective-permute-start.16) | collective-permute-done | bytes 27680 | tf_op jit(solution)/shard_map/ppermute | solution.py:91
  163.3 2.2 %fusion.13 = f32[6,36,384]{2,1,0:T(8,128)S(1)} fusion(f32[6,36,384]{2,1,0:T(8,128)S(1)} %copy-done.4, s32[6,384]{1,0:T(8,128)S(1)} %bitcast.132, f32[6,36,480]{2,1,0:T(8,128)S(1)} %broadcast_in_dim.26, f32[6,36,384]{2,1,0:T(8,128)S(1)} %copy-done.9), kind=kOutput, calls=%fused_computation.22 | convolution fusion | flops 432241920 | bytes 1419264 | tf_op jit(solution)/shard_map/fnq,fqe->fne/dot_general | solution.py:145
  (210 shorter events, 43.8 us)
Async XLA Ops:
  3.4 25.4 %copy-start.27 = (s32[1,480]{1,0:T(1,128)S(1)}, s32[1,480]{1,0:T(1,128)}, u32[]{:S(2)}) copy-start(s32[1,480]{1,0:T(1,128)} %param.40) | copy-start | bytes 5764
  3.4 25.4 %copy-start.28 = (s32[6]{0:T(128)S(1)}, s32[6]{0:T(128)}, u32[]{:S(2)}) copy-start(s32[6]{0:T(128)} %constant.162) | copy-start | bytes 76
  4.3 29.2 %collective-permute-start.2 = (f32[36,48]{1,0:T(8,128)S(1)}, f32[36,48]{1,0:T(8,128)S(1)}, u32[]{:S(2)}, u32[]{:S(2)}) collective-permute-start(f32[36,48]{1,0:T(8,128)S(1)} %get-tuple-element.21), channel_id=1, source_target_pairs={{0,32},{64,96},{128,160},{192,224},{256,288},{320,352},{384,416},{... | collective-permute-start | bytes 20744 | tf_op jit(solution)/shard_map/ppermute | solution.py:101
  20.4 13.8 %collective-permute-start.3 = (f32[36,48]{1,0:T(8,128)S(1)}, f32[36,48]{1,0:T(8,128)S(1)}, u32[]{:S(2)}, u32[]{:S(2)}) collective-permute-start(f32[36,48]{1,0:T(8,128)S(1)} %get-tuple-element.22), channel_id=1, source_target_pairs={{32,64},{96,128},{160,192},{224,256},{288,320},{352,384},{416,448}... | collective-permute-start | bytes 20744 | tf_op jit(solution)/shard_map/ppermute | solution.py:104
  24.1 10.1 %collective-permute-start = (f32[44,192]{1,0:T(8,128)S(1)}, f32[44,192]{1,0:T(8,128)S(1)}, u32[]{:S(2)}, u32[]{:S(2)}) collective-permute-start(f32[44,192]{1,0:T(8,128)S(1)} %get-tuple-element.11), channel_id=1, source_target_pairs={{0,1},{1,2},{2,3},{3,4},{4,5},{5,6},{6,7},{7,8},{8,9},{9,10},{10,1... | collective-permute-start | bytes 101384 | tf_op jit(solution)/shard_map/ppermute | solution.py:91
  27.3 6.9 %collective-permute-start.1 = (f32[44,192]{1,0:T(8,128)S(1)}, f32[44,192]{1,0:T(8,128)S(1)}, u32[]{:S(2)}, u32[]{:S(2)}) collective-permute-start(f32[44,192]{1,0:T(8,128)S(1)} %get-tuple-element.12), channel_id=1, source_target_pairs={{1,0},{2,1},{3,2},{4,3},{5,4},{6,5},{7,6},{8,7},{9,8},{10,9},{11,1... | collective-permute-start | bytes 101384 | tf_op jit(solution)/shard_map/ppermute | solution.py:91
  40.8 26.3 %copy-start.11 = (f32[72,9]{1,0:T(8,128)S(1)}, f32[72,9]{1,0:T(8,128)}, u32[]{:S(2)}) copy-start(f32[72,9]{1,0:T(8,128)} %constant.150.clone) | copy-start | bytes 7780
  41.1 23.4 %collective-permute-start.6 = (f32[9,48]{1,0:T(8,128)S(1)}, f32[9,48]{1,0:T(8,128)S(1)}, u32[]{:S(2)}, u32[]{:S(2)}) collective-permute-start(f32[9,48]{1,0:T(8,128)S(1)} %get-tuple-element.31), channel_id=1, source_target_pairs={{0,32},{64,96},{128,160},{192,224},{256,288},{320,352},{384,416},{... | collective-permute-start | bytes 5192 | tf_op jit(solution)/shard_map/ppermute | solution.py:101
  43.0 21.5 %collective-permute-start.7 = (f32[9,48]{1,0:T(8,128)S(1)}, f32[9,48]{1,0:T(8,128)S(1)}, u32[]{:S(2)}, u32[]{:S(2)}) collective-permute-start(f32[9,48]{1,0:T(8,128)S(1)} %get-tuple-element.32), channel_id=1, source_target_pairs={{32,64},{96,128},{160,192},{224,256},{288,320},{352,384},{416,448}... | collective-permute-start | bytes 5192 | tf_op jit(solution)/shard_map/ppermute | solution.py:104
  58.6 5.9 %collective-permute-start.4 = (f32[9,192]{1,0:T(8,128)S(1)}, f32[9,192]{1,0:T(8,128)S(1)}, u32[]{:S(2)}, u32[]{:S(2)}) collective-permute-start(f32[9,192]{1,0:T(8,128)S(1)} %get-tuple-element.23), channel_id=1, source_target_pairs={{0,1},{1,2},{2,3},{3,4},{4,5},{5,6},{6,7},{7,8},{8,9},{9,10},{10,1... | collective-permute-start | bytes 20744 | tf_op jit(solution)/shard_map/ppermute | solution.py:91
  62.6 4.5 %collective-permute-start.5 = (f32[9,192]{1,0:T(8,128)S(1)}, f32[9,192]{1,0:T(8,128)S(1)}, u32[]{:S(2)}, u32[]{:S(2)}) collective-permute-start(f32[9,192]{1,0:T(8,128)S(1)} %get-tuple-element.24), channel_id=1, source_target_pairs={{1,0},{2,1},{3,2},{4,3},{5,4},{6,5},{7,6},{8,7},{9,8},{10,9},{11,1... | collective-permute-start | bytes 20744 | tf_op jit(solution)/shard_map/ppermute | solution.py:91
  71.6 6.4 %collective-permute-start.8 = (f32[23,7,63]{2,1,0:T(8,128)S(1)}, f32[23,7,63]{2,1,0:T(8,128)S(1)}, u32[]{:S(2)}, u32[]{:S(2)}) collective-permute-start(f32[23,7,63]{2,1,0:T(8,128)S(1)} %slice.217), channel_id=1, source_target_pairs={{0,1},{1,0},{2,3},{3,2},{4,5},{5,4},{6,7},{7,6},{8,9},{9,8},{10,11... | collective-permute-start | bytes 121724 | tf_op jit(solution)/shard_map/ppermute | solution.py:217
  78.1 8.8 %collective-permute-start.9 = (f32[23,7,63]{2,1,0:T(8,128)S(1)}, f32[23,7,63]{2,1,0:T(8,128)S(1)}, u32[]{:S(2)}, u32[]{:S(2)}) collective-permute-start(f32[23,7,63]{2,1,0:T(8,128)S(1)} %slice_add_fusion), channel_id=1, source_target_pairs={{0,2},{1,3},{2,0},{3,1},{4,6},{5,7},{6,4},{7,5},{8,10},{9,11},{10,... | collective-permute-start | bytes 121724 | tf_op jit(solution)/shard_map/ppermute | solution.py:217
  86.9 5.3 %collective-permute-start.10 = (f32[23,7,63]{2,1,0:T(8,128)S(1)}, f32[23,7,63]{2,1,0:T(8,128)S(1)}, u32[]{:S(2)}, u32[]{:S(2)}) collective-permute-start(f32[23,7,63]{2,1,0:T(8,128)S(1)} %add.221), channel_id=1, source_target_pairs={{0,4},{1,5},{2,6},{3,7},{4,0},{5,1},{6,2},{7,3},{8,12},{9,13},{10,... | collective-permute-start | bytes 121724 | tf_op jit(solution)/shard_map/ppermute | solution.py:217
  90.3 23.2 %copy-start.32 = (f32[63]{0:T(128)S(1)}, f32[63]{0:T(128)}, u32[]{:S(2)}) copy-start(f32[63]{0:T(128)} %get-tuple-element.43) | copy-start | bytes 760
  90.3 23.2 %copy-start.33 = (f32[63]{0:T(128)S(1)}, f32[63]{0:T(128)}, u32[]{:S(2)}) copy-start(f32[63]{0:T(128)} %get-tuple-element.44) | copy-start | bytes 760
  92.3 8.9 %collective-permute-start.11 = (f32[23,7,63]{2,1,0:T(8,128)S(1)}, f32[23,7,63]{2,1,0:T(8,128)S(1)}, u32[]{:S(2)}, u32[]{:S(2)}) collective-permute-start(f32[23,7,63]{2,1,0:T(8,128)S(1)} %add.222), channel_id=1, source_target_pairs={{0,8},{1,9},{2,10},{3,11},{4,12},{5,13},{6,14},{7,15},{8,0},{9,1},... | collective-permute-start | bytes 121724 | tf_op jit(solution)/shard_map/ppermute | solution.py:217
  101.2 11.5 %collective-permute-start.12 = (f32[23,7,63]{2,1,0:T(8,128)S(1)}, f32[23,7,63]{2,1,0:T(8,128)S(1)}, u32[]{:S(2)}, u32[]{:S(2)}) collective-permute-start(f32[23,7,63]{2,1,0:T(8,128)S(1)} %add.223), channel_id=1, source_target_pairs={{0,16},{1,17},{2,18},{3,19},{4,20},{5,21},{6,22},{7,23},{8,24},{9,... | collective-permute-start | bytes 121724 | tf_op jit(solution)/shard_map/ppermute | solution.py:217
  118.6 15.5 %collective-permute-start.13 = (f32[9,48]{1,0:T(8,128)S(1)}, f32[9,48]{1,0:T(8,128)S(1)}, u32[]{:S(2)}, u32[]{:S(2)}) collective-permute-start(f32[9,48]{1,0:T(8,128)S(1)} %get-tuple-element.27), channel_id=1, source_target_pairs={{0,32},{64,96},{128,160},{192,224},{256,288},{320,352},{384,416},{... | collective-permute-start | bytes 5192 | tf_op jit(solution)/shard_map/ppermute | solution.py:101
  120.6 13.9 %collective-permute-start.14 = (f32[9,48]{1,0:T(8,128)S(1)}, f32[9,48]{1,0:T(8,128)S(1)}, u32[]{:S(2)}, u32[]{:S(2)}) collective-permute-start(f32[9,48]{1,0:T(8,128)S(1)} %get-tuple-element.28), channel_id=1, source_target_pairs={{32,64},{96,128},{160,192},{224,256},{288,320},{352,384},{416,448}... | collective-permute-start | bytes 5192 | tf_op jit(solution)/shard_map/ppermute | solution.py:104
  139.1 20.5 %collective-permute-start.17 = (f32[36,48]{1,0:T(8,128)S(1)}, f32[36,48]{1,0:T(8,128)S(1)}, u32[]{:S(2)}, u32[]{:S(2)}) collective-permute-start(f32[36,48]{1,0:T(8,128)S(1)} %get-tuple-element.17), channel_id=1, source_target_pairs={{0,32},{64,96},{128,160},{192,224},{256,288},{320,352},{384,416},{... | collective-permute-start | bytes 20744 | tf_op jit(solution)/shard_map/ppermute | solution.py:101
  141.0 18.5 %collective-permute-start.18 = (f32[36,48]{1,0:T(8,128)S(1)}, f32[36,48]{1,0:T(8,128)S(1)}, u32[]{:S(2)}, u32[]{:S(2)}) collective-permute-start(f32[36,48]{1,0:T(8,128)S(1)} %get-tuple-element.18), channel_id=1, source_target_pairs={{32,64},{96,128},{160,192},{224,256},{288,320},{352,384},{416,448}... | collective-permute-start | bytes 20744 | tf_op jit(solution)/shard_map/ppermute | solution.py:104
  154.4 5.2 %collective-permute-start.15 = (f32[36,192]{1,0:T(8,128)S(1)}, f32[36,192]{1,0:T(8,128)S(1)}, u32[]{:S(2)}, u32[]{:S(2)}) collective-permute-start(f32[36,192]{1,0:T(8,128)S(1)} %get-tuple-element.13), channel_id=1, source_target_pairs={{0,1},{1,2},{2,3},{3,4},{4,5},{5,6},{6,7},{7,8},{8,9},{9,10},{10,1... | collective-permute-start | bytes 82952 | tf_op jit(solution)/shard_map/ppermute | solution.py:91
  156.9 4.7 %collective-permute-start.16 = (f32[36,192]{1,0:T(8,128)S(1)}, f32[36,192]{1,0:T(8,128)S(1)}, u32[]{:S(2)}, u32[]{:S(2)}) collective-permute-start(f32[36,192]{1,0:T(8,128)S(1)} %get-tuple-element.14), channel_id=1, source_target_pairs={{1,0},{2,1},{3,2},{4,3},{5,4},{6,5},{7,6},{8,7},{9,8},{10,9},{11,1... | collective-permute-start | bytes 82952 | tf_op jit(solution)/shard_map/ppermute | solution.py:91
  (29 other events, 170.6 us)

commit v8 on v7

--- a/solution.py
+++ b/solution.py
@@ -20,7 +20,7 @@
 
 
 def mm(a, b):
-    return jnp.dot(a, b, precision=HIGHEST, preferred_element_type=jnp.float32)
+    return jnp.dot(a, b, precision=HIGH, preferred_element_type=jnp.float32)
 
 
 def pick(a, b):

time: 170 us -> 169 us (level)
    dot_general x15, matrix products: 7.6 us -> 5.88 us  [mm(): return jnp.dot(a, b, precision=HIGH, preferred_element_type=jnp.float32)]
where the time goes in v8:
time: 169 us; the launch traced here: 166 us
  starting transfers between devices  103 us (61%)
  matrix products  24.8 us (15%)
  waiting for transfers between devices  20.7 us (12%)
  local copies, waits for them, and re-layouts  13.5 us (8%)
  other arithmetic  2.59 us (2%)
    ppermute x4, starting transfers between devices, region_exchange(): lax.ppermute(jnp.where(odd, region_out[1], region_out[0]), 'region', far_...  43.1 us
    ppermute x5, starting transfers between devices, gather_slab(): interior = interior + lax.ppermute(interior, 'group', partner)  24.2 us
    ppermute x4, starting transfers between devices, region_exchange(): lax.ppermute(jnp.where(odd, region_out[0], region_out[1]), 'region', near...  21.8 us
    ppermute x5, waiting for transfers between devices, gather_slab(): interior = interior + lax.ppermute(interior, 'group', partner)  15 us
    ppermute x6, starting transfers between devices, shift(): return lax.ppermute(block, axis, pairs)  13.5 us
    dot_general x4, matrix products, apply_level(): jnp.einsum('fnq,fqe->fne', source, gather.astype(jnp.float32), precision=...  8.57 us
    unnamed x69, local copies, waits for them, and re-layouts  6.2 us
    dot_general x15, matrix products, mm(): return jnp.dot(a, b, precision=HIGH, preferred_element_type=jnp.float32)  5.88 us
  transfers between devices with their start and end apart: 19, of which 9 were waited for; matrix products, arithmetic and copies ran while one was open for 6% of the time, Pallas kernels for 0%

profile of v8, /device:TPU:1, one launch (start us, length us, event | category | flops | bytes accessed | tf_op | source)
XLA Modules:
  0.0 165.7 jit_solution(11907884484306783290)
XLA Ops:
  3.8 16.1 %collective-permute-start.2 = (f32[36,48]{1,0:T(8,128)S(1)}, f32[36,48]{1,0:T(8,128)S(1)}, u32[]{:S(2)}, u32[]{:S(2)}) collective-permute-start(f32[36,48]{1,0:T(8,128)S(1)} %get-tuple-element.21), channel_id=1, source_target_pairs={{0,32},{64,96},{128,160},{192,224},{256,288},{320,352},{384,416},{... | collective-permute-start | bytes 20744 | tf_op jit(solution)/shard_map/ppermute | solution.py:101
  19.8 2.7 %collective-permute-start.3 = (f32[36,48]{1,0:T(8,128)S(1)}, f32[36,48]{1,0:T(8,128)S(1)}, u32[]{:S(2)}, u32[]{:S(2)}) collective-permute-start(f32[36,48]{1,0:T(8,128)S(1)} %get-tuple-element.22), channel_id=1, source_target_pairs={{32,64},{96,128},{160,192},{224,256},{288,320},{352,384},{416,448}... | collective-permute-start | bytes 20744 | tf_op jit(solution)/shard_map/ppermute | solution.py:104
  23.6 3.2 %collective-permute-start = (f32[44,192]{1,0:T(8,128)S(1)}, f32[44,192]{1,0:T(8,128)S(1)}, u32[]{:S(2)}, u32[]{:S(2)}) collective-permute-start(f32[44,192]{1,0:T(8,128)S(1)} %get-tuple-element.11), channel_id=1, source_target_pairs={{0,1},{1,2},{2,3},{3,4},{4,5},{5,6},{6,7},{7,8},{8,9},{9,10},{10,1... | collective-permute-start | bytes 101384 | tf_op jit(solution)/shard_map/ppermute | solution.py:91
  35.3 2.2 %fusion.12 = f32[6,36,384]{2,1,0:T(8,128)S(1)} fusion(f32[6,36,384]{2,1,0:T(8,128)S(1)} %reshape.335, s32[6,384]{1,0:T(8,128)S(1)} %bitcast.129, f32[6,36,480]{2,1,0:T(8,128)S(1)} %broadcast_in_dim.19, f32[6,36,384]{2,1,0:T(8,128)S(1)} %copy-done.8), kind=kOutput, calls=%fused_computation.21 | convolution fusion | flops 432241920 | bytes 1419264 | tf_op jit(solution)/shard_map/fnq,fqe->fne/dot_general | solution.py:145
  42.2 15.1 %collective-permute-start.7 = (f32[9,48]{1,0:T(8,128)S(1)}, f32[9,48]{1,0:T(8,128)S(1)}, u32[]{:S(2)}, u32[]{:S(2)}) collective-permute-start(f32[9,48]{1,0:T(8,128)S(1)} %get-tuple-element.32), channel_id=1, source_target_pairs={{32,64},{96,128},{160,192},{224,256},{288,320},{352,384},{416,448}... | collective-permute-start | bytes 5192 | tf_op jit(solution)/shard_map/ppermute | solution.py:104
  57.8 4.0 %collective-permute-start.4 = (f32[9,192]{1,0:T(8,128)S(1)}, f32[9,192]{1,0:T(8,128)S(1)}, u32[]{:S(2)}, u32[]{:S(2)}) collective-permute-start(f32[9,192]{1,0:T(8,128)S(1)} %get-tuple-element.23), channel_id=1, source_target_pairs={{0,1},{1,2},{2,3},{3,4},{4,5},{5,6},{6,7},{7,8},{8,9},{9,10},{10,1... | collective-permute-start | bytes 20744 | tf_op jit(solution)/shard_map/ppermute | solution.py:91
  63.7 2.5 %collective-permute-done.5 = f32[9,192]{1,0:T(8,128)S(1)} collective-permute-done((f32[9,192]{1,0:T(8,128)S(1)}, f32[9,192]{1,0:T(8,128)S(1)}, u32[]{:S(2)}, u32[]{:S(2)}) %collective-permute-start.5) | collective-permute-done | bytes 6944 | tf_op jit(solution)/shard_map/ppermute | solution.py:91
  66.7 2.1 %fusion.18 = f32[6,9,384]{2,1,0:T(8,128)S(1)} fusion(f32[6,9,384]{2,1,0:T(8,128)S(1)} %reshape.339, s32[6,384]{1,0:T(8,128)S(1)} %bitcast.130, f32[6,9,480]{2,1,0:T(8,128)S(1)} %broadcast_in_dim.22, f32[6,9,384]{2,1,0:T(8,128)S(1)} %gather_fusion.1), kind=kOutput, calls=%fused_computation.31 | convolution fusion | flops 109553472 | bytes 361728 | tf_op jit(solution)/shard_map/fnq,fqe->fne/dot_general | solution.py:145
  70.8 3.4 %collective-permute-start.8 = (f32[23,7,63]{2,1,0:T(8,128)S(1)}, f32[23,7,63]{2,1,0:T(8,128)S(1)}, u32[]{:S(2)}, u32[]{:S(2)}) collective-permute-start(f32[23,7,63]{2,1,0:T(8,128)S(1)} %slice.217), channel_id=1, source_target_pairs={{0,1},{1,0},{2,3},{3,2},{4,5},{5,4},{6,7},{7,6},{8,9},{9,8},{10,11... | collective-permute-start | bytes 121724 | tf_op jit(solution)/shard_map/ppermute | solution.py:217
  74.3 2.9 %collective-permute-done.8 = f32[23,7,63]{2,1,0:T(8,128)S(1)} collective-permute-done((f32[23,7,63]{2,1,0:T(8,128)S(1)}, f32[23,7,63]{2,1,0:T(8,128)S(1)}, u32[]{:S(2)}, u32[]{:S(2)}) %collective-permute-start.8) | collective-permute-done | bytes 40604 | tf_op jit(solution)/shard_map/ppermute | solution.py:217
  77.3 6.9 %collective-permute-start.9 = (f32[23,7,63]{2,1,0:T(8,128)S(1)}, f32[23,7,63]{2,1,0:T(8,128)S(1)}, u32[]{:S(2)}, u32[]{:S(2)}) collective-permute-start(f32[23,7,63]{2,1,0:T(8,128)S(1)} %slice_add_fusion), channel_id=1, source_target_pairs={{0,2},{1,3},{2,0},{3,1},{4,6},{5,7},{6,4},{7,5},{8,10},{9,11},{10,... | collective-permute-start | bytes 121724 | tf_op jit(solution)/shard_map/ppermute | solution.py:217
  84.2 1.9 %collective-permute-done.9 = f32[23,7,63]{2,1,0:T(8,128)S(1)} collective-permute-done((f32[23,7,63]{2,1,0:T(8,128)S(1)}, f32[23,7,63]{2,1,0:T(8,128)S(1)}, u32[]{:S(2)}, u32[]{:S(2)}) %collective-permute-start.9) | collective-permute-done | bytes 40604 | tf_op jit(solution)/shard_map/ppermute | solution.py:217
  86.1 2.6 %collective-permute-start.10 = (f32[23,7,63]{2,1,0:T(8,128)S(1)}, f32[23,7,63]{2,1,0:T(8,128)S(1)}, u32[]{:S(2)}, u32[]{:S(2)}) collective-permute-start(f32[23,7,63]{2,1,0:T(8,128)S(1)} %add.221), channel_id=1, source_target_pairs={{0,4},{1,5},{2,6},{3,7},{4,0},{5,1},{6,2},{7,3},{8,12},{9,13},{10,... | collective-permute-start | bytes 121724 | tf_op jit(solution)/shard_map/ppermute | solution.py:217
  91.5 6.0 %collective-permute-start.11 = (f32[23,7,63]{2,1,0:T(8,128)S(1)}, f32[23,7,63]{2,1,0:T(8,128)S(1)}, u32[]{:S(2)}, u32[]{:S(2)}) collective-permute-start(f32[23,7,63]{2,1,0:T(8,128)S(1)} %add.222), channel_id=1, source_target_pairs={{0,8},{1,9},{2,10},{3,11},{4,12},{5,13},{6,14},{7,15},{8,0},{9,1},... | collective-permute-start | bytes 121724 | tf_op jit(solution)/shard_map/ppermute | solution.py:217
  97.5 2.9 %collective-permute-done.11 = f32[23,7,63]{2,1,0:T(8,128)S(1)} collective-permute-done((f32[23,7,63]{2,1,0:T(8,128)S(1)}, f32[23,7,63]{2,1,0:T(8,128)S(1)}, u32[]{:S(2)}, u32[]{:S(2)}) %collective-permute-start.11) | collective-permute-done | bytes 40604 | tf_op jit(solution)/shard_map/ppermute | solution.py:217
  100.4 5.3 %collective-permute-start.12 = (f32[23,7,63]{2,1,0:T(8,128)S(1)}, f32[23,7,63]{2,1,0:T(8,128)S(1)}, u32[]{:S(2)}, u32[]{:S(2)}) collective-permute-start(f32[23,7,63]{2,1,0:T(8,128)S(1)} %add.223), channel_id=1, source_target_pairs={{0,16},{1,17},{2,18},{3,19},{4,20},{5,21},{6,22},{7,23},{8,24},{9,... | collective-permute-start | bytes 121724 | tf_op jit(solution)/shard_map/ppermute | solution.py:217
  105.8 6.1 %collective-permute-done.12 = f32[23,7,63]{2,1,0:T(8,128)S(1)} collective-permute-done((f32[23,7,63]{2,1,0:T(8,128)S(1)}, f32[23,7,63]{2,1,0:T(8,128)S(1)}, u32[]{:S(2)}, u32[]{:S(2)}) %collective-permute-start.12) | collective-permute-done | bytes 40604 | tf_op jit(solution)/shard_map/ppermute | solution.py:217
  117.7 1.9 %collective-permute-start.13 = (f32[9,48]{1,0:T(8,128)S(1)}, f32[9,48]{1,0:T(8,128)S(1)}, u32[]{:S(2)}, u32[]{:S(2)}) collective-permute-start(f32[9,48]{1,0:T(8,128)S(1)} %get-tuple-element.27), channel_id=1, source_target_pairs={{0,32},{64,96},{128,160},{192,224},{256,288},{320,352},{384,416},{... | collective-permute-start | bytes 5192 | tf_op jit(solution)/shard_map/ppermute | solution.py:101
  119.6 12.5 %collective-permute-start.14 = (f32[9,48]{1,0:T(8,128)S(1)}, f32[9,48]{1,0:T(8,128)S(1)}, u32[]{:S(2)}, u32[]{:S(2)}) collective-permute-start(f32[9,48]{1,0:T(8,128)S(1)} %get-tuple-element.28), channel_id=1, source_target_pairs={{32,64},{96,128},{160,192},{224,256},{288,320},{352,384},{416,448}... | collective-permute-start | bytes 5192 | tf_op jit(solution)/shard_map/ppermute | solution.py:104
  133.9 2.1 %fusion.19 = f32[6,9,384]{2,1,0:T(8,128)S(1)} fusion(f32[6,9,384]{2,1,0:T(8,128)S(1)} %reshape.345, s32[6,384]{1,0:T(8,128)S(1)} %bitcast.131, f32[6,9,480]{2,1,0:T(8,128)S(1)} %broadcast_in_dim.24, f32[6,9,384]{2,1,0:T(8,128)S(1)} %gather_fusion.2), kind=kOutput, calls=%fused_computation.32 | convolution fusion | flops 109553472 | bytes 361728 | tf_op jit(solution)/shard_map/fnq,fqe->fne/dot_general | solution.py:145
  139.7 12.8 %collective-permute-start.18 = (f32[36,48]{1,0:T(8,128)S(1)}, f32[36,48]{1,0:T(8,128)S(1)}, u32[]{:S(2)}, u32[]{:S(2)}) collective-permute-start(f32[36,48]{1,0:T(8,128)S(1)} %get-tuple-element.18), channel_id=1, source_target_pairs={{32,64},{96,128},{160,192},{224,256},{288,320},{352,384},{416,448}... | collective-permute-start | bytes 20744 | tf_op jit(solution)/shard_map/ppermute | solution.py:104
  153.1 2.5 %collective-permute-start.15 = (f32[36,192]{1,0:T(8,128)S(1)}, f32[36,192]{1,0:T(8,128)S(1)}, u32[]{:S(2)}, u32[]{:S(2)}) collective-permute-start(f32[36,192]{1,0:T(8,128)S(1)} %get-tuple-element.13), channel_id=1, source_target_pairs={{0,1},{1,2},{2,3},{3,4},{4,5},{5,6},{6,7},{7,8},{8,9},{9,10},{10,1... | collective-permute-start | bytes 82952 | tf_op jit(solution)/shard_map/ppermute | solution.py:91
  158.2 2.0 %collective-permute-done.16 = f32[36,192]{1,0:T(8,128)S(1)} collective-permute-done((f32[36,192]{1,0:T(8,128)S(1)}, f32[36,192]{1,0:T(8,128)S(1)}, u32[]{:S(2)}, u32[]{:S(2)}) %collective-permute-start.16) | collective-permute-done | bytes 27680 | tf_op jit(solution)/shard_map/ppermute | solution.py:91
  161.9 2.2 %fusion.13 = f32[6,36,384]{2,1,0:T(8,128)S(1)} fusion(f32[6,36,384]{2,1,0:T(8,128)S(1)} %copy-done.4, s32[6,384]{1,0:T(8,128)S(1)} %bitcast.132, f32[6,36,480]{2,1,0:T(8,128)S(1)} %broadcast_in_dim.26, f32[6,36,384]{2,1,0:T(8,128)S(1)} %copy-done.9), kind=kOutput, calls=%fused_computation.22 | convolution fusion | flops 432241920 | bytes 1419264 | tf_op jit(solution)/shard_map/fnq,fqe->fne/dot_general | solution.py:145
  (210 shorter events, 42.3 us)
Async XLA Ops:
  2.8 25.4 %copy-start.27 = (s32[1,480]{1,0:T(1,128)S(1)}, s32[1,480]{1,0:T(1,128)}, u32[]{:S(2)}) copy-start(s32[1,480]{1,0:T(1,128)} %param.40) | copy-start | bytes 5764
  2.9 25.4 %copy-start.28 = (s32[6]{0:T(128)S(1)}, s32[6]{0:T(128)}, u32[]{:S(2)}) copy-start(s32[6]{0:T(128)} %constant.162) | copy-start | bytes 76
  3.8 29.2 %collective-permute-start.2 = (f32[36,48]{1,0:T(8,128)S(1)}, f32[36,48]{1,0:T(8,128)S(1)}, u32[]{:S(2)}, u32[]{:S(2)}) collective-permute-start(f32[36,48]{1,0:T(8,128)S(1)} %get-tuple-element.21), channel_id=1, source_target_pairs={{0,32},{64,96},{128,160},{192,224},{256,288},{320,352},{384,416},{... | collective-permute-start | bytes 20744 | tf_op jit(solution)/shard_map/ppermute | solution.py:101
  19.8 13.8 %collective-permute-start.3 = (f32[36,48]{1,0:T(8,128)S(1)}, f32[36,48]{1,0:T(8,128)S(1)}, u32[]{:S(2)}, u32[]{:S(2)}) collective-permute-start(f32[36,48]{1,0:T(8,128)S(1)} %get-tuple-element.22), channel_id=1, source_target_pairs={{32,64},{96,128},{160,192},{224,256},{288,320},{352,384},{416,448}... | collective-permute-start | bytes 20744 | tf_op jit(solution)/shard_map/ppermute | solution.py:104
  23.6 10.1 %collective-permute-start = (f32[44,192]{1,0:T(8,128)S(1)}, f32[44,192]{1,0:T(8,128)S(1)}, u32[]{:S(2)}, u32[]{:S(2)}) collective-permute-start(f32[44,192]{1,0:T(8,128)S(1)} %get-tuple-element.11), channel_id=1, source_target_pairs={{0,1},{1,2},{2,3},{3,4},{4,5},{5,6},{6,7},{7,8},{8,9},{9,10},{10,1... | collective-permute-start | bytes 101384 | tf_op jit(solution)/shard_map/ppermute | solution.py:91
  26.8 6.9 %collective-permute-start.1 = (f32[44,192]{1,0:T(8,128)S(1)}, f32[44,192]{1,0:T(8,128)S(1)}, u32[]{:S(2)}, u32[]{:S(2)}) collective-permute-start(f32[44,192]{1,0:T(8,128)S(1)} %get-tuple-element.12), channel_id=1, source_target_pairs={{1,0},{2,1},{3,2},{4,3},{5,4},{6,5},{7,6},{8,7},{9,8},{10,9},{11,1... | collective-permute-start | bytes 101384 | tf_op jit(solution)/shard_map/ppermute | solution.py:91
  40.0 26.3 %copy-start.11 = (f32[72,9]{1,0:T(8,128)S(1)}, f32[72,9]{1,0:T(8,128)}, u32[]{:S(2)}) copy-start(f32[72,9]{1,0:T(8,128)} %constant.150.clone) | copy-start | bytes 7780
  40.3 23.4 %collective-permute-start.6 = (f32[9,48]{1,0:T(8,128)S(1)}, f32[9,48]{1,0:T(8,128)S(1)}, u32[]{:S(2)}, u32[]{:S(2)}) collective-permute-start(f32[9,48]{1,0:T(8,128)S(1)} %get-tuple-element.31), channel_id=1, source_target_pairs={{0,32},{64,96},{128,160},{192,224},{256,288},{320,352},{384,416},{... | collective-permute-start | bytes 5192 | tf_op jit(solution)/shard_map/ppermute | solution.py:101
  42.2 21.5 %collective-permute-start.7 = (f32[9,48]{1,0:T(8,128)S(1)}, f32[9,48]{1,0:T(8,128)S(1)}, u32[]{:S(2)}, u32[]{:S(2)}) collective-permute-start(f32[9,48]{1,0:T(8,128)S(1)} %get-tuple-element.32), channel_id=1, source_target_pairs={{32,64},{96,128},{160,192},{224,256},{288,320},{352,384},{416,448}... | collective-permute-start | bytes 5192 | tf_op jit(solution)/shard_map/ppermute | solution.py:104
  57.8 5.9 %collective-permute-start.4 = (f32[9,192]{1,0:T(8,128)S(1)}, f32[9,192]{1,0:T(8,128)S(1)}, u32[]{:S(2)}, u32[]{:S(2)}) collective-permute-start(f32[9,192]{1,0:T(8,128)S(1)} %get-tuple-element.23), channel_id=1, source_target_pairs={{0,1},{1,2},{2,3},{3,4},{4,5},{5,6},{6,7},{7,8},{8,9},{9,10},{10,1... | collective-permute-start | bytes 20744 | tf_op jit(solution)/shard_map/ppermute | solution.py:91
  61.8 4.5 %collective-permute-start.5 = (f32[9,192]{1,0:T(8,128)S(1)}, f32[9,192]{1,0:T(8,128)S(1)}, u32[]{:S(2)}, u32[]{:S(2)}) collective-permute-start(f32[9,192]{1,0:T(8,128)S(1)} %get-tuple-element.24), channel_id=1, source_target_pairs={{1,0},{2,1},{3,2},{4,3},{5,4},{6,5},{7,6},{8,7},{9,8},{10,9},{11,1... | collective-permute-start | bytes 20744 | tf_op jit(solution)/shard_map/ppermute | solution.py:91
  70.8 6.4 %collective-permute-start.8 = (f32[23,7,63]{2,1,0:T(8,128)S(1)}, f32[23,7,63]{2,1,0:T(8,128)S(1)}, u32[]{:S(2)}, u32[]{:S(2)}) collective-permute-start(f32[23,7,63]{2,1,0:T(8,128)S(1)} %slice.217), channel_id=1, source_target_pairs={{0,1},{1,0},{2,3},{3,2},{4,5},{5,4},{6,7},{7,6},{8,9},{9,8},{10,11... | collective-permute-start | bytes 121724 | tf_op jit(solution)/shard_map/ppermute | solution.py:217
  77.3 8.8 %collective-permute-start.9 = (f32[23,7,63]{2,1,0:T(8,128)S(1)}, f32[23,7,63]{2,1,0:T(8,128)S(1)}, u32[]{:S(2)}, u32[]{:S(2)}) collective-permute-start(f32[23,7,63]{2,1,0:T(8,128)S(1)} %slice_add_fusion), channel_id=1, source_target_pairs={{0,2},{1,3},{2,0},{3,1},{4,6},{5,7},{6,4},{7,5},{8,10},{9,11},{10,... | collective-permute-start | bytes 121724 | tf_op jit(solution)/shard_map/ppermute | solution.py:217
  86.1 5.3 %collective-permute-start.10 = (f32[23,7,63]{2,1,0:T(8,128)S(1)}, f32[23,7,63]{2,1,0:T(8,128)S(1)}, u32[]{:S(2)}, u32[]{:S(2)}) collective-permute-start(f32[23,7,63]{2,1,0:T(8,128)S(1)} %add.221), channel_id=1, source_target_pairs={{0,4},{1,5},{2,6},{3,7},{4,0},{5,1},{6,2},{7,3},{8,12},{9,13},{10,... | collective-permute-start | bytes 121724 | tf_op jit(solution)/shard_map/ppermute | solution.py:217
  89.5 23.2 %copy-start.32 = (f32[63]{0:T(128)S(1)}, f32[63]{0:T(128)}, u32[]{:S(2)}) copy-start(f32[63]{0:T(128)} %get-tuple-element.43) | copy-start | bytes 760
  89.5 23.2 %copy-start.33 = (f32[63]{0:T(128)S(1)}, f32[63]{0:T(128)}, u32[]{:S(2)}) copy-start(f32[63]{0:T(128)} %get-tuple-element.44) | copy-start | bytes 760
  91.5 8.9 %collective-permute-start.11 = (f32[23,7,63]{2,1,0:T(8,128)S(1)}, f32[23,7,63]{2,1,0:T(8,128)S(1)}, u32[]{:S(2)}, u32[]{:S(2)}) collective-permute-start(f32[23,7,63]{2,1,0:T(8,128)S(1)} %add.222), channel_id=1, source_target_pairs={{0,8},{1,9},{2,10},{3,11},{4,12},{5,13},{6,14},{7,15},{8,0},{9,1},... | collective-permute-start | bytes 121724 | tf_op jit(solution)/shard_map/ppermute | solution.py:217
  100.4 11.5 %collective-permute-start.12 = (f32[23,7,63]{2,1,0:T(8,128)S(1)}, f32[23,7,63]{2,1,0:T(8,128)S(1)}, u32[]{:S(2)}, u32[]{:S(2)}) collective-permute-start(f32[23,7,63]{2,1,0:T(8,128)S(1)} %add.223), channel_id=1, source_target_pairs={{0,16},{1,17},{2,18},{3,19},{4,20},{5,21},{6,22},{7,23},{8,24},{9,... | collective-permute-start | bytes 121724 | tf_op jit(solution)/shard_map/ppermute | solution.py:217
  117.7 15.4 %collective-permute-start.13 = (f32[9,48]{1,0:T(8,128)S(1)}, f32[9,48]{1,0:T(8,128)S(1)}, u32[]{:S(2)}, u32[]{:S(2)}) collective-permute-start(f32[9,48]{1,0:T(8,128)S(1)} %get-tuple-element.27), channel_id=1, source_target_pairs={{0,32},{64,96},{128,160},{192,224},{256,288},{320,352},{384,416},{... | collective-permute-start | bytes 5192 | tf_op jit(solution)/shard_map/ppermute | solution.py:101
  119.6 13.9 %collective-permute-start.14 = (f32[9,48]{1,0:T(8,128)S(1)}, f32[9,48]{1,0:T(8,128)S(1)}, u32[]{:S(2)}, u32[]{:S(2)}) collective-permute-start(f32[9,48]{1,0:T(8,128)S(1)} %get-tuple-element.28), channel_id=1, source_target_pairs={{32,64},{96,128},{160,192},{224,256},{288,320},{352,384},{416,448}... | collective-permute-start | bytes 5192 | tf_op jit(solution)/shard_map/ppermute | solution.py:104
  137.7 20.5 %collective-permute-start.17 = (f32[36,48]{1,0:T(8,128)S(1)}, f32[36,48]{1,0:T(8,128)S(1)}, u32[]{:S(2)}, u32[]{:S(2)}) collective-permute-start(f32[36,48]{1,0:T(8,128)S(1)} %get-tuple-element.17), channel_id=1, source_target_pairs={{0,32},{64,96},{128,160},{192,224},{256,288},{320,352},{384,416},{... | collective-permute-start | bytes 20744 | tf_op jit(solution)/shard_map/ppermute | solution.py:101
  139.7 18.6 %collective-permute-start.18 = (f32[36,48]{1,0:T(8,128)S(1)}, f32[36,48]{1,0:T(8,128)S(1)}, u32[]{:S(2)}, u32[]{:S(2)}) collective-permute-start(f32[36,48]{1,0:T(8,128)S(1)} %get-tuple-element.18), channel_id=1, source_target_pairs={{32,64},{96,128},{160,192},{224,256},{288,320},{352,384},{416,448}... | collective-permute-start | bytes 20744 | tf_op jit(solution)/shard_map/ppermute | solution.py:104
  153.1 5.2 %collective-permute-start.15 = (f32[36,192]{1,0:T(8,128)S(1)}, f32[36,192]{1,0:T(8,128)S(1)}, u32[]{:S(2)}, u32[]{:S(2)}) collective-permute-start(f32[36,192]{1,0:T(8,128)S(1)} %get-tuple-element.13), channel_id=1, source_target_pairs={{0,1},{1,2},{2,3},{3,4},{4,5},{5,6},{6,7},{7,8},{8,9},{9,10},{10,1... | collective-permute-start | bytes 82952 | tf_op jit(solution)/shard_map/ppermute | solution.py:91
  155.5 4.8 %collective-permute-start.16 = (f32[36,192]{1,0:T(8,128)S(1)}, f32[36,192]{1,0:T(8,128)S(1)}, u32[]{:S(2)}, u32[]{:S(2)}) collective-permute-start(f32[36,192]{1,0:T(8,128)S(1)} %get-tuple-element.14), channel_id=1, source_target_pairs={{1,0},{2,1},{3,2},{4,3},{5,4},{6,5},{7,6},{8,7},{9,8},{10,9},{11,1... | collective-permute-start | bytes 82952 | tf_op jit(solution)/shard_map/ppermute | solution.py:91
  (29 other events, 169.1 us)

commit v9 on v7

--- a/solution.py
+++ b/solution.py
@@ -107,7 +107,7 @@
     return jnp.where(odd, near_recv, far_recv), jnp.where(odd, far_recv, near_recv)
 
 
-def apply_level(current, stiffness, points, tables, extra=None, group_ghosts=None):
+def apply_level(current, stiffness, points, tables, extra=None, group_ghosts=None, sends=None):
     gather, pick_group, pick_region, codes = tables
     plane = points * points
     cube = points**3
@@ -116,17 +116,22 @@
     both = mm(jnp.concatenate([stiffness, select], axis=0), current)
     product = both[:cube]
     traces = both[cube:].reshape(6, plane, elements)
-    region_out = jnp.einsum(
-        "snj,sjk->snk", traces[2:4], pick_region, precision=HIGH,
-        preferred_element_type=jnp.float32,
-    )
+    if sends is None:
+        sends = (
+            jnp.einsum(
+                "snj,sjk->snk", traces[0:2], pick_group, precision=HIGH,
+                preferred_element_type=jnp.float32,
+            ),
+            jnp.einsum(
+                "snj,sjk->snk", traces[2:4], pick_region, precision=HIGH,
+                preferred_element_type=jnp.float32,
+            ),
+        )
+    region_out = sends[1]
     from_region_low, from_region_high = region_exchange(region_out)
     received = None
     if group_ghosts is None:
-        group_out = jnp.einsum(
-            "snj,sjk->snk", traces[0:2], pick_group, precision=HIGH,
-            preferred_element_type=jnp.float32,
-        )
+        group_out = sends[0]
         if extra is not None:
             group_out = jnp.concatenate([group_out, extra], axis=1)
         from_group_low = shift(group_out[1], "group", 1)
@@ -243,8 +248,22 @@
         preferred_element_type=jnp.float32,
     )
 
+    face_smooth = mm(jnp.asarray(trace_matrix(FINE_PTS)), smooth_fine).reshape(6, -1, smooth_fine.shape[1])
+    first_sends = tuple(
+        jnp.einsum(
+            "snj,sjk->snk",
+            face_smooth[faces],
+            jnp.einsum("jq,sqk->sjk", right_side, chosen, precision=HIGH,
+                       preferred_element_type=jnp.float32),
+            precision=HIGHEST,
+            preferred_element_type=jnp.float32,
+        )
+        for faces, chosen in ((slice(0, 2), tables[1]), (slice(2, 4), tables[2]))
+    )
     smoothed = mm(smooth_fine, right_side)
-    operated, received = apply_level(smoothed, stiff_fine, FINE_PTS, tables, extra=sent_ids)
+    operated, received = apply_level(
+        smoothed, stiff_fine, FINE_PTS, tables, extra=sent_ids, sends=first_sends
+    )
     residual = right_side - operated
     neighbor_ids = jnp.round(jnp.concatenate(received, axis=1)).astype(jnp.int32)
     middle_rhs = mm(restrict_fine, residual)

time: 170 us -> 174 us (1.024)
  matrix products: 26.5 us -> 29 us
    reshape x4, local copies, waits for them, and re-layouts: 0.11 us -> 2.08 us  [apply_level(): jumps = (traces - outside).reshape(6 * plane, elements)]
    unnamed x69 -> x67, local copies, waits for them, and re-layouts: 6.01 us -> 4.91 us
    dot_general x15 -> x16, matrix products: 7.6 us -> 7.9 us  [mm(): return jnp.dot(a, b, precision=HIGHEST, preferred_element_type=jnp.float32)]
  transfers between devices with their start and end apart: 19 -> 19, of which waited for: 9 -> 8; matrix products, arithmetic and copies ran while one was open for 6% -> 7% of each run, Pallas kernels for 0% -> 0%
where the time goes in v9:
time: 174 us; the launch traced here: 171 us
  starting transfers between devices  104 us (60%)
  matrix products  29 us (17%)
  waiting for transfers between devices  19.9 us (11%)
  local copies, waits for them, and re-layouts  14.1 us (8%)
  other arithmetic  2.53 us (1%)
    ppermute x4, starting transfers between devices, region_exchange(): lax.ppermute(jnp.where(odd, region_out[1], region_out[0]), 'region', far_...  43.9 us
    ppermute x5, starting transfers between devices, gather_slab(): interior = interior + lax.ppermute(interior, 'group', partner)  24.2 us
    ppermute x4, starting transfers between devices, region_exchange(): lax.ppermute(jnp.where(odd, region_out[0], region_out[1]), 'region', near...  21.8 us
    ppermute x5, waiting for transfers between devices, gather_slab(): interior = interior + lax.ppermute(interior, 'group', partner)  15.2 us
    ppermute x6, starting transfers between devices, shift(): return lax.ppermute(block, axis, pairs)  13.9 us
    dot_general x4, matrix products, apply_level(): jnp.einsum('fnq,fqe->fne', source, gather.astype(jnp.float32), precision=...  10.1 us
    dot_general x16, matrix products, mm(): return jnp.dot(a, b, precision=HIGHEST, preferred_element_type=jnp.float32)  7.9 us
    dot_general x11, matrix products, pick(): return jnp.dot(a, b, precision=HIGH, preferred_element_type=jnp.float32)  5.18 us
  transfers between devices with their start and end apart: 19, of which 8 were waited for; matrix products, arithmetic and copies ran while one was open for 7% of the time, Pallas kernels for 0%

profile of v9, /device:TPU:1, one launch (start us, length us, event | category | flops | bytes accessed | tf_op | source)
XLA Modules:
  0.0 170.9 jit_solution(7098674518747622923)
XLA Ops:
  2.8 16.1 %collective-permute-start.2 = (f32[36,48]{1,0:T(8,128)S(1)}, f32[36,48]{1,0:T(8,128)S(1)}, u32[]{:S(2)}, u32[]{:S(2)}) collective-permute-start(f32[36,48]{1,0:T(8,128)S(1)} %get-tuple-element.21), channel_id=1, source_target_pairs={{0,32},{64,96},{128,160},{192,224},{256,288},{320,352},{384,416},{... | collective-permute-start | bytes 20744 | tf_op jit(solution)/shard_map/ppermute | solution.py:101
  18.9 2.7 %collective-permute-start.3 = (f32[36,48]{1,0:T(8,128)S(1)}, f32[36,48]{1,0:T(8,128)S(1)}, u32[]{:S(2)}, u32[]{:S(2)}) collective-permute-start(f32[36,48]{1,0:T(8,128)S(1)} %get-tuple-element.22), channel_id=1, source_target_pairs={{32,64},{96,128},{160,192},{224,256},{288,320},{352,384},{416,448}... | collective-permute-start | bytes 20744 | tf_op jit(solution)/shard_map/ppermute | solution.py:104
  23.1 3.3 %collective-permute-start = (f32[44,192]{1,0:T(8,128)S(1)}, f32[44,192]{1,0:T(8,128)S(1)}, u32[]{:S(2)}, u32[]{:S(2)}) collective-permute-start(f32[44,192]{1,0:T(8,128)S(1)} %get-tuple-element.11), channel_id=1, source_target_pairs={{0,1},{1,2},{2,3},{3,4},{4,5},{5,6},{6,7},{7,8},{8,9},{9,10},{10,1... | collective-permute-start | bytes 101384 | tf_op jit(solution)/shard_map/ppermute | solution.py:91
  36.2 2.9 %fusion.12 = f32[6,36,384]{2,1,0:T(8,128)} fusion(f32[6,36,384]{2,1,0:T(8,128)S(1)} %reshape.336, s32[6,384]{1,0:T(8,128)S(1)} %bitcast.142, f32[6,36,480]{2,1,0:T(8,128)S(1)} %broadcast_in_dim.19, f32[6,36,384]{2,1,0:T(8,128)S(1)} %copy-done.6), kind=kOutput, calls=%fused_computation.21 | convolution fusion | flops 432241920 | bytes 1419264 | tf_op jit(solution)/shard_map/fnq,fqe->fne/dot_general | solution.py:150
  42.2 1.9 %collective-permute-start.6 = (f32[9,48]{1,0:T(8,128)S(1)}, f32[9,48]{1,0:T(8,128)S(1)}, u32[]{:S(2)}, u32[]{:S(2)}) collective-permute-start(f32[9,48]{1,0:T(8,128)S(1)} %get-tuple-element.31), channel_id=1, source_target_pairs={{0,32},{64,96},{128,160},{192,224},{256,288},{320,352},{384,416},{... | collective-permute-start | bytes 5192 | tf_op jit(solution)/shard_map/ppermute | solution.py:101
  44.1 15.8 %collective-permute-start.7 = (f32[9,48]{1,0:T(8,128)S(1)}, f32[9,48]{1,0:T(8,128)S(1)}, u32[]{:S(2)}, u32[]{:S(2)}) collective-permute-start(f32[9,48]{1,0:T(8,128)S(1)} %get-tuple-element.32), channel_id=1, source_target_pairs={{32,64},{96,128},{160,192},{224,256},{288,320},{352,384},{416,448}... | collective-permute-start | bytes 5192 | tf_op jit(solution)/shard_map/ppermute | solution.py:104
  60.5 4.0 %collective-permute-start.4 = (f32[9,192]{1,0:T(8,128)S(1)}, f32[9,192]{1,0:T(8,128)S(1)}, u32[]{:S(2)}, u32[]{:S(2)}) collective-permute-start(f32[9,192]{1,0:T(8,128)S(1)} %get-tuple-element.23), channel_id=1, source_target_pairs={{0,1},{1,2},{2,3},{3,4},{4,5},{5,6},{6,7},{7,8},{8,9},{9,10},{10,1... | collective-permute-start | bytes 20744 | tf_op jit(solution)/shard_map/ppermute | solution.py:91
  66.4 2.5 %collective-permute-done.5 = f32[9,192]{1,0:T(8,128)S(1)} collective-permute-done((f32[9,192]{1,0:T(8,128)S(1)}, f32[9,192]{1,0:T(8,128)S(1)}, u32[]{:S(2)}, u32[]{:S(2)}) %collective-permute-start.5) | collective-permute-done | bytes 6944 | tf_op jit(solution)/shard_map/ppermute | solution.py:91
  69.3 2.1 %fusion.18 = f32[6,9,384]{2,1,0:T(8,128)S(1)} fusion(f32[6,9,384]{2,1,0:T(8,128)S(1)} %reshape.340, s32[6,384]{1,0:T(8,128)S(1)} %bitcast.143, f32[6,9,480]{2,1,0:T(8,128)S(1)} %broadcast_in_dim.22, f32[6,9,384]{2,1,0:T(8,128)S(1)} %gather_fusion.1), kind=kOutput, calls=%fused_computation.31 | convolution fusion | flops 109553472 | bytes 361728 | tf_op jit(solution)/shard_map/fnq,fqe->fne/dot_general | solution.py:150
  73.5 3.4 %collective-permute-start.8 = (f32[23,7,63]{2,1,0:T(8,128)S(1)}, f32[23,7,63]{2,1,0:T(8,128)S(1)}, u32[]{:S(2)}, u32[]{:S(2)}) collective-permute-start(f32[23,7,63]{2,1,0:T(8,128)S(1)} %slice.215), channel_id=1, source_target_pairs={{0,1},{1,0},{2,3},{3,2},{4,5},{5,4},{6,7},{7,6},{8,9},{9,8},{10,11... | collective-permute-start | bytes 121724 | tf_op jit(solution)/shard_map/ppermute | solution.py:222
  76.9 2.9 %collective-permute-done.8 = f32[23,7,63]{2,1,0:T(8,128)S(1)} collective-permute-done((f32[23,7,63]{2,1,0:T(8,128)S(1)}, f32[23,7,63]{2,1,0:T(8,128)S(1)}, u32[]{:S(2)}, u32[]{:S(2)}) %collective-permute-start.8) | collective-permute-done | bytes 40604 | tf_op jit(solution)/shard_map/ppermute | solution.py:222
  80.0 6.9 %collective-permute-start.9 = (f32[23,7,63]{2,1,0:T(8,128)S(1)}, f32[23,7,63]{2,1,0:T(8,128)S(1)}, u32[]{:S(2)}, u32[]{:S(2)}) collective-permute-start(f32[23,7,63]{2,1,0:T(8,128)S(1)} %slice_add_fusion), channel_id=1, source_target_pairs={{0,2},{1,3},{2,0},{3,1},{4,6},{5,7},{6,4},{7,5},{8,10},{9,11},{10,... | collective-permute-start | bytes 121724 | tf_op jit(solution)/shard_map/ppermute | solution.py:222
  86.8 1.9 %collective-permute-done.9 = f32[23,7,63]{2,1,0:T(8,128)S(1)} collective-permute-done((f32[23,7,63]{2,1,0:T(8,128)S(1)}, f32[23,7,63]{2,1,0:T(8,128)S(1)}, u32[]{:S(2)}, u32[]{:S(2)}) %collective-permute-start.9) | collective-permute-done | bytes 40604 | tf_op jit(solution)/shard_map/ppermute | solution.py:222
  88.8 2.6 %collective-permute-start.10 = (f32[23,7,63]{2,1,0:T(8,128)S(1)}, f32[23,7,63]{2,1,0:T(8,128)S(1)}, u32[]{:S(2)}, u32[]{:S(2)}) collective-permute-start(f32[23,7,63]{2,1,0:T(8,128)S(1)} %add.221), channel_id=1, source_target_pairs={{0,4},{1,5},{2,6},{3,7},{4,0},{5,1},{6,2},{7,3},{8,12},{9,13},{10,... | collective-permute-start | bytes 121724 | tf_op jit(solution)/shard_map/ppermute | solution.py:222
  94.1 6.0 %collective-permute-start.11 = (f32[23,7,63]{2,1,0:T(8,128)S(1)}, f32[23,7,63]{2,1,0:T(8,128)S(1)}, u32[]{:S(2)}, u32[]{:S(2)}) collective-permute-start(f32[23,7,63]{2,1,0:T(8,128)S(1)} %add.222), channel_id=1, source_target_pairs={{0,8},{1,9},{2,10},{3,11},{4,12},{5,13},{6,14},{7,15},{8,0},{9,1},... | collective-permute-start | bytes 121724 | tf_op jit(solution)/shard_map/ppermute | solution.py:222
  100.2 2.9 %collective-permute-done.11 = f32[23,7,63]{2,1,0:T(8,128)S(1)} collective-permute-done((f32[23,7,63]{2,1,0:T(8,128)S(1)}, f32[23,7,63]{2,1,0:T(8,128)S(1)}, u32[]{:S(2)}, u32[]{:S(2)}) %collective-permute-start.11) | collective-permute-done | bytes 40604 | tf_op jit(solution)/shard_map/ppermute | solution.py:222
  103.1 5.3 %collective-permute-start.12 = (f32[23,7,63]{2,1,0:T(8,128)S(1)}, f32[23,7,63]{2,1,0:T(8,128)S(1)}, u32[]{:S(2)}, u32[]{:S(2)}) collective-permute-start(f32[23,7,63]{2,1,0:T(8,128)S(1)} %add.223), channel_id=1, source_target_pairs={{0,16},{1,17},{2,18},{3,19},{4,20},{5,21},{6,22},{7,23},{8,24},{9,... | collective-permute-start | bytes 121724 | tf_op jit(solution)/shard_map/ppermute | solution.py:222
  108.4 6.3 %collective-permute-done.12 = f32[23,7,63]{2,1,0:T(8,128)S(1)} collective-permute-done((f32[23,7,63]{2,1,0:T(8,128)S(1)}, f32[23,7,63]{2,1,0:T(8,128)S(1)}, u32[]{:S(2)}, u32[]{:S(2)}) %collective-permute-start.12) | collective-permute-done | bytes 40604 | tf_op jit(solution)/shard_map/ppermute | solution.py:222
  120.7 1.9 %collective-permute-start.13 = (f32[9,48]{1,0:T(8,128)S(1)}, f32[9,48]{1,0:T(8,128)S(1)}, u32[]{:S(2)}, u32[]{:S(2)}) collective-permute-start(f32[9,48]{1,0:T(8,128)S(1)} %get-tuple-element.27), channel_id=1, source_target_pairs={{0,32},{64,96},{128,160},{192,224},{256,288},{320,352},{384,416},{... | collective-permute-start | bytes 5192 | tf_op jit(solution)/shard_map/ppermute | solution.py:101
  122.6 12.6 %collective-permute-start.14 = (f32[9,48]{1,0:T(8,128)S(1)}, f32[9,48]{1,0:T(8,128)S(1)}, u32[]{:S(2)}, u32[]{:S(2)}) collective-permute-start(f32[9,48]{1,0:T(8,128)S(1)} %get-tuple-element.28), channel_id=1, source_target_pairs={{32,64},{96,128},{160,192},{224,256},{288,320},{352,384},{416,448}... | collective-permute-start | bytes 5192 | tf_op jit(solution)/shard_map/ppermute | solution.py:104
  136.9 2.1 %fusion.19 = f32[6,9,384]{2,1,0:T(8,128)S(1)} fusion(f32[6,9,384]{2,1,0:T(8,128)S(1)} %reshape.346, s32[6,384]{1,0:T(8,128)S(1)} %bitcast.144, f32[6,9,480]{2,1,0:T(8,128)S(1)} %broadcast_in_dim.24, f32[6,9,384]{2,1,0:T(8,128)S(1)} %gather_fusion.2), kind=kOutput, calls=%fused_computation.32 | convolution fusion | flops 109553472 | bytes 361728 | tf_op jit(solution)/shard_map/fnq,fqe->fne/dot_general | solution.py:150
  143.1 12.9 %collective-permute-start.18 = (f32[36,48]{1,0:T(8,128)S(1)}, f32[36,48]{1,0:T(8,128)S(1)}, u32[]{:S(2)}, u32[]{:S(2)}) collective-permute-start(f32[36,48]{1,0:T(8,128)S(1)} %get-tuple-element.18), channel_id=1, source_target_pairs={{32,64},{96,128},{160,192},{224,256},{288,320},{352,384},{416,448}... | collective-permute-start | bytes 20744 | tf_op jit(solution)/shard_map/ppermute | solution.py:104
  156.4 2.5 %collective-permute-start.15 = (f32[36,192]{1,0:T(8,128)S(1)}, f32[36,192]{1,0:T(8,128)S(1)}, u32[]{:S(2)}, u32[]{:S(2)}) collective-permute-start(f32[36,192]{1,0:T(8,128)S(1)} %get-tuple-element.13), channel_id=1, source_target_pairs={{0,1},{1,2},{2,3},{3,4},{4,5},{5,6},{6,7},{7,8},{8,9},{9,10},{10,1... | collective-permute-start | bytes 82952 | tf_op jit(solution)/shard_map/ppermute | solution.py:91
  165.2 2.9 %fusion.13 = f32[6,36,384]{2,1,0:T(8,128)} fusion(f32[6,36,384]{2,1,0:T(8,128)S(1)} %reshape.350, s32[6,384]{1,0:T(8,128)S(1)} %bitcast.145, f32[6,36,480]{2,1,0:T(8,128)S(1)} %broadcast_in_dim.26, f32[6,36,384]{2,1,0:T(8,128)S(1)} %copy-done.7), kind=kOutput, calls=%fused_computation.22 | convolution fusion | flops 432241920 | bytes 1419264 | tf_op jit(solution)/shard_map/fnq,fqe->fne/dot_general | solution.py:150
  (211 shorter events, 45.0 us)
Async XLA Ops:
  2.8 31.1 %collective-permute-start.2 = (f32[36,48]{1,0:T(8,128)S(1)}, f32[36,48]{1,0:T(8,128)S(1)}, u32[]{:S(2)}, u32[]{:S(2)}) collective-permute-start(f32[36,48]{1,0:T(8,128)S(1)} %get-tuple-element.21), channel_id=1, source_target_pairs={{0,32},{64,96},{128,160},{192,224},{256,288},{320,352},{384,416},{... | collective-permute-start | bytes 20744 | tf_op jit(solution)/shard_map/ppermute | solution.py:101
  18.9 15.1 %collective-permute-start.3 = (f32[36,48]{1,0:T(8,128)S(1)}, f32[36,48]{1,0:T(8,128)S(1)}, u32[]{:S(2)}, u32[]{:S(2)}) collective-permute-start(f32[36,48]{1,0:T(8,128)S(1)} %get-tuple-element.22), channel_id=1, source_target_pairs={{32,64},{96,128},{160,192},{224,256},{288,320},{352,384},{416,448}... | collective-permute-start | bytes 20744 | tf_op jit(solution)/shard_map/ppermute | solution.py:104
  23.1 10.9 %collective-permute-start = (f32[44,192]{1,0:T(8,128)S(1)}, f32[44,192]{1,0:T(8,128)S(1)}, u32[]{:S(2)}, u32[]{:S(2)}) collective-permute-start(f32[44,192]{1,0:T(8,128)S(1)} %get-tuple-element.11), channel_id=1, source_target_pairs={{0,1},{1,2},{2,3},{3,4},{4,5},{5,6},{6,7},{7,8},{8,9},{9,10},{10,1... | collective-permute-start | bytes 101384 | tf_op jit(solution)/shard_map/ppermute | solution.py:91
  26.5 7.6 %collective-permute-start.1 = (f32[44,192]{1,0:T(8,128)S(1)}, f32[44,192]{1,0:T(8,128)S(1)}, u32[]{:S(2)}, u32[]{:S(2)}) collective-permute-start(f32[44,192]{1,0:T(8,128)S(1)} %get-tuple-element.12), channel_id=1, source_target_pairs={{1,0},{2,1},{3,2},{4,3},{5,4},{6,5},{7,6},{8,7},{9,8},{10,9},{11,1... | collective-permute-start | bytes 101384 | tf_op jit(solution)/shard_map/ppermute | solution.py:91
  41.9 27.0 %copy-start.9 = (f32[72,9]{1,0:T(8,128)S(1)}, f32[72,9]{1,0:T(8,128)}, u32[]{:S(2)}) copy-start(f32[72,9]{1,0:T(8,128)} %constant.150.clone) | copy-start | bytes 7780
  42.2 24.1 %collective-permute-start.6 = (f32[9,48]{1,0:T(8,128)S(1)}, f32[9,48]{1,0:T(8,128)S(1)}, u32[]{:S(2)}, u32[]{:S(2)}) collective-permute-start(f32[9,48]{1,0:T(8,128)S(1)} %get-tuple-element.31), channel_id=1, source_target_pairs={{0,32},{64,96},{128,160},{192,224},{256,288},{320,352},{384,416},{... | collective-permute-start | bytes 5192 | tf_op jit(solution)/shard_map/ppermute | solution.py:101
  44.1 22.2 %collective-permute-start.7 = (f32[9,48]{1,0:T(8,128)S(1)}, f32[9,48]{1,0:T(8,128)S(1)}, u32[]{:S(2)}, u32[]{:S(2)}) collective-permute-start(f32[9,48]{1,0:T(8,128)S(1)} %get-tuple-element.32), channel_id=1, source_target_pairs={{32,64},{96,128},{160,192},{224,256},{288,320},{352,384},{416,448}... | collective-permute-start | bytes 5192 | tf_op jit(solution)/shard_map/ppermute | solution.py:104
  60.5 5.9 %collective-permute-start.4 = (f32[9,192]{1,0:T(8,128)S(1)}, f32[9,192]{1,0:T(8,128)S(1)}, u32[]{:S(2)}, u32[]{:S(2)}) collective-permute-start(f32[9,192]{1,0:T(8,128)S(1)} %get-tuple-element.23), channel_id=1, source_target_pairs={{0,1},{1,2},{2,3},{3,4},{4,5},{5,6},{6,7},{7,8},{8,9},{9,10},{10,1... | collective-permute-start | bytes 20744 | tf_op jit(solution)/shard_map/ppermute | solution.py:91
  64.5 4.5 %collective-permute-start.5 = (f32[9,192]{1,0:T(8,128)S(1)}, f32[9,192]{1,0:T(8,128)S(1)}, u32[]{:S(2)}, u32[]{:S(2)}) collective-permute-start(f32[9,192]{1,0:T(8,128)S(1)} %get-tuple-element.24), channel_id=1, source_target_pairs={{1,0},{2,1},{3,2},{4,3},{5,4},{6,5},{7,6},{8,7},{9,8},{10,9},{11,1... | collective-permute-start | bytes 20744 | tf_op jit(solution)/shard_map/ppermute | solution.py:91
  73.5 6.4 %collective-permute-start.8 = (f32[23,7,63]{2,1,0:T(8,128)S(1)}, f32[23,7,63]{2,1,0:T(8,128)S(1)}, u32[]{:S(2)}, u32[]{:S(2)}) collective-permute-start(f32[23,7,63]{2,1,0:T(8,128)S(1)} %slice.215), channel_id=1, source_target_pairs={{0,1},{1,0},{2,3},{3,2},{4,5},{5,4},{6,7},{7,6},{8,9},{9,8},{10,11... | collective-permute-start | bytes 121724 | tf_op jit(solution)/shard_map/ppermute | solution.py:222
  80.0 8.8 %collective-permute-start.9 = (f32[23,7,63]{2,1,0:T(8,128)S(1)}, f32[23,7,63]{2,1,0:T(8,128)S(1)}, u32[]{:S(2)}, u32[]{:S(2)}) collective-permute-start(f32[23,7,63]{2,1,0:T(8,128)S(1)} %slice_add_fusion), channel_id=1, source_target_pairs={{0,2},{1,3},{2,0},{3,1},{4,6},{5,7},{6,4},{7,5},{8,10},{9,11},{10,... | collective-permute-start | bytes 121724 | tf_op jit(solution)/shard_map/ppermute | solution.py:222
  88.8 5.3 %collective-permute-start.10 = (f32[23,7,63]{2,1,0:T(8,128)S(1)}, f32[23,7,63]{2,1,0:T(8,128)S(1)}, u32[]{:S(2)}, u32[]{:S(2)}) collective-permute-start(f32[23,7,63]{2,1,0:T(8,128)S(1)} %add.221), channel_id=1, source_target_pairs={{0,4},{1,5},{2,6},{3,7},{4,0},{5,1},{6,2},{7,3},{8,12},{9,13},{10,... | collective-permute-start | bytes 121724 | tf_op jit(solution)/shard_map/ppermute | solution.py:222
  92.2 23.4 %copy-start.23 = (f32[23,7]{0,1:T(8,128)S(1)}, f32[23,7]{0,1:T(8,128)}, u32[]{:S(2)}) copy-start(f32[23,7]{0,1:T(8,128)} %get-tuple-element.37) | copy-start | bytes 1936
  92.2 23.4 %copy-start.24 = (f32[23,7]{0,1:T(8,128)S(1)}, f32[23,7]{0,1:T(8,128)}, u32[]{:S(2)}) copy-start(f32[23,7]{0,1:T(8,128)} %get-tuple-element.38) | copy-start | bytes 1936
  92.2 23.4 %copy-start.31 = (f32[63]{0:T(128)S(1)}, f32[63]{0:T(128)}, u32[]{:S(2)}) copy-start(f32[63]{0:T(128)} %get-tuple-element.43) | copy-start | bytes 760
  92.2 23.4 %copy-start.32 = (f32[63]{0:T(128)S(1)}, f32[63]{0:T(128)}, u32[]{:S(2)}) copy-start(f32[63]{0:T(128)} %get-tuple-element.44) | copy-start | bytes 760
  94.1 8.9 %collective-permute-start.11 = (f32[23,7,63]{2,1,0:T(8,128)S(1)}, f32[23,7,63]{2,1,0:T(8,128)S(1)}, u32[]{:S(2)}, u32[]{:S(2)}) collective-permute-start(f32[23,7,63]{2,1,0:T(8,128)S(1)} %add.222), channel_id=1, source_target_pairs={{0,8},{1,9},{2,10},{3,11},{4,12},{5,13},{6,14},{7,15},{8,0},{9,1},... | collective-permute-start | bytes 121724 | tf_op jit(solution)/shard_map/ppermute | solution.py:222
  103.1 11.6 %collective-permute-start.12 = (f32[23,7,63]{2,1,0:T(8,128)S(1)}, f32[23,7,63]{2,1,0:T(8,128)S(1)}, u32[]{:S(2)}, u32[]{:S(2)}) collective-permute-start(f32[23,7,63]{2,1,0:T(8,128)S(1)} %add.223), channel_id=1, source_target_pairs={{0,16},{1,17},{2,18},{3,19},{4,20},{5,21},{6,22},{7,23},{8,24},{9,... | collective-permute-start | bytes 121724 | tf_op jit(solution)/shard_map/ppermute | solution.py:222
  120.7 15.5 %collective-permute-start.13 = (f32[9,48]{1,0:T(8,128)S(1)}, f32[9,48]{1,0:T(8,128)S(1)}, u32[]{:S(2)}, u32[]{:S(2)}) collective-permute-start(f32[9,48]{1,0:T(8,128)S(1)} %get-tuple-element.27), channel_id=1, source_target_pairs={{0,32},{64,96},{128,160},{192,224},{256,288},{320,352},{384,416},{... | collective-permute-start | bytes 5192 | tf_op jit(solution)/shard_map/ppermute | solution.py:101
  122.6 13.9 %collective-permute-start.14 = (f32[9,48]{1,0:T(8,128)S(1)}, f32[9,48]{1,0:T(8,128)S(1)}, u32[]{:S(2)}, u32[]{:S(2)}) collective-permute-start(f32[9,48]{1,0:T(8,128)S(1)} %get-tuple-element.28), channel_id=1, source_target_pairs={{32,64},{96,128},{160,192},{224,256},{288,320},{352,384},{416,448}... | collective-permute-start | bytes 5192 | tf_op jit(solution)/shard_map/ppermute | solution.py:104
  141.1 20.7 %collective-permute-start.17 = (f32[36,48]{1,0:T(8,128)S(1)}, f32[36,48]{1,0:T(8,128)S(1)}, u32[]{:S(2)}, u32[]{:S(2)}) collective-permute-start(f32[36,48]{1,0:T(8,128)S(1)} %get-tuple-element.17), channel_id=1, source_target_pairs={{0,32},{64,96},{128,160},{192,224},{256,288},{320,352},{384,416},{... | collective-permute-start | bytes 20744 | tf_op jit(solution)/shard_map/ppermute | solution.py:101
  143.1 18.7 %collective-permute-start.18 = (f32[36,48]{1,0:T(8,128)S(1)}, f32[36,48]{1,0:T(8,128)S(1)}, u32[]{:S(2)}, u32[]{:S(2)}) collective-permute-start(f32[36,48]{1,0:T(8,128)S(1)} %get-tuple-element.18), channel_id=1, source_target_pairs={{32,64},{96,128},{160,192},{224,256},{288,320},{352,384},{416,448}... | collective-permute-start | bytes 20744 | tf_op jit(solution)/shard_map/ppermute | solution.py:104
  156.4 5.4 %collective-permute-start.15 = (f32[36,192]{1,0:T(8,128)S(1)}, f32[36,192]{1,0:T(8,128)S(1)}, u32[]{:S(2)}, u32[]{:S(2)}) collective-permute-start(f32[36,192]{1,0:T(8,128)S(1)} %get-tuple-element.13), channel_id=1, source_target_pairs={{0,1},{1,2},{2,3},{3,4},{4,5},{5,6},{6,7},{7,8},{8,9},{9,10},{10,1... | collective-permute-start | bytes 82952 | tf_op jit(solution)/shard_map/ppermute | solution.py:91
  158.9 4.7 %collective-permute-start.16 = (f32[36,192]{1,0:T(8,128)S(1)}, f32[36,192]{1,0:T(8,128)S(1)}, u32[]{:S(2)}, u32[]{:S(2)}) collective-permute-start(f32[36,192]{1,0:T(8,128)S(1)} %get-tuple-element.14), channel_id=1, source_target_pairs={{1,0},{2,1},{3,2},{4,3},{5,4},{6,5},{7,6},{8,7},{9,8},{10,9},{11,1... | collective-permute-start | bytes 82952 | tf_op jit(solution)/shard_map/ppermute | solution.py:91
  (28 other events, 139.5 us)

commit v10 on v7

--- a/solution.py
+++ b/solution.py
@@ -91,18 +91,18 @@
     return lax.ppermute(block, axis, pairs)
 
 
-def region_exchange(region_out):
-    count = lax.axis_size("region")
-    odd = (lax.axis_index("region") % 2) == 1
+def region_exchange(region_out, axis="region"):
+    count = lax.axis_size(axis)
+    odd = (lax.axis_index(axis) % 2) == 1
     far_pairs = [(i, i + 1) for i in range(1, count - 1, 2)]
     far_pairs += [(i, i - 1) for i in range(2, count, 2)]
     near_pairs = [(i, i + 1) for i in range(0, count - 1, 2)]
     near_pairs += [(i + 1, i) for i in range(0, count - 1, 2)]
     near_recv = lax.ppermute(
-        jnp.where(odd, region_out[0], region_out[1]), "region", near_pairs
+        jnp.where(odd, region_out[0], region_out[1]), axis, near_pairs
     )
     far_recv = lax.ppermute(
-        jnp.where(odd, region_out[1], region_out[0]), "region", far_pairs
+        jnp.where(odd, region_out[1], region_out[0]), axis, far_pairs
     )
     return jnp.where(odd, near_recv, far_recv), jnp.where(odd, far_recv, near_recv)
 
@@ -116,11 +116,6 @@
     both = mm(jnp.concatenate([stiffness, select], axis=0), current)
     product = both[:cube]
     traces = both[cube:].reshape(6, plane, elements)
-    region_out = jnp.einsum(
-        "snj,sjk->snk", traces[2:4], pick_region, precision=HIGH,
-        preferred_element_type=jnp.float32,
-    )
-    from_region_low, from_region_high = region_exchange(region_out)
     received = None
     if group_ghosts is None:
         group_out = jnp.einsum(
@@ -129,10 +124,14 @@
         )
         if extra is not None:
             group_out = jnp.concatenate([group_out, extra], axis=1)
-        from_group_low = shift(group_out[1], "group", 1)
-        from_group_high = shift(group_out[0], "group", -1)
+        from_group_low, from_group_high = region_exchange(group_out, "group")
         received = (from_group_low[plane:], from_group_high[plane:])
         group_ghosts = (from_group_low[:plane], from_group_high[:plane])
+    region_out = jnp.einsum(
+        "snj,sjk->snk", traces[2:4], pick_region, precision=HIGH,
+        preferred_element_type=jnp.float32,
+    )
+    from_region_low, from_region_high = region_exchange(region_out)
     raw = jnp.concatenate(
         [group_ghosts[0], group_ghosts[1], from_region_low, from_region_high], axis=1
     )

time: 170 us -> 174 us (1.024)
  the two profiles are of different devices: /device:TPU:1 before, /device:TPU:30 now
where the time goes in v10:
time: 174 us; the launch traced here: 173 us
  starting transfers between devices  88.2 us (51%)
  waiting for transfers between devices  40.4 us (23%)
  matrix products  26.5 us (15%)
  local copies, waits for them, and re-layouts  13.6 us (8%)
  other arithmetic  2.63 us (2%)
    ppermute x7, starting transfers between devices, region_exchange(): lax.ppermute(jnp.where(odd, region_out[1], region_out[0]), axis, far_pairs)  62.8 us
    ppermute x5, waiting for transfers between devices, gather_slab(): interior = interior + lax.ppermute(interior, 'group', partner)  29.6 us
    ppermute x7, starting transfers between devices, region_exchange(): lax.ppermute(jnp.where(odd, region_out[0], region_out[1]), axis, near_pairs)  14.2 us
    ppermute x5, starting transfers between devices, gather_slab(): interior = interior + lax.ppermute(interior, 'group', partner)  11.3 us
    ppermute x7, waiting for transfers between devices, region_exchange(): lax.ppermute(jnp.where(odd, region_out[1], region_out[0]), axis, far_pairs)  10.4 us
    dot_general x4, matrix products, apply_level(): jnp.einsum('fnq,fqe->fne', source, gather.astype(jnp.float32), precision=...  8.58 us
    dot_general x15, matrix products, mm(): return jnp.dot(a, b, precision=HIGHEST, preferred_element_type=jnp.float32)  7.6 us
    unnamed x69, local copies, waits for them, and re-layouts  6.06 us
  transfers between devices with their start and end apart: 19, of which 9 were waited for; matrix products, arithmetic and copies ran while one was open for 5% of the time, Pallas kernels for 0%

profile of v10, /device:TPU:30, one launch (start us, length us, event | category | flops | bytes accessed | tf_op | source)
XLA Modules:
  0.0 172.8 jit_solution(8579667322968210029)
XLA Ops:
  5.0 2.7 %collective-permute-start = (f32[44,192]{1,0:T(8,128)S(1)}, f32[44,192]{1,0:T(8,128)S(1)}, u32[]{:S(2)}, u32[]{:S(2)}) collective-permute-start(f32[44,192]{1,0:T(8,128)S(1)} %get-tuple-element.13), channel_id=1, source_target_pairs={{0,1},{2,3},{4,5},{6,7},{8,9},{10,11},{12,13},{14,15},{16,17},{18,... | collective-permute-start | bytes 101384 | tf_op jit(solution)/shard_map/ppermute | solution.py:101
  7.7 4.3 %collective-permute-start.1 = (f32[44,192]{1,0:T(8,128)S(1)}, f32[44,192]{1,0:T(8,128)S(1)}, u32[]{:S(2)}, u32[]{:S(2)}) collective-permute-start(f32[44,192]{1,0:T(8,128)S(1)} %get-tuple-element.14), channel_id=1, source_target_pairs={{1,2},{3,4},{5,6},{7,8},{9,10},{11,12},{13,14},{15,16},{17,18},{19... | collective-permute-start | bytes 101384 | tf_op jit(solution)/shard_map/ppermute | solution.py:104
  14.3 22.5 %collective-permute-start.3 = (f32[36,48]{1,0:T(8,128)S(1)}, f32[36,48]{1,0:T(8,128)S(1)}, u32[]{:S(2)}, u32[]{:S(2)}) collective-permute-start(f32[36,48]{1,0:T(8,128)S(1)} %get-tuple-element.26), channel_id=1, source_target_pairs={{32,64},{96,128},{160,192},{224,256},{288,320},{352,384},{416,448}... | collective-permute-start | bytes 20744 | tf_op jit(solution)/shard_map/ppermute | solution.py:104
  43.3 2.2 %fusion.12 = f32[6,36,384]{2,1,0:T(8,128)S(1)} fusion(f32[6,36,384]{2,1,0:T(8,128)S(1)} %reshape.347, s32[6,384]{1,0:T(8,128)S(1)} %bitcast.129, f32[6,36,480]{2,1,0:T(8,128)S(1)} %broadcast_in_dim.19, f32[6,36,384]{2,1,0:T(8,128)S(1)} %copy-done.9), kind=kOutput, calls=%fused_computation.21 | convolution fusion | flops 432241920 | bytes 1419264 | tf_op jit(solution)/shard_map/fnq,fqe->fne/dot_general | solution.py:144
  50.9 9.9 %collective-permute-start.7 = (f32[9,48]{1,0:T(8,128)S(1)}, f32[9,48]{1,0:T(8,128)S(1)}, u32[]{:S(2)}, u32[]{:S(2)}) collective-permute-start(f32[9,48]{1,0:T(8,128)S(1)} %get-tuple-element.38), channel_id=1, source_target_pairs={{32,64},{96,128},{160,192},{224,256},{288,320},{352,384},{416,448}... | collective-permute-start | bytes 5192 | tf_op jit(solution)/shard_map/ppermute | solution.py:104
  62.8 4.8 %collective-permute-start.5 = (f32[9,192]{1,0:T(8,128)S(1)}, f32[9,192]{1,0:T(8,128)S(1)}, u32[]{:S(2)}, u32[]{:S(2)}) collective-permute-start(f32[9,192]{1,0:T(8,128)S(1)} %get-tuple-element.30), channel_id=1, source_target_pairs={{1,2},{3,4},{5,6},{7,8},{9,10},{11,12},{13,14},{15,16},{17,18},{19... | collective-permute-start | bytes 20744 | tf_op jit(solution)/shard_map/ppermute | solution.py:104
  68.2 2.3 %collective-permute-done.5 = f32[9,192]{1,0:T(8,128)S(1)} collective-permute-done((f32[9,192]{1,0:T(8,128)S(1)}, f32[9,192]{1,0:T(8,128)S(1)}, u32[]{:S(2)}, u32[]{:S(2)}) %collective-permute-start.5) | collective-permute-done | bytes 6944 | tf_op jit(solution)/shard_map/ppermute | solution.py:104
  71.0 2.1 %fusion.18 = f32[6,9,384]{2,1,0:T(8,128)S(1)} fusion(f32[6,9,384]{2,1,0:T(8,128)S(1)} %reshape.351, s32[6,384]{1,0:T(8,128)S(1)} %bitcast.130, f32[6,9,480]{2,1,0:T(8,128)S(1)} %broadcast_in_dim.22, f32[6,9,384]{2,1,0:T(8,128)S(1)} %gather_fusion.1), kind=kOutput, calls=%fused_computation.31 | convolution fusion | flops 109553472 | bytes 361728 | tf_op jit(solution)/shard_map/fnq,fqe->fne/dot_general | solution.py:144
  77.3 5.3 %collective-permute-done.8 = f32[23,7,63]{2,1,0:T(8,128)S(1)} collective-permute-done((f32[23,7,63]{2,1,0:T(8,128)S(1)}, f32[23,7,63]{2,1,0:T(8,128)S(1)}, u32[]{:S(2)}, u32[]{:S(2)}) %collective-permute-start.8) | collective-permute-done | bytes 40604 | tf_op jit(solution)/shard_map/ppermute | solution.py:216
  84.6 6.0 %collective-permute-done.9 = f32[23,7,63]{2,1,0:T(8,128)S(1)} collective-permute-done((f32[23,7,63]{2,1,0:T(8,128)S(1)}, f32[23,7,63]{2,1,0:T(8,128)S(1)}, u32[]{:S(2)}, u32[]{:S(2)}) %collective-permute-start.9) | collective-permute-done | bytes 40604 | tf_op jit(solution)/shard_map/ppermute | solution.py:216
  90.6 2.4 %collective-permute-start.10 = (f32[23,7,63]{2,1,0:T(8,128)S(1)}, f32[23,7,63]{2,1,0:T(8,128)S(1)}, u32[]{:S(2)}, u32[]{:S(2)}) collective-permute-start(f32[23,7,63]{2,1,0:T(8,128)S(1)} %add.227), channel_id=1, source_target_pairs={{0,4},{1,5},{2,6},{3,7},{4,0},{5,1},{6,2},{7,3},{8,12},{9,13},{10,... | collective-permute-start | bytes 121724 | tf_op jit(solution)/shard_map/ppermute | solution.py:216
  94.5 3.4 %collective-permute-done.10 = f32[23,7,63]{2,1,0:T(8,128)S(1)} collective-permute-done((f32[23,7,63]{2,1,0:T(8,128)S(1)}, f32[23,7,63]{2,1,0:T(8,128)S(1)}, u32[]{:S(2)}, u32[]{:S(2)}) %collective-permute-start.10) | collective-permute-done | bytes 40604 | tf_op jit(solution)/shard_map/ppermute | solution.py:216
  97.9 2.7 %collective-permute-start.11 = (f32[23,7,63]{2,1,0:T(8,128)S(1)}, f32[23,7,63]{2,1,0:T(8,128)S(1)}, u32[]{:S(2)}, u32[]{:S(2)}) collective-permute-start(f32[23,7,63]{2,1,0:T(8,128)S(1)} %add.228), channel_id=1, source_target_pairs={{0,8},{1,9},{2,10},{3,11},{4,12},{5,13},{6,14},{7,15},{8,0},{9,1},... | collective-permute-start | bytes 121724 | tf_op jit(solution)/shard_map/ppermute | solution.py:216
  100.7 6.8 %collective-permute-done.11 = f32[23,7,63]{2,1,0:T(8,128)S(1)} collective-permute-done((f32[23,7,63]{2,1,0:T(8,128)S(1)}, f32[23,7,63]{2,1,0:T(8,128)S(1)}, u32[]{:S(2)}, u32[]{:S(2)}) %collective-permute-start.11) | collective-permute-done | bytes 40604 | tf_op jit(solution)/shard_map/ppermute | solution.py:216
  107.5 2.4 %collective-permute-start.12 = (f32[23,7,63]{2,1,0:T(8,128)S(1)}, f32[23,7,63]{2,1,0:T(8,128)S(1)}, u32[]{:S(2)}, u32[]{:S(2)}) collective-permute-start(f32[23,7,63]{2,1,0:T(8,128)S(1)} %add.229), channel_id=1, source_target_pairs={{0,16},{1,17},{2,18},{3,19},{4,20},{5,21},{6,22},{7,23},{8,24},{9,... | collective-permute-start | bytes 121724 | tf_op jit(solution)/shard_map/ppermute | solution.py:216
  109.9 8.1 %collective-permute-done.12 = f32[23,7,63]{2,1,0:T(8,128)S(1)} collective-permute-done((f32[23,7,63]{2,1,0:T(8,128)S(1)}, f32[23,7,63]{2,1,0:T(8,128)S(1)}, u32[]{:S(2)}, u32[]{:S(2)}) %collective-permute-start.12) | collective-permute-done | bytes 40604 | tf_op jit(solution)/shard_map/ppermute | solution.py:216
  123.9 1.9 %collective-permute-start.13 = (f32[9,48]{1,0:T(8,128)S(1)}, f32[9,48]{1,0:T(8,128)S(1)}, u32[]{:S(2)}, u32[]{:S(2)}) collective-permute-start(f32[9,48]{1,0:T(8,128)S(1)} %get-tuple-element.33), channel_id=1, source_target_pairs={{0,32},{64,96},{128,160},{192,224},{256,288},{320,352},{384,416},{... | collective-permute-start | bytes 5192 | tf_op jit(solution)/shard_map/ppermute | solution.py:101
  125.8 9.6 %collective-permute-start.14 = (f32[9,48]{1,0:T(8,128)S(1)}, f32[9,48]{1,0:T(8,128)S(1)}, u32[]{:S(2)}, u32[]{:S(2)}) collective-permute-start(f32[9,48]{1,0:T(8,128)S(1)} %get-tuple-element.34), channel_id=1, source_target_pairs={{32,64},{96,128},{160,192},{224,256},{288,320},{352,384},{416,448}... | collective-permute-start | bytes 5192 | tf_op jit(solution)/shard_map/ppermute | solution.py:104
  136.4 4.0 %collective-permute-done.14 = f32[9,48]{1,0:T(8,128)S(1)} collective-permute-done((f32[9,48]{1,0:T(8,128)S(1)}, f32[9,48]{1,0:T(8,128)S(1)}, u32[]{:S(2)}, u32[]{:S(2)}) %collective-permute-start.14) | collective-permute-done | bytes 1760 | tf_op jit(solution)/shard_map/ppermute | solution.py:104
  140.8 2.1 %fusion.19 = f32[6,9,384]{2,1,0:T(8,128)S(1)} fusion(f32[6,9,384]{2,1,0:T(8,128)S(1)} %reshape.357, s32[6,384]{1,0:T(8,128)S(1)} %bitcast.131, f32[6,9,480]{2,1,0:T(8,128)S(1)} %broadcast_in_dim.24, f32[6,9,384]{2,1,0:T(8,128)S(1)} %gather_fusion.2), kind=kOutput, calls=%fused_computation.32 | convolution fusion | flops 109553472 | bytes 361728 | tf_op jit(solution)/shard_map/fnq,fqe->fne/dot_general | solution.py:144
  147.5 9.7 %collective-permute-start.18 = (f32[36,48]{1,0:T(8,128)S(1)}, f32[36,48]{1,0:T(8,128)S(1)}, u32[]{:S(2)}, u32[]{:S(2)}) collective-permute-start(f32[36,48]{1,0:T(8,128)S(1)} %get-tuple-element.22), channel_id=1, source_target_pairs={{32,64},{96,128},{160,192},{224,256},{288,320},{352,384},{416,448}... | collective-permute-start | bytes 20744 | tf_op jit(solution)/shard_map/ppermute | solution.py:104
  159.2 2.1 %collective-permute-start.16 = (f32[36,192]{1,0:T(8,128)S(1)}, f32[36,192]{1,0:T(8,128)S(1)}, u32[]{:S(2)}, u32[]{:S(2)}) collective-permute-start(f32[36,192]{1,0:T(8,128)S(1)} %get-tuple-element.18), channel_id=1, source_target_pairs={{1,2},{3,4},{5,6},{7,8},{9,10},{11,12},{13,14},{15,16},{17,18},{19... | collective-permute-start | bytes 82952 | tf_op jit(solution)/shard_map/ppermute | solution.py:104
  163.1 4.0 %collective-permute-done.16 = f32[36,192]{1,0:T(8,128)S(1)} collective-permute-done((f32[36,192]{1,0:T(8,128)S(1)}, f32[36,192]{1,0:T(8,128)S(1)}, u32[]{:S(2)}, u32[]{:S(2)}) %collective-permute-start.16) | collective-permute-done | bytes 27680 | tf_op jit(solution)/shard_map/ppermute | solution.py:104
  168.8 2.2 %fusion.13 = f32[6,36,384]{2,1,0:T(8,128)S(1)} fusion(f32[6,36,384]{2,1,0:T(8,128)S(1)} %copy-done.4, s32[6,384]{1,0:T(8,128)S(1)} %bitcast.132, f32[6,36,480]{2,1,0:T(8,128)S(1)} %broadcast_in_dim.26, f32[6,36,384]{2,1,0:T(8,128)S(1)} %copy-done.8), kind=kOutput, calls=%fused_computation.22 | convolution fusion | flops 432241920 | bytes 1419264 | tf_op jit(solution)/shard_map/fnq,fqe->fne/dot_general | solution.py:144
  (213 shorter events, 48.0 us)
Async XLA Ops:
  3.4 33.5 %copy-start.27 = (s32[1,480]{1,0:T(1,128)S(1)}, s32[1,480]{1,0:T(1,128)}, u32[]{:S(2)}) copy-start(s32[1,480]{1,0:T(1,128)} %param.40) | copy-start | bytes 5764
  3.4 33.5 %copy-start.28 = (s32[6]{0:T(128)S(1)}, s32[6]{0:T(128)}, u32[]{:S(2)}) copy-start(s32[6]{0:T(128)} %constant.170) | copy-start | bytes 76
  5.0 36.5 %collective-permute-start = (f32[44,192]{1,0:T(8,128)S(1)}, f32[44,192]{1,0:T(8,128)S(1)}, u32[]{:S(2)}, u32[]{:S(2)}) collective-permute-start(f32[44,192]{1,0:T(8,128)S(1)} %get-tuple-element.13), channel_id=1, source_target_pairs={{0,1},{2,3},{4,5},{6,7},{8,9},{10,11},{12,13},{14,15},{16,17},{18,... | collective-permute-start | bytes 101384 | tf_op jit(solution)/shard_map/ppermute | solution.py:101
  7.7 33.9 %collective-permute-start.1 = (f32[44,192]{1,0:T(8,128)S(1)}, f32[44,192]{1,0:T(8,128)S(1)}, u32[]{:S(2)}, u32[]{:S(2)}) collective-permute-start(f32[44,192]{1,0:T(8,128)S(1)} %get-tuple-element.14), channel_id=1, source_target_pairs={{1,2},{3,4},{5,6},{7,8},{9,10},{11,12},{13,14},{15,16},{17,18},{19... | collective-permute-start | bytes 101384 | tf_op jit(solution)/shard_map/ppermute | solution.py:104
  12.4 29.2 %collective-permute-start.2 = (f32[36,48]{1,0:T(8,128)S(1)}, f32[36,48]{1,0:T(8,128)S(1)}, u32[]{:S(2)}, u32[]{:S(2)}) collective-permute-start(f32[36,48]{1,0:T(8,128)S(1)} %get-tuple-element.25), channel_id=1, source_target_pairs={{0,32},{64,96},{128,160},{192,224},{256,288},{320,352},{384,416},{... | collective-permute-start | bytes 20744 | tf_op jit(solution)/shard_map/ppermute | solution.py:101
  14.3 27.3 %collective-permute-start.3 = (f32[36,48]{1,0:T(8,128)S(1)}, f32[36,48]{1,0:T(8,128)S(1)}, u32[]{:S(2)}, u32[]{:S(2)}) collective-permute-start(f32[36,48]{1,0:T(8,128)S(1)} %get-tuple-element.26), channel_id=1, source_target_pairs={{32,64},{96,128},{160,192},{224,256},{288,320},{352,384},{416,448}... | collective-permute-start | bytes 20744 | tf_op jit(solution)/shard_map/ppermute | solution.py:104
  49.0 19.1 %collective-permute-start.6 = (f32[9,48]{1,0:T(8,128)S(1)}, f32[9,48]{1,0:T(8,128)S(1)}, u32[]{:S(2)}, u32[]{:S(2)}) collective-permute-start(f32[9,48]{1,0:T(8,128)S(1)} %get-tuple-element.37), channel_id=1, source_target_pairs={{0,32},{64,96},{128,160},{192,224},{256,288},{320,352},{384,416},{... | collective-permute-start | bytes 5192 | tf_op jit(solution)/shard_map/ppermute | solution.py:101
  50.9 17.2 %collective-permute-start.7 = (f32[9,48]{1,0:T(8,128)S(1)}, f32[9,48]{1,0:T(8,128)S(1)}, u32[]{:S(2)}, u32[]{:S(2)}) collective-permute-start(f32[9,48]{1,0:T(8,128)S(1)} %get-tuple-element.38), channel_id=1, source_target_pairs={{32,64},{96,128},{160,192},{224,256},{288,320},{352,384},{416,448}... | collective-permute-start | bytes 5192 | tf_op jit(solution)/shard_map/ppermute | solution.py:104
  60.9 7.3 %collective-permute-start.4 = (f32[9,192]{1,0:T(8,128)S(1)}, f32[9,192]{1,0:T(8,128)S(1)}, u32[]{:S(2)}, u32[]{:S(2)}) collective-permute-start(f32[9,192]{1,0:T(8,128)S(1)} %get-tuple-element.29), channel_id=1, source_target_pairs={{0,1},{2,3},{4,5},{6,7},{8,9},{10,11},{12,13},{14,15},{16,17},{18,... | collective-permute-start | bytes 20744 | tf_op jit(solution)/shard_map/ppermute | solution.py:101
  62.8 7.7 %collective-permute-start.5 = (f32[9,192]{1,0:T(8,128)S(1)}, f32[9,192]{1,0:T(8,128)S(1)}, u32[]{:S(2)}, u32[]{:S(2)}) collective-permute-start(f32[9,192]{1,0:T(8,128)S(1)} %get-tuple-element.30), channel_id=1, source_target_pairs={{1,2},{3,4},{5,6},{7,8},{9,10},{11,12},{13,14},{15,16},{17,18},{19... | collective-permute-start | bytes 20744 | tf_op jit(solution)/shard_map/ppermute | solution.py:104
  75.3 7.2 %collective-permute-start.8 = (f32[23,7,63]{2,1,0:T(8,128)S(1)}, f32[23,7,63]{2,1,0:T(8,128)S(1)}, u32[]{:S(2)}, u32[]{:S(2)}) collective-permute-start(f32[23,7,63]{2,1,0:T(8,128)S(1)} %slice.223), channel_id=1, source_target_pairs={{0,1},{1,0},{2,3},{3,2},{4,5},{5,4},{6,7},{7,6},{8,9},{9,8},{10,11... | collective-permute-start | bytes 121724 | tf_op jit(solution)/shard_map/ppermute | solution.py:216
  82.6 8.0 %collective-permute-start.9 = (f32[23,7,63]{2,1,0:T(8,128)S(1)}, f32[23,7,63]{2,1,0:T(8,128)S(1)}, u32[]{:S(2)}, u32[]{:S(2)}) collective-permute-start(f32[23,7,63]{2,1,0:T(8,128)S(1)} %slice_add_fusion), channel_id=1, source_target_pairs={{0,2},{1,3},{2,0},{3,1},{4,6},{5,7},{6,4},{7,5},{8,10},{9,11},{10,... | collective-permute-start | bytes 121724 | tf_op jit(solution)/shard_map/ppermute | solution.py:216
  90.6 7.2 %collective-permute-start.10 = (f32[23,7,63]{2,1,0:T(8,128)S(1)}, f32[23,7,63]{2,1,0:T(8,128)S(1)}, u32[]{:S(2)}, u32[]{:S(2)}) collective-permute-start(f32[23,7,63]{2,1,0:T(8,128)S(1)} %add.227), channel_id=1, source_target_pairs={{0,4},{1,5},{2,6},{3,7},{4,0},{5,1},{6,2},{7,3},{8,12},{9,13},{10,... | collective-permute-start | bytes 121724 | tf_op jit(solution)/shard_map/ppermute | solution.py:216
  93.7 25.1 %copy-start.26 = (f32[23,7]{0,1:T(8,128)S(1)}, f32[23,7]{0,1:T(8,128)}, u32[]{:S(2)}) copy-start(f32[23,7]{0,1:T(8,128)} %get-tuple-element.44) | copy-start | bytes 1936
  93.7 25.1 %copy-start.32 = (f32[63]{0:T(128)S(1)}, f32[63]{0:T(128)}, u32[]{:S(2)}) copy-start(f32[63]{0:T(128)} %get-tuple-element.49) | copy-start | bytes 760
  93.8 25.1 %copy-start.33 = (f32[63]{0:T(128)S(1)}, f32[63]{0:T(128)}, u32[]{:S(2)}) copy-start(f32[63]{0:T(128)} %get-tuple-element.50) | copy-start | bytes 760
  97.9 9.6 %collective-permute-start.11 = (f32[23,7,63]{2,1,0:T(8,128)S(1)}, f32[23,7,63]{2,1,0:T(8,128)S(1)}, u32[]{:S(2)}, u32[]{:S(2)}) collective-permute-start(f32[23,7,63]{2,1,0:T(8,128)S(1)} %add.228), channel_id=1, source_target_pairs={{0,8},{1,9},{2,10},{3,11},{4,12},{5,13},{6,14},{7,15},{8,0},{9,1},... | collective-permute-start | bytes 121724 | tf_op jit(solution)/shard_map/ppermute | solution.py:216
  107.5 10.5 %collective-permute-start.12 = (f32[23,7,63]{2,1,0:T(8,128)S(1)}, f32[23,7,63]{2,1,0:T(8,128)S(1)}, u32[]{:S(2)}, u32[]{:S(2)}) collective-permute-start(f32[23,7,63]{2,1,0:T(8,128)S(1)} %add.229), channel_id=1, source_target_pairs={{0,16},{1,17},{2,18},{3,19},{4,20},{5,21},{6,22},{7,23},{8,24},{9,... | collective-permute-start | bytes 121724 | tf_op jit(solution)/shard_map/ppermute | solution.py:216
  123.9 12.5 %collective-permute-start.13 = (f32[9,48]{1,0:T(8,128)S(1)}, f32[9,48]{1,0:T(8,128)S(1)}, u32[]{:S(2)}, u32[]{:S(2)}) collective-permute-start(f32[9,48]{1,0:T(8,128)S(1)} %get-tuple-element.33), channel_id=1, source_target_pairs={{0,32},{64,96},{128,160},{192,224},{256,288},{320,352},{384,416},{... | collective-permute-start | bytes 5192 | tf_op jit(solution)/shard_map/ppermute | solution.py:101
  125.8 14.6 %collective-permute-start.14 = (f32[9,48]{1,0:T(8,128)S(1)}, f32[9,48]{1,0:T(8,128)S(1)}, u32[]{:S(2)}, u32[]{:S(2)}) collective-permute-start(f32[9,48]{1,0:T(8,128)S(1)} %get-tuple-element.34), channel_id=1, source_target_pairs={{32,64},{96,128},{160,192},{224,256},{288,320},{352,384},{416,448}... | collective-permute-start | bytes 5192 | tf_op jit(solution)/shard_map/ppermute | solution.py:104
  145.6 17.1 %collective-permute-start.17 = (f32[36,48]{1,0:T(8,128)S(1)}, f32[36,48]{1,0:T(8,128)S(1)}, u32[]{:S(2)}, u32[]{:S(2)}) collective-permute-start(f32[36,48]{1,0:T(8,128)S(1)} %get-tuple-element.21), channel_id=1, source_target_pairs={{0,32},{64,96},{128,160},{192,224},{256,288},{320,352},{384,416},{... | collective-permute-start | bytes 20744 | tf_op jit(solution)/shard_map/ppermute | solution.py:101
  147.5 15.2 %collective-permute-start.18 = (f32[36,48]{1,0:T(8,128)S(1)}, f32[36,48]{1,0:T(8,128)S(1)}, u32[]{:S(2)}, u32[]{:S(2)}) collective-permute-start(f32[36,48]{1,0:T(8,128)S(1)} %get-tuple-element.22), channel_id=1, source_target_pairs={{32,64},{96,128},{160,192},{224,256},{288,320},{352,384},{416,448}... | collective-permute-start | bytes 20744 | tf_op jit(solution)/shard_map/ppermute | solution.py:104
  157.2 5.9 %collective-permute-start.15 = (f32[36,192]{1,0:T(8,128)S(1)}, f32[36,192]{1,0:T(8,128)S(1)}, u32[]{:S(2)}, u32[]{:S(2)}) collective-permute-start(f32[36,192]{1,0:T(8,128)S(1)} %get-tuple-element.17), channel_id=1, source_target_pairs={{0,1},{2,3},{4,5},{6,7},{8,9},{10,11},{12,13},{14,15},{16,17},{18,... | collective-permute-start | bytes 82952 | tf_op jit(solution)/shard_map/ppermute | solution.py:101
  159.2 8.0 %collective-permute-start.16 = (f32[36,192]{1,0:T(8,128)S(1)}, f32[36,192]{1,0:T(8,128)S(1)}, u32[]{:S(2)}, u32[]{:S(2)}) collective-permute-start(f32[36,192]{1,0:T(8,128)S(1)} %get-tuple-element.18), channel_id=1, source_target_pairs={{1,2},{3,4},{5,6},{7,8},{9,10},{11,12},{13,14},{15,16},{17,18},{19... | collective-permute-start | bytes 82952 | tf_op jit(solution)/shard_map/ppermute | solution.py:104
  (29 other events, 119.8 us)

commit v11 on v7

--- a/solution.py
+++ b/solution.py
@@ -180,9 +180,9 @@
 
 
 def transform(volume, basis_z, basis_y, basis_x):
-    turned = jnp.einsum("zyx,xk->zyk", volume, basis_x, precision=HIGHEST)
-    turned = jnp.einsum("zyk,yj->zjk", turned, basis_y, precision=HIGHEST)
-    return jnp.einsum("zjk,zi->ijk", turned, basis_z, precision=HIGHEST)
+    turned = jnp.einsum("zyx,xk->zyk", volume, basis_x, precision=HIGH)
+    turned = jnp.einsum("zyk,yj->zjk", turned, basis_y, precision=HIGH)
+    return jnp.einsum("zjk,zi->ijk", turned, basis_z, precision=HIGH)
 
 
 def coarse_solve(interior):

time: 170 us -> 170 us (level)
  no operation moved by 1% of the time
where the time goes in v11:
time: 170 us; the launch traced here: 167 us
  starting transfers between devices  103 us (61%)
  matrix products  26.1 us (15%)
  waiting for transfers between devices  20.7 us (12%)
  local copies, waits for them, and re-layouts  13.3 us (8%)
  other arithmetic  2.59 us (2%)
    ppermute x4, starting transfers between devices, region_exchange(): lax.ppermute(jnp.where(odd, region_out[1], region_out[0]), 'region', far_...  43.2 us
    ppermute x5, starting transfers between devices, gather_slab(): interior = interior + lax.ppermute(interior, 'group', partner)  24.2 us
    ppermute x4, starting transfers between devices, region_exchange(): lax.ppermute(jnp.where(odd, region_out[0], region_out[1]), 'region', near...  21.8 us
    ppermute x5, waiting for transfers between devices, gather_slab(): interior = interior + lax.ppermute(interior, 'group', partner)  15 us
    ppermute x6, starting transfers between devices, shift(): return lax.ppermute(block, axis, pairs)  13.5 us
    dot_general x4, matrix products, apply_level(): jnp.einsum('fnq,fqe->fne', source, gather.astype(jnp.float32), precision=...  8.58 us
    dot_general x15, matrix products, mm(): return jnp.dot(a, b, precision=HIGHEST, preferred_element_type=jnp.float32)  7.6 us
    unnamed x69, local copies, waits for them, and re-layouts  6.01 us
  transfers between devices with their start and end apart: 19, of which 9 were waited for; matrix products, arithmetic and copies ran while one was open for 6% of the time, Pallas kernels for 0%

profile of v11, /device:TPU:1, one launch (start us, length us, event | category | flops | bytes accessed | tf_op | source)
XLA Modules:
  0.0 166.9 jit_solution(12140978366878948004)
XLA Ops:
  4.3 16.1 %collective-permute-start.2 = (f32[36,48]{1,0:T(8,128)S(1)}, f32[36,48]{1,0:T(8,128)S(1)}, u32[]{:S(2)}, u32[]{:S(2)}) collective-permute-start(f32[36,48]{1,0:T(8,128)S(1)} %get-tuple-element.21), channel_id=1, source_target_pairs={{0,32},{64,96},{128,160},{192,224},{256,288},{320,352},{384,416},{... | collective-permute-start | bytes 20744 | tf_op jit(solution)/shard_map/ppermute | solution.py:101
  20.4 2.7 %collective-permute-start.3 = (f32[36,48]{1,0:T(8,128)S(1)}, f32[36,48]{1,0:T(8,128)S(1)}, u32[]{:S(2)}, u32[]{:S(2)}) collective-permute-start(f32[36,48]{1,0:T(8,128)S(1)} %get-tuple-element.22), channel_id=1, source_target_pairs={{32,64},{96,128},{160,192},{224,256},{288,320},{352,384},{416,448}... | collective-permute-start | bytes 20744 | tf_op jit(solution)/shard_map/ppermute | solution.py:104
  24.1 3.2 %collective-permute-start = (f32[44,192]{1,0:T(8,128)S(1)}, f32[44,192]{1,0:T(8,128)S(1)}, u32[]{:S(2)}, u32[]{:S(2)}) collective-permute-start(f32[44,192]{1,0:T(8,128)S(1)} %get-tuple-element.11), channel_id=1, source_target_pairs={{0,1},{1,2},{2,3},{3,4},{4,5},{5,6},{6,7},{7,8},{8,9},{9,10},{10,1... | collective-permute-start | bytes 101384 | tf_op jit(solution)/shard_map/ppermute | solution.py:91
  35.8 2.2 %fusion.12 = f32[6,36,384]{2,1,0:T(8,128)S(1)} fusion(f32[6,36,384]{2,1,0:T(8,128)S(1)} %reshape.335, s32[6,384]{1,0:T(8,128)S(1)} %bitcast.129, f32[6,36,480]{2,1,0:T(8,128)S(1)} %broadcast_in_dim.19, f32[6,36,384]{2,1,0:T(8,128)S(1)} %copy-done.8), kind=kOutput, calls=%fused_computation.21 | convolution fusion | flops 432241920 | bytes 1419264 | tf_op jit(solution)/shard_map/fnq,fqe->fne/dot_general | solution.py:145
  43.0 15.1 %collective-permute-start.7 = (f32[9,48]{1,0:T(8,128)S(1)}, f32[9,48]{1,0:T(8,128)S(1)}, u32[]{:S(2)}, u32[]{:S(2)}) collective-permute-start(f32[9,48]{1,0:T(8,128)S(1)} %get-tuple-element.32), channel_id=1, source_target_pairs={{32,64},{96,128},{160,192},{224,256},{288,320},{352,384},{416,448}... | collective-permute-start | bytes 5192 | tf_op jit(solution)/shard_map/ppermute | solution.py:104
  58.6 4.0 %collective-permute-start.4 = (f32[9,192]{1,0:T(8,128)S(1)}, f32[9,192]{1,0:T(8,128)S(1)}, u32[]{:S(2)}, u32[]{:S(2)}) collective-permute-start(f32[9,192]{1,0:T(8,128)S(1)} %get-tuple-element.23), channel_id=1, source_target_pairs={{0,1},{1,2},{2,3},{3,4},{4,5},{5,6},{6,7},{7,8},{8,9},{9,10},{10,1... | collective-permute-start | bytes 20744 | tf_op jit(solution)/shard_map/ppermute | solution.py:91
  64.5 2.5 %collective-permute-done.5 = f32[9,192]{1,0:T(8,128)S(1)} collective-permute-done((f32[9,192]{1,0:T(8,128)S(1)}, f32[9,192]{1,0:T(8,128)S(1)}, u32[]{:S(2)}, u32[]{:S(2)}) %collective-permute-start.5) | collective-permute-done | bytes 6944 | tf_op jit(solution)/shard_map/ppermute | solution.py:91
  67.5 2.1 %fusion.18 = f32[6,9,384]{2,1,0:T(8,128)S(1)} fusion(f32[6,9,384]{2,1,0:T(8,128)S(1)} %reshape.339, s32[6,384]{1,0:T(8,128)S(1)} %bitcast.130, f32[6,9,480]{2,1,0:T(8,128)S(1)} %broadcast_in_dim.22, f32[6,9,384]{2,1,0:T(8,128)S(1)} %gather_fusion.1), kind=kOutput, calls=%fused_computation.31 | convolution fusion | flops 109553472 | bytes 361728 | tf_op jit(solution)/shard_map/fnq,fqe->fne/dot_general | solution.py:145
  71.6 3.5 %collective-permute-start.8 = (f32[23,7,63]{2,1,0:T(8,128)S(1)}, f32[23,7,63]{2,1,0:T(8,128)S(1)}, u32[]{:S(2)}, u32[]{:S(2)}) collective-permute-start(f32[23,7,63]{2,1,0:T(8,128)S(1)} %slice.217), channel_id=1, source_target_pairs={{0,1},{1,0},{2,3},{3,2},{4,5},{5,4},{6,7},{7,6},{8,9},{9,8},{10,11... | collective-permute-start | bytes 121724 | tf_op jit(solution)/shard_map/ppermute | solution.py:217
  75.1 2.9 %collective-permute-done.8 = f32[23,7,63]{2,1,0:T(8,128)S(1)} collective-permute-done((f32[23,7,63]{2,1,0:T(8,128)S(1)}, f32[23,7,63]{2,1,0:T(8,128)S(1)}, u32[]{:S(2)}, u32[]{:S(2)}) %collective-permute-start.8) | collective-permute-done | bytes 40604 | tf_op jit(solution)/shard_map/ppermute | solution.py:217
  78.1 6.8 %collective-permute-start.9 = (f32[23,7,63]{2,1,0:T(8,128)S(1)}, f32[23,7,63]{2,1,0:T(8,128)S(1)}, u32[]{:S(2)}, u32[]{:S(2)}) collective-permute-start(f32[23,7,63]{2,1,0:T(8,128)S(1)} %slice_add_fusion), channel_id=1, source_target_pairs={{0,2},{1,3},{2,0},{3,1},{4,6},{5,7},{6,4},{7,5},{8,10},{9,11},{10,... | collective-permute-start | bytes 121724 | tf_op jit(solution)/shard_map/ppermute | solution.py:217
  85.0 1.9 %collective-permute-done.9 = f32[23,7,63]{2,1,0:T(8,128)S(1)} collective-permute-done((f32[23,7,63]{2,1,0:T(8,128)S(1)}, f32[23,7,63]{2,1,0:T(8,128)S(1)}, u32[]{:S(2)}, u32[]{:S(2)}) %collective-permute-start.9) | collective-permute-done | bytes 40604 | tf_op jit(solution)/shard_map/ppermute | solution.py:217
  86.9 2.6 %collective-permute-start.10 = (f32[23,7,63]{2,1,0:T(8,128)S(1)}, f32[23,7,63]{2,1,0:T(8,128)S(1)}, u32[]{:S(2)}, u32[]{:S(2)}) collective-permute-start(f32[23,7,63]{2,1,0:T(8,128)S(1)} %add.221), channel_id=1, source_target_pairs={{0,4},{1,5},{2,6},{3,7},{4,0},{5,1},{6,2},{7,3},{8,12},{9,13},{10,... | collective-permute-start | bytes 121724 | tf_op jit(solution)/shard_map/ppermute | solution.py:217
  92.3 6.0 %collective-permute-start.11 = (f32[23,7,63]{2,1,0:T(8,128)S(1)}, f32[23,7,63]{2,1,0:T(8,128)S(1)}, u32[]{:S(2)}, u32[]{:S(2)}) collective-permute-start(f32[23,7,63]{2,1,0:T(8,128)S(1)} %add.222), channel_id=1, source_target_pairs={{0,8},{1,9},{2,10},{3,11},{4,12},{5,13},{6,14},{7,15},{8,0},{9,1},... | collective-permute-start | bytes 121724 | tf_op jit(solution)/shard_map/ppermute | solution.py:217
  98.3 2.9 %collective-permute-done.11 = f32[23,7,63]{2,1,0:T(8,128)S(1)} collective-permute-done((f32[23,7,63]{2,1,0:T(8,128)S(1)}, f32[23,7,63]{2,1,0:T(8,128)S(1)}, u32[]{:S(2)}, u32[]{:S(2)}) %collective-permute-start.11) | collective-permute-done | bytes 40604 | tf_op jit(solution)/shard_map/ppermute | solution.py:217
  101.2 5.3 %collective-permute-start.12 = (f32[23,7,63]{2,1,0:T(8,128)S(1)}, f32[23,7,63]{2,1,0:T(8,128)S(1)}, u32[]{:S(2)}, u32[]{:S(2)}) collective-permute-start(f32[23,7,63]{2,1,0:T(8,128)S(1)} %add.223), channel_id=1, source_target_pairs={{0,16},{1,17},{2,18},{3,19},{4,20},{5,21},{6,22},{7,23},{8,24},{9,... | collective-permute-start | bytes 121724 | tf_op jit(solution)/shard_map/ppermute | solution.py:217
  106.6 6.1 %collective-permute-done.12 = f32[23,7,63]{2,1,0:T(8,128)S(1)} collective-permute-done((f32[23,7,63]{2,1,0:T(8,128)S(1)}, f32[23,7,63]{2,1,0:T(8,128)S(1)}, u32[]{:S(2)}, u32[]{:S(2)}) %collective-permute-start.12) | collective-permute-done | bytes 40604 | tf_op jit(solution)/shard_map/ppermute | solution.py:217
  120.2 12.6 %collective-permute-start.14 = (f32[9,48]{1,0:T(8,128)S(1)}, f32[9,48]{1,0:T(8,128)S(1)}, u32[]{:S(2)}, u32[]{:S(2)}) collective-permute-start(f32[9,48]{1,0:T(8,128)S(1)} %get-tuple-element.28), channel_id=1, source_target_pairs={{32,64},{96,128},{160,192},{224,256},{288,320},{352,384},{416,448}... | collective-permute-start | bytes 5192 | tf_op jit(solution)/shard_map/ppermute | solution.py:104
  134.4 2.1 %fusion.19 = f32[6,9,384]{2,1,0:T(8,128)S(1)} fusion(f32[6,9,384]{2,1,0:T(8,128)S(1)} %reshape.345, s32[6,384]{1,0:T(8,128)S(1)} %bitcast.131, f32[6,9,480]{2,1,0:T(8,128)S(1)} %broadcast_in_dim.24, f32[6,9,384]{2,1,0:T(8,128)S(1)} %gather_fusion.2), kind=kOutput, calls=%fused_computation.32 | convolution fusion | flops 109553472 | bytes 361728 | tf_op jit(solution)/shard_map/fnq,fqe->fne/dot_general | solution.py:145
  138.7 1.9 %collective-permute-start.17 = (f32[36,48]{1,0:T(8,128)S(1)}, f32[36,48]{1,0:T(8,128)S(1)}, u32[]{:S(2)}, u32[]{:S(2)}) collective-permute-start(f32[36,48]{1,0:T(8,128)S(1)} %get-tuple-element.17), channel_id=1, source_target_pairs={{0,32},{64,96},{128,160},{192,224},{256,288},{320,352},{384,416},{... | collective-permute-start | bytes 20744 | tf_op jit(solution)/shard_map/ppermute | solution.py:101
  140.6 12.8 %collective-permute-start.18 = (f32[36,48]{1,0:T(8,128)S(1)}, f32[36,48]{1,0:T(8,128)S(1)}, u32[]{:S(2)}, u32[]{:S(2)}) collective-permute-start(f32[36,48]{1,0:T(8,128)S(1)} %get-tuple-element.18), channel_id=1, source_target_pairs={{32,64},{96,128},{160,192},{224,256},{288,320},{352,384},{416,448}... | collective-permute-start | bytes 20744 | tf_op jit(solution)/shard_map/ppermute | solution.py:104
  154.0 2.4 %collective-permute-start.15 = (f32[36,192]{1,0:T(8,128)S(1)}, f32[36,192]{1,0:T(8,128)S(1)}, u32[]{:S(2)}, u32[]{:S(2)}) collective-permute-start(f32[36,192]{1,0:T(8,128)S(1)} %get-tuple-element.13), channel_id=1, source_target_pairs={{0,1},{1,2},{2,3},{3,4},{4,5},{5,6},{6,7},{7,8},{8,9},{9,10},{10,1... | collective-permute-start | bytes 82952 | tf_op jit(solution)/shard_map/ppermute | solution.py:91
  159.2 2.0 %collective-permute-done.16 = f32[36,192]{1,0:T(8,128)S(1)} collective-permute-done((f32[36,192]{1,0:T(8,128)S(1)}, f32[36,192]{1,0:T(8,128)S(1)}, u32[]{:S(2)}, u32[]{:S(2)}) %collective-permute-start.16) | collective-permute-done | bytes 27680 | tf_op jit(solution)/shard_map/ppermute | solution.py:91
  162.9 2.2 %fusion.13 = f32[6,36,384]{2,1,0:T(8,128)S(1)} fusion(f32[6,36,384]{2,1,0:T(8,128)S(1)} %copy-done.4, s32[6,384]{1,0:T(8,128)S(1)} %bitcast.132, f32[6,36,480]{2,1,0:T(8,128)S(1)} %broadcast_in_dim.26, f32[6,36,384]{2,1,0:T(8,128)S(1)} %copy-done.9), kind=kOutput, calls=%fused_computation.22 | convolution fusion | flops 432241920 | bytes 1419264 | tf_op jit(solution)/shard_map/fnq,fqe->fne/dot_general | solution.py:145
  (210 shorter events, 43.4 us)
Async XLA Ops:
  3.4 25.4 %copy-start.27 = (s32[1,480]{1,0:T(1,128)S(1)}, s32[1,480]{1,0:T(1,128)}, u32[]{:S(2)}) copy-start(s32[1,480]{1,0:T(1,128)} %param.40) | copy-start | bytes 5764
  3.4 25.4 %copy-start.28 = (s32[6]{0:T(128)S(1)}, s32[6]{0:T(128)}, u32[]{:S(2)}) copy-start(s32[6]{0:T(128)} %constant.162) | copy-start | bytes 76
  4.3 29.2 %collective-permute-start.2 = (f32[36,48]{1,0:T(8,128)S(1)}, f32[36,48]{1,0:T(8,128)S(1)}, u32[]{:S(2)}, u32[]{:S(2)}) collective-permute-start(f32[36,48]{1,0:T(8,128)S(1)} %get-tuple-element.21), channel_id=1, source_target_pairs={{0,32},{64,96},{128,160},{192,224},{256,288},{320,352},{384,416},{... | collective-permute-start | bytes 20744 | tf_op jit(solution)/shard_map/ppermute | solution.py:101
  20.4 13.8 %collective-permute-start.3 = (f32[36,48]{1,0:T(8,128)S(1)}, f32[36,48]{1,0:T(8,128)S(1)}, u32[]{:S(2)}, u32[]{:S(2)}) collective-permute-start(f32[36,48]{1,0:T(8,128)S(1)} %get-tuple-element.22), channel_id=1, source_target_pairs={{32,64},{96,128},{160,192},{224,256},{288,320},{352,384},{416,448}... | collective-permute-start | bytes 20744 | tf_op jit(solution)/shard_map/ppermute | solution.py:104
  24.1 10.1 %collective-permute-start = (f32[44,192]{1,0:T(8,128)S(1)}, f32[44,192]{1,0:T(8,128)S(1)}, u32[]{:S(2)}, u32[]{:S(2)}) collective-permute-start(f32[44,192]{1,0:T(8,128)S(1)} %get-tuple-element.11), channel_id=1, source_target_pairs={{0,1},{1,2},{2,3},{3,4},{4,5},{5,6},{6,7},{7,8},{8,9},{9,10},{10,1... | collective-permute-start | bytes 101384 | tf_op jit(solution)/shard_map/ppermute | solution.py:91
  27.3 6.9 %collective-permute-start.1 = (f32[44,192]{1,0:T(8,128)S(1)}, f32[44,192]{1,0:T(8,128)S(1)}, u32[]{:S(2)}, u32[]{:S(2)}) collective-permute-start(f32[44,192]{1,0:T(8,128)S(1)} %get-tuple-element.12), channel_id=1, source_target_pairs={{1,0},{2,1},{3,2},{4,3},{5,4},{6,5},{7,6},{8,7},{9,8},{10,9},{11,1... | collective-permute-start | bytes 101384 | tf_op jit(solution)/shard_map/ppermute | solution.py:91
  40.8 26.3 %copy-start.11 = (f32[72,9]{1,0:T(8,128)S(1)}, f32[72,9]{1,0:T(8,128)}, u32[]{:S(2)}) copy-start(f32[72,9]{1,0:T(8,128)} %constant.150.clone) | copy-start | bytes 7780
  41.1 23.4 %collective-permute-start.6 = (f32[9,48]{1,0:T(8,128)S(1)}, f32[9,48]{1,0:T(8,128)S(1)}, u32[]{:S(2)}, u32[]{:S(2)}) collective-permute-start(f32[9,48]{1,0:T(8,128)S(1)} %get-tuple-element.31), channel_id=1, source_target_pairs={{0,32},{64,96},{128,160},{192,224},{256,288},{320,352},{384,416},{... | collective-permute-start | bytes 5192 | tf_op jit(solution)/shard_map/ppermute | solution.py:101
  43.0 21.5 %collective-permute-start.7 = (f32[9,48]{1,0:T(8,128)S(1)}, f32[9,48]{1,0:T(8,128)S(1)}, u32[]{:S(2)}, u32[]{:S(2)}) collective-permute-start(f32[9,48]{1,0:T(8,128)S(1)} %get-tuple-element.32), channel_id=1, source_target_pairs={{32,64},{96,128},{160,192},{224,256},{288,320},{352,384},{416,448}... | collective-permute-start | bytes 5192 | tf_op jit(solution)/shard_map/ppermute | solution.py:104
  58.6 5.9 %collective-permute-start.4 = (f32[9,192]{1,0:T(8,128)S(1)}, f32[9,192]{1,0:T(8,128)S(1)}, u32[]{:S(2)}, u32[]{:S(2)}) collective-permute-start(f32[9,192]{1,0:T(8,128)S(1)} %get-tuple-element.23), channel_id=1, source_target_pairs={{0,1},{1,2},{2,3},{3,4},{4,5},{5,6},{6,7},{7,8},{8,9},{9,10},{10,1... | collective-permute-start | bytes 20744 | tf_op jit(solution)/shard_map/ppermute | solution.py:91
  62.6 4.5 %collective-permute-start.5 = (f32[9,192]{1,0:T(8,128)S(1)}, f32[9,192]{1,0:T(8,128)S(1)}, u32[]{:S(2)}, u32[]{:S(2)}) collective-permute-start(f32[9,192]{1,0:T(8,128)S(1)} %get-tuple-element.24), channel_id=1, source_target_pairs={{1,0},{2,1},{3,2},{4,3},{5,4},{6,5},{7,6},{8,7},{9,8},{10,9},{11,1... | collective-permute-start | bytes 20744 | tf_op jit(solution)/shard_map/ppermute | solution.py:91
  71.6 6.4 %collective-permute-start.8 = (f32[23,7,63]{2,1,0:T(8,128)S(1)}, f32[23,7,63]{2,1,0:T(8,128)S(1)}, u32[]{:S(2)}, u32[]{:S(2)}) collective-permute-start(f32[23,7,63]{2,1,0:T(8,128)S(1)} %slice.217), channel_id=1, source_target_pairs={{0,1},{1,0},{2,3},{3,2},{4,5},{5,4},{6,7},{7,6},{8,9},{9,8},{10,11... | collective-permute-start | bytes 121724 | tf_op jit(solution)/shard_map/ppermute | solution.py:217
  78.1 8.8 %collective-permute-start.9 = (f32[23,7,63]{2,1,0:T(8,128)S(1)}, f32[23,7,63]{2,1,0:T(8,128)S(1)}, u32[]{:S(2)}, u32[]{:S(2)}) collective-permute-start(f32[23,7,63]{2,1,0:T(8,128)S(1)} %slice_add_fusion), channel_id=1, source_target_pairs={{0,2},{1,3},{2,0},{3,1},{4,6},{5,7},{6,4},{7,5},{8,10},{9,11},{10,... | collective-permute-start | bytes 121724 | tf_op jit(solution)/shard_map/ppermute | solution.py:217
  86.9 5.3 %collective-permute-start.10 = (f32[23,7,63]{2,1,0:T(8,128)S(1)}, f32[23,7,63]{2,1,0:T(8,128)S(1)}, u32[]{:S(2)}, u32[]{:S(2)}) collective-permute-start(f32[23,7,63]{2,1,0:T(8,128)S(1)} %add.221), channel_id=1, source_target_pairs={{0,4},{1,5},{2,6},{3,7},{4,0},{5,1},{6,2},{7,3},{8,12},{9,13},{10,... | collective-permute-start | bytes 121724 | tf_op jit(solution)/shard_map/ppermute | solution.py:217
  90.3 23.1 %copy-start.32 = (f32[63]{0:T(128)S(1)}, f32[63]{0:T(128)}, u32[]{:S(2)}) copy-start(f32[63]{0:T(128)} %get-tuple-element.43) | copy-start | bytes 760
  90.3 23.1 %copy-start.33 = (f32[63]{0:T(128)S(1)}, f32[63]{0:T(128)}, u32[]{:S(2)}) copy-start(f32[63]{0:T(128)} %get-tuple-element.44) | copy-start | bytes 760
  92.3 8.9 %collective-permute-start.11 = (f32[23,7,63]{2,1,0:T(8,128)S(1)}, f32[23,7,63]{2,1,0:T(8,128)S(1)}, u32[]{:S(2)}, u32[]{:S(2)}) collective-permute-start(f32[23,7,63]{2,1,0:T(8,128)S(1)} %add.222), channel_id=1, source_target_pairs={{0,8},{1,9},{2,10},{3,11},{4,12},{5,13},{6,14},{7,15},{8,0},{9,1},... | collective-permute-start | bytes 121724 | tf_op jit(solution)/shard_map/ppermute | solution.py:217
  101.2 11.5 %collective-permute-start.12 = (f32[23,7,63]{2,1,0:T(8,128)S(1)}, f32[23,7,63]{2,1,0:T(8,128)S(1)}, u32[]{:S(2)}, u32[]{:S(2)}) collective-permute-start(f32[23,7,63]{2,1,0:T(8,128)S(1)} %add.223), channel_id=1, source_target_pairs={{0,16},{1,17},{2,18},{3,19},{4,20},{5,21},{6,22},{7,23},{8,24},{9,... | collective-permute-start | bytes 121724 | tf_op jit(solution)/shard_map/ppermute | solution.py:217
  118.2 15.5 %collective-permute-start.13 = (f32[9,48]{1,0:T(8,128)S(1)}, f32[9,48]{1,0:T(8,128)S(1)}, u32[]{:S(2)}, u32[]{:S(2)}) collective-permute-start(f32[9,48]{1,0:T(8,128)S(1)} %get-tuple-element.27), channel_id=1, source_target_pairs={{0,32},{64,96},{128,160},{192,224},{256,288},{320,352},{384,416},{... | collective-permute-start | bytes 5192 | tf_op jit(solution)/shard_map/ppermute | solution.py:101
  120.2 13.9 %collective-permute-start.14 = (f32[9,48]{1,0:T(8,128)S(1)}, f32[9,48]{1,0:T(8,128)S(1)}, u32[]{:S(2)}, u32[]{:S(2)}) collective-permute-start(f32[9,48]{1,0:T(8,128)S(1)} %get-tuple-element.28), channel_id=1, source_target_pairs={{32,64},{96,128},{160,192},{224,256},{288,320},{352,384},{416,448}... | collective-permute-start | bytes 5192 | tf_op jit(solution)/shard_map/ppermute | solution.py:104
  138.7 20.5 %collective-permute-start.17 = (f32[36,48]{1,0:T(8,128)S(1)}, f32[36,48]{1,0:T(8,128)S(1)}, u32[]{:S(2)}, u32[]{:S(2)}) collective-permute-start(f32[36,48]{1,0:T(8,128)S(1)} %get-tuple-element.17), channel_id=1, source_target_pairs={{0,32},{64,96},{128,160},{192,224},{256,288},{320,352},{384,416},{... | collective-permute-start | bytes 20744 | tf_op jit(solution)/shard_map/ppermute | solution.py:101
  140.6 18.5 %collective-permute-start.18 = (f32[36,48]{1,0:T(8,128)S(1)}, f32[36,48]{1,0:T(8,128)S(1)}, u32[]{:S(2)}, u32[]{:S(2)}) collective-permute-start(f32[36,48]{1,0:T(8,128)S(1)} %get-tuple-element.18), channel_id=1, source_target_pairs={{32,64},{96,128},{160,192},{224,256},{288,320},{352,384},{416,448}... | collective-permute-start | bytes 20744 | tf_op jit(solution)/shard_map/ppermute | solution.py:104
  154.0 5.2 %collective-permute-start.15 = (f32[36,192]{1,0:T(8,128)S(1)}, f32[36,192]{1,0:T(8,128)S(1)}, u32[]{:S(2)}, u32[]{:S(2)}) collective-permute-start(f32[36,192]{1,0:T(8,128)S(1)} %get-tuple-element.13), channel_id=1, source_target_pairs={{0,1},{1,2},{2,3},{3,4},{4,5},{5,6},{6,7},{7,8},{8,9},{9,10},{10,1... | collective-permute-start | bytes 82952 | tf_op jit(solution)/shard_map/ppermute | solution.py:91
  156.5 4.8 %collective-permute-start.16 = (f32[36,192]{1,0:T(8,128)S(1)}, f32[36,192]{1,0:T(8,128)S(1)}, u32[]{:S(2)}, u32[]{:S(2)}) collective-permute-start(f32[36,192]{1,0:T(8,128)S(1)} %get-tuple-element.14), channel_id=1, source_target_pairs={{1,0},{2,1},{3,2},{4,3},{5,4},{6,5},{7,6},{8,7},{9,8},{10,9},{11,1... | collective-permute-start | bytes 82952 | tf_op jit(solution)/shard_map/ppermute | solution.py:91
  (29 other events, 170.3 us)
